TPU v7x, 128 devices: a whole 4x4x4 slice. The times are simulated.
128 devices in a mesh: req: 4 (over z), vocab: 32 (over y, x, core).
Axes of the slice: x: 4, y: 4, z: 4, core: 2. Of those that a mesh axis runs over, the one named last changes fastest.
Arguments:
- hidden: bfloat16 [16, 1536, 2048], P('req', 'vocab'), may hold values from -80 to 80
- norm_gain: float32 [2048], replicated, may hold values from 0.6 to 1.4
- head_weight: bfloat16 [2048, 32000], P(None, 'vocab'), may hold values from -2 to 2
- token_ids: int32 [16, 1536], P('req', 'vocab'), may hold values from 0 to 31999
- lengths: int32 [16], replicated, may hold values from 1 to 1536, 15360 in all
- group_ids: int32 [16], replicated, may hold values from 0 to 3
Outputs:
- logprob: float32 [16, 1536], P('req', 'vocab')
- entropy: float32 [16, 1536], P('req', 'vocab')
- centered: float32 [16], replicated
Inputs may be any that keep to these rules, and one draw needn't show every extreme that they name: The lengths sum to 15360; the longest is 1536.
All inputs are finite; a program needn't handle non-finite values.
Results may differ from a plain program's by a relative error of at most 0.00093.
Values may be sent and summed in bfloat16 or wider, within the bound.
No kernel may reach another device: no remote copies, remote signals or barrier semaphores. Data moves between devices by JAX's collectives and lax.ppermute only.
A program may use at most 128 MiB of HBM per device.

v0:
```python
import jax
import jax.numpy as jnp
import numpy as np
from jax import lax
from jax.sharding import Mesh
from jax.sharding import PartitionSpec as P

norm_eps = 1e-06
BLOCK = 384


def block_stats(rows, tokens, weight, offset):
    logits = jnp.dot(rows, weight, preferred_element_type=jnp.float32)
    row_top = jnp.max(logits, axis=1)
    exps = jnp.exp(logits - row_top[:, None])
    exp_total = jnp.sum(exps, axis=1)
    moment = jnp.sum(exps * logits, axis=1)
    columns = jnp.arange(weight.shape[1], dtype=jnp.int32)
    picked = jnp.sum(jnp.where(columns[None, :] == (tokens - offset)[:, None], logits, 0.0), axis=1)
    return jnp.stack([row_top, exp_total, moment, picked])


def merge(a, b):
    top = jnp.maximum(a[0], b[0])
    ea = jnp.exp(a[0] - top)
    eb = jnp.exp(b[0] - top)
    return jnp.stack([top, a[1] * ea + b[1] * eb, a[2] * ea + b[2] * eb, a[3] + b[3]])


def xor_gather(x, axis, size, index):
    bit = 1
    while bit < size:
        other = lax.ppermute(x, axis, [(i, i ^ bit) for i in range(size)])
        upper = (index & bit) != 0
        x = jnp.concatenate([jnp.where(upper, other, x), jnp.where(upper, x, other)], axis=0)
        bit *= 2
    return x


def xor_reduce(x, axis, size, combine):
    bit = 1
    while bit < size:
        x = combine(x, lax.ppermute(x, axis, [(i, i ^ bit) for i in range(size)]))
        bit *= 2
    return x


def body(hidden, norm_gain, head_weight, token_ids, lengths, group_ids):
    req_dev, pos_dev, model_width = hidden.shape
    vocab_dev = head_weight.shape[1]
    n_chip = lax.axis_size("chip")
    n_core = lax.axis_size("core")
    n_req = lax.axis_size("req")
    chip = lax.axis_index("chip")
    core = lax.axis_index("core")
    req_index = lax.axis_index("req")
    values = hidden.astype(jnp.float32)
    squares = jnp.mean(values * values, axis=-1, keepdims=True)
    normed = (values * lax.rsqrt(squares + norm_eps) * norm_gain).astype(jnp.bfloat16)
    rows = lax.all_gather(normed, "chip", axis=1, tiled=True)
    other = lax.ppermute(head_weight, "core", [(0, 1), (1, 0)])
    first = core == 0
    weight = jnp.concatenate([jnp.where(first, head_weight, other), jnp.where(first, other, head_weight)], axis=1)
    offset = chip * (n_core * vocab_dev)
    half_len = rows.shape[1]
    tokens = xor_gather(token_ids.T, "chip", n_chip, chip)
    own_lengths = lax.dynamic_slice_in_dim(lengths, req_index * req_dev, req_dev)
    per_request = []
    for k in range(req_dev):
        blocks = []
        for start in range(0, half_len, BLOCK):
            size = min(BLOCK, half_len - start)
            blocks.append(block_stats(rows[k, start : start + size], tokens[start : start + size, k], weight, offset))
        per_request.append(jnp.concatenate(blocks, axis=1))
    stats = jnp.stack(per_request, axis=1)
    stats = xor_reduce(stats, "chip", n_chip, merge)
    row_top, exp_total, moment, token_logit = stats[0], stats[1], stats[2], stats[3]
    log_total = row_top + jnp.log(exp_total)
    raw_logprob = token_logit - log_total
    raw_entropy = log_total - moment / exp_total
    index = jnp.arange(half_len, dtype=jnp.int32)
    positions = ((index // pos_dev) * n_core + core) * pos_dev + index % pos_dev
    is_live = positions[None, :] < own_lengths[:, None]
    logprob = jnp.where(is_live, raw_logprob, 0.0)
    entropy = jnp.where(is_live, raw_entropy, 0.0)
    half_seq = jnp.sum(logprob, axis=1)
    own_seq = half_seq + lax.ppermute(half_seq, "core", [(0, 1), (1, 0)])
    request_count = lengths.shape[0]
    slots = jnp.arange(request_count, dtype=jnp.int32)
    global_rows = req_index * req_dev + jnp.arange(req_dev, dtype=jnp.int32)
    seq_sum = jnp.sum(jnp.where(slots[None, :] == global_rows[:, None], own_seq[:, None], 0.0), axis=0)
    seq_sum = xor_reduce(seq_sum, "req", n_req, jnp.add)
    same = (group_ids[:, None] == group_ids[None, :]).astype(jnp.float32)
    members = jnp.sum(same, axis=1)
    group_mean = jnp.sum(same * seq_sum[None, :], axis=1) / members
    spread = jnp.sum(same * (seq_sum[None, :] - group_mean[:, None]) ** 2, axis=1) / members
    group_std = jnp.maximum(jnp.sqrt(spread), 1.0)
    centered = (seq_sum - group_mean) / group_std
    own = chip * pos_dev
    return (
        lax.dynamic_slice_in_dim(logprob, own, pos_dev, axis=1),
        lax.dynamic_slice_in_dim(entropy, own, pos_dev, axis=1),
        centered,
    )


def solution(mesh):
    n_req, n_vocab = mesh.devices.shape
    split = Mesh(np.asarray(mesh.devices).reshape(n_req, n_vocab // 2, 2), ("req", "chip", "core"))
    vocab = ("chip", "core")
    return jax.shard_map(
        body,
        mesh=split,
        in_specs=(P("req", vocab, None), P(), P(None, vocab), P("req", vocab), P(), P()),
        out_specs=(P("req", vocab), P("req", vocab), P()),
        check_vma=False,
    )
```

profile of v0, /device:TPU:2, one launch (start us, length us, event | category | flops | bytes accessed | tf_op | source)
XLA Modules:
  0.0 201.5 jit_solution(6005130480237795806)
XLA Ops:
  7.2 0.0 all-gather.2.cloned.1.call-start
  7.2 1.4 fusion.8
  8.6 2.4 %fusion.10 = bf16[4,48,2048]{2,1,0:T(8,128)(2,1)} fusion(bf16[4,48,2048]{2,1,0:T(8,128)(2,1)} %param.6, f32[2048]{0:T(1024)} %param.7, f32[4,48]{1,0:T(4,128)S(1)} %add_rsqrt_fusion), kind=kLoop, calls=%fused_computation.47 | loop fusion | flops 1572864 | bytes 1581824 | tf_op jit(solution)/shard_map/convert_element_type | solution.py:59
  11.0 0.0 all-gather.2.cloned.1.call-update
  11.0 0.1 collective-permute-start
  11.1 0.5 collective-permute-start.1
  11.6 3.4 %collective-permute-done.1 = s32[48,4]{0,1:T(4,128)S(1)} collective-permute-done((s32[48,4]{0,1:T(4,128)}, s32[48,4]{0,1:T(4,128)S(1)}, u32[]{:S(2)}, u32[]{:S(2)}) %collective-permute-start.1) | collective-permute-done | bytes 800 | tf_op jit(solution)/shard_map/ppermute | solution.py:33
  14.9 0.7 broadcast_select_fusion.7
  15.6 0.1 pad_add_fusion.2
  15.7 2.1 %collective-permute-start.2 = (s32[96,4]{0,1:T(4,128)S(1)}, s32[96,4]{0,1:T(4,128)S(1)}, u32[]{:S(2)}, u32[]{:S(2)}) collective-permute-start(s32[96,4]{0,1:T(4,128)S(1)} %pad_add_fusion.2), channel_id=1, source_target_pairs={{0,4},{2,6},{4,0},{6,2},{8,12},{10,14},{12,8},{14,10},{16,20},{18,... | collective-permute-start | bytes 4616 | tf_op jit(solution)/shard_map/ppermute | solution.py:33
  17.9 3.0 %collective-permute-done.2 = s32[96,4]{0,1:T(4,128)S(1)} collective-permute-done((s32[96,4]{0,1:T(4,128)S(1)}, s32[96,4]{0,1:T(4,128)S(1)}, u32[]{:S(2)}, u32[]{:S(2)}) %collective-permute-start.2) | collective-permute-done | bytes 1568 | tf_op jit(solution)/shard_map/ppermute | solution.py:33
  20.8 0.1 broadcast_select_fusion.9
  20.9 0.1 pad_add_fusion.1
  21.0 1.6 collective-permute-start.3
  22.6 2.0 %collective-permute-done.3 = s32[192,4]{0,1:T(4,128)S(1)} collective-permute-done((s32[192,4]{0,1:T(4,128)S(1)}, s32[192,4]{0,1:T(4,128)S(1)}, u32[]{:S(2)}, u32[]{:S(2)}) %collective-permute-start.3) | collective-permute-done | bytes 3104 | tf_op jit(solution)/shard_map/ppermute | solution.py:33
  24.6 0.1 broadcast_select_fusion.5
  24.7 0.1 pad_add_fusion
  24.7 3.2 %collective-permute-start.4 = (s32[384,4]{0,1:T(4,128)S(1)}, s32[384,4]{0,1:T(4,128)S(1)}, u32[]{:S(2)}, u32[]{:S(2)}) collective-permute-start(s32[384,4]{0,1:T(4,128)S(1)} %pad_add_fusion), channel_id=1, source_target_pairs={{0,16},{2,18},{4,20},{6,22},{8,24},{10,26},{12,28},{14,30},{16,0},... | collective-permute-start | bytes 18440 | tf_op jit(solution)/shard_map/ppermute | solution.py:33
  28.0 2.1 %collective-permute-done.4 = s32[384,4]{0,1:T(4,128)S(1)} collective-permute-done((s32[384,4]{0,1:T(4,128)S(1)}, s32[384,4]{0,1:T(4,128)S(1)}, u32[]{:S(2)}, u32[]{:S(2)}) %collective-permute-start.4) | collective-permute-done | bytes 6176 | tf_op jit(solution)/shard_map/ppermute | solution.py:33
  30.0 0.1 broadcast_select_fusion.3
  30.2 0.0 collective-permute-done
  30.2 6.0 %broadcast_select_fusion.1 = (bf16[2048,1000]{0,1:T(8,128)(2,1)}, bf16[2048,1000]{0,1:T(8,128)(2,1)}) fusion(bf16[2048,1000]{0,1:T(8,128)(2,1)} %param.8, bf16[2048,1000]{0,1:T(8,128)(2,1)} %collective-permute-done, pred[]{:T(512)S(6)} %eq.151), kind=kLoop, calls=%fused_computation.2 | loop fusion | flops 4096000 | bytes 16384001 | tf_op jit(solution)/shard_map/jit(_where)/select_n | solution.py:63
  36.2 67.0 %all-gather.2.cloned.1.call-done = bf16[4,768,2048]{2,1,0:T(8,128)(2,1)} async-done(((bf16[4,48,2048]{2,1,0:T(8,128)(2,1)}), bf16[4,768,2048]{2,1,0:T(8,128)(2,1)}) %all-gather.2.cloned.1.call-update) | async-done | bytes 12582928 | tf_op jit(solution)/shard_map/all_gather | solution.py:60
  103.2 8.4 %fusion.78 = (f32[384]{0:T(512)S(1)}, f32[384,2000]{0,1:T(8,128)S(1)}) fusion(bf16[2048,1000]{0,1:T(8,128)(2,1)} %get-tuple-element.48, bf16[2048,1000]{0,1:T(8,128)(2,1)} %get-tuple-element.47, bf16[4,768,2048]{2,1,0:T(8,128)(2,1)} %all-gather.2.cloned.1.call-done), kind=kOutput, calls=%fused_computation.212 | convolution fusion | flops 3162879488 | bytes 12838400 | tf_op jit(solution)/shard_map/dot_general | solution.py:13
  111.7 1.0 fusion.7
  112.7 6.0 %fusion.77 = (f32[384]{0:T(512)S(1)}, f32[384,2000]{0,1:T(8,128)S(1)}) fusion(bf16[2048,1000]{0,1:T(8,128)(2,1)S(1)} %copy-done.1, bf16[2048,1000]{0,1:T(8,128)(2,1)S(1)} %copy-done, bf16[4,768,2048]{2,1,0:T(8,128)(2,1)} %all-gather.2.cloned.1.call-done), kind=kOutput, calls=%fused_computation.211 | convolution fusion | flops 3162879488 | bytes 12838400 | tf_op jit(solution)/shard_map/dot_general | solution.py:13
  118.7 1.0 fusion.6
  119.8 6.1 %fusion.76 = (f32[384]{0:T(512)S(1)}, f32[384,2000]{0,1:T(8,128)S(1)}) fusion(bf16[2048,1000]{0,1:T(8,128)(2,1)S(1)} %copy-done.1, bf16[2048,1000]{0,1:T(8,128)(2,1)S(1)} %copy-done, bf16[4,768,2048]{2,1,0:T(8,128)(2,1)} %all-gather.2.cloned.1.call-done), kind=kOutput, calls=%fused_computation.210 | convolution fusion | flops 3162879488 | bytes 12838400 | tf_op jit(solution)/shard_map/dot_general | solution.py:13
  125.9 1.0 fusion.5
  127.0 6.0 %fusion.75 = (f32[384]{0:T(512)S(1)}, f32[384,2000]{0,1:T(8,128)S(1)}) fusion(bf16[2048,1000]{0,1:T(8,128)(2,1)S(1)} %copy-done.1, bf16[2048,1000]{0,1:T(8,128)(2,1)S(1)} %copy-done, bf16[4,768,2048]{2,1,0:T(8,128)(2,1)} %all-gather.2.cloned.1.call-done), kind=kOutput, calls=%fused_computation.209 | convolution fusion | flops 3162879488 | bytes 12838400 | tf_op jit(solution)/shard_map/dot_general | solution.py:13
  133.0 1.0 fusion.4
  134.1 6.5 %fusion.74 = (f32[384]{0:T(512)S(1)}, f32[384,2000]{0,1:T(8,128)S(1)}) fusion(bf16[2048,1000]{0,1:T(8,128)(2,1)S(1)} %copy-done.1, bf16[2048,1000]{0,1:T(8,128)(2,1)S(1)} %copy-done, bf16[4,768,2048]{2,1,0:T(8,128)(2,1)} %all-gather.2.cloned.1.call-done), kind=kOutput, calls=%fused_computation.208 | convolution fusion | flops 3162879488 | bytes 12838400 | tf_op jit(solution)/shard_map/dot_general | solution.py:13
  140.6 1.0 fusion.3
  141.7 5.9 %fusion.73 = (f32[384]{0:T(512)S(1)}, f32[384,2000]{0,1:T(8,128)S(1)}) fusion(bf16[2048,1000]{0,1:T(8,128)(2,1)S(1)} %copy-done.1, bf16[2048,1000]{0,1:T(8,128)(2,1)S(1)} %copy-done, bf16[4,768,2048]{2,1,0:T(8,128)(2,1)} %all-gather.2.cloned.1.call-done), kind=kOutput, calls=%fused_computation.207 | convolution fusion | flops 3162879488 | bytes 12838400 | tf_op jit(solution)/shard_map/dot_general | solution.py:13
  147.6 1.0 fusion.2
  148.7 6.0 %fusion.72 = (f32[384]{0:T(512)S(1)}, f32[384,2000]{0,1:T(8,128)S(1)}) fusion(bf16[2048,1000]{0,1:T(8,128)(2,1)S(1)} %copy-done.1, bf16[2048,1000]{0,1:T(8,128)(2,1)S(1)} %copy-done, bf16[4,768,2048]{2,1,0:T(8,128)(2,1)} %all-gather.2.cloned.1.call-done), kind=kOutput, calls=%fused_computation.206 | convolution fusion | flops 3162879488 | bytes 12838400 | tf_op jit(solution)/shard_map/dot_general | solution.py:13
  154.7 1.2 fusion.1
  155.9 6.1 %fusion.71 = (f32[384]{0:T(512)S(1)}, f32[384,2000]{0,1:T(8,128)S(1)}) fusion(bf16[2048,1000]{0,1:T(8,128)(2,1)S(1)} %copy-done.1, bf16[2048,1000]{0,1:T(8,128)(2,1)S(1)} %copy-done, bf16[4,768,2048]{2,1,0:T(8,128)(2,1)} %all-gather.2.cloned.1.call-done), kind=kOutput, calls=%fused_computation.205 | convolution fusion | flops 3162879488 | bytes 12838400 | tf_op jit(solution)/shard_map/dot_general | solution.py:13
  162.0 0.0 copy-start.3
  162.0 0.0 copy-start.2
  162.0 1.0 fusion
  163.1 0.1 pad_maximum_fusion.1
  163.2 0.6 collective-permute-start.5
  163.8 3.5 %collective-permute-done.5 = f32[4,4,768]{2,1,0:T(4,128)S(1)} collective-permute-done((f32[4,4,768]{2,1,0:T(4,128)S(1)}, f32[4,4,768]{2,1,0:T(4,128)S(1)}, u32[]{:S(2)}, u32[]{:S(2)}) %collective-permute-start.5) | collective-permute-done | bytes 49184 | tf_op jit(solution)/shard_map/ppermute | solution.py:43
  167.4 2.2 %collective-permute-start.6 = (f32[4,4,768]{2,1,0:T(4,128)S(1)}, f32[4,4,768]{2,1,0:T(4,128)S(1)}, u32[]{:S(2)}, u32[]{:S(2)}) collective-permute-start(f32[4,4,768]{2,1,0:T(4,128)S(1)} %pad_maximum_fusion.2), channel_id=1, source_target_pairs={{0,4},{2,6},{4,0},{6,2},{8,12},{10,14},{12,8},{14,10},{16,20},{18,... | collective-permute-start | bytes 147464 | tf_op jit(solution)/shard_map/ppermute | solution.py:43
  169.6 3.5 %collective-permute-done.6 = f32[4,4,768]{2,1,0:T(4,128)S(1)} collective-permute-done((f32[4,4,768]{2,1,0:T(4,128)S(1)}, f32[4,4,768]{2,1,0:T(4,128)S(1)}, u32[]{:S(2)}, u32[]{:S(2)}) %collective-permute-start.6) | collective-permute-done | bytes 49184 | tf_op jit(solution)/shard_map/ppermute | solution.py:43
  173.2 0.3 collective-permute-start.7
  173.5 4.2 %collective-permute-done.7 = f32[4,4,768]{2,1,0:T(4,128)S(1)} collective-permute-done((f32[4,4,768]{2,1,0:T(4,128)S(1)}, f32[4,4,768]{2,1,0:T(4,128)S(1)}, u32[]{:S(2)}, u32[]{:S(2)}) %collective-permute-start.7) | collective-permute-done | bytes 49184 | tf_op jit(solution)/shard_map/ppermute | solution.py:43
  177.7 1.9 collective-permute-start.8
  179.6 0.1 dynamic_slice.9
  179.7 3.7 %collective-permute-done.8 = f32[4,4,768]{2,1,0:T(4,128)S(1)} collective-permute-done((f32[4,4,768]{2,1,0:T(4,128)S(1)}, f32[4,4,768]{2,1,0:T(4,128)S(1)}, u32[]{:S(2)}, u32[]{:S(2)}) %collective-permute-start.8) | collective-permute-done | bytes 49184 | tf_op jit(solution)/shard_map/ppermute | solution.py:43
  183.4 0.2 fusion.68
  183.6 0.1 collective-permute-start.9
  183.7 1.1 collective-permute-done.9
  184.8 0.1 select_reduce_fusion.8
  184.9 1.6 collective-permute-start.10
  186.5 0.6 constant_dynamic-slice_fusion.8
  187.1 1.4 collective-permute-done.10
  188.5 3.2 %collective-permute-start.11 = (f32[16]{0:T(128)S(1)}, f32[16]{0:T(128)S(1)}, u32[]{:S(2)}, u32[]{:S(2)}) collective-permute-start(f32[16]{0:T(128)S(1)} %add.175), channel_id=1, source_target_pairs={{0,64},{32,96},{64,0},{96,32},{1,65},{33,97},{65,1},{97,33},{2,66}... | collective-permute-start | bytes 200 | tf_op jit(solution)/shard_map/ppermute | solution.py:43
  191.7 0.7 fusion.54
  192.3 1.2 collective-permute-done.11
  193.6 0.2 fusion.40
  193.8 0.2 fusion.41
  194.0 0.5 maximum_divide_fusion
  (64 shorter events, 0.5 us)
Async XLA Ops:
  7.2 96.0 %all-gather.2.cloned.1.call-start = ((), (), s32[]{:S(2)}) async-start(), calls=%async_computation | async-start | bytes 13369344 | tf_op jit(solution)/shard_map/all_gather | solution.py:60
  11.0 19.2 %collective-permute-start = (bf16[2048,1000]{0,1:T(8,128)(2,1)}, bf16[2048,1000]{0,1:T(8,128)(2,1)}, u32[]{:S(2)}, u32[]{:S(2)}) collective-permute-start(bf16[2048,1000]{0,1:T(8,128)(2,1)} %param.8), channel_id=1, source_target_pairs={{0,1},{1,0},{2,3},{3,2},{4,5},{5,4},{6,7},{7,6},{8,9},{9,8},{10,11... | collective-permute-start | bytes 12288008 | tf_op jit(solution)/shard_map/ppermute | solution.py:61
  11.1 3.9 %collective-permute-start.1 = (s32[48,4]{0,1:T(4,128)}, s32[48,4]{0,1:T(4,128)S(1)}, u32[]{:S(2)}, u32[]{:S(2)}) collective-permute-start(s32[48,4]{0,1:T(4,128)} %bitcast.191), channel_id=1, source_target_pairs={{0,2},{2,0},{4,6},{6,4},{8,10},{10,8},{12,14},{14,12},{16,18},{18,... | collective-permute-start | bytes 2312 | tf_op jit(solution)/shard_map/ppermute | solution.py:33
  15.7 5.1 %collective-permute-start.2 = (s32[96,4]{0,1:T(4,128)S(1)}, s32[96,4]{0,1:T(4,128)S(1)}, u32[]{:S(2)}, u32[]{:S(2)}) collective-permute-start(s32[96,4]{0,1:T(4,128)S(1)} %pad_add_fusion.2), channel_id=1, source_target_pairs={{0,4},{2,6},{4,0},{6,2},{8,12},{10,14},{12,8},{14,10},{16,20},{18,... | collective-permute-start | bytes 4616 | tf_op jit(solution)/shard_map/ppermute | solution.py:33
  21.0 3.6 %collective-permute-start.3 = (s32[192,4]{0,1:T(4,128)S(1)}, s32[192,4]{0,1:T(4,128)S(1)}, u32[]{:S(2)}, u32[]{:S(2)}) collective-permute-start(s32[192,4]{0,1:T(4,128)S(1)} %pad_add_fusion.1), channel_id=1, source_target_pairs={{0,8},{2,10},{4,12},{6,14},{8,0},{10,2},{12,4},{14,6},{16,24},{18,... | collective-permute-start | bytes 9224 | tf_op jit(solution)/shard_map/ppermute | solution.py:33
  24.7 5.3 %collective-permute-start.4 = (s32[384,4]{0,1:T(4,128)S(1)}, s32[384,4]{0,1:T(4,128)S(1)}, u32[]{:S(2)}, u32[]{:S(2)}) collective-permute-start(s32[384,4]{0,1:T(4,128)S(1)} %pad_add_fusion), channel_id=1, source_target_pairs={{0,16},{2,18},{4,20},{6,22},{8,24},{10,26},{12,28},{14,30},{16,0},... | collective-permute-start | bytes 18440 | tf_op jit(solution)/shard_map/ppermute | solution.py:33
  103.2 9.5 %copy-start = (bf16[2048,1000]{0,1:T(8,128)(2,1)S(1)}, bf16[2048,1000]{0,1:T(8,128)(2,1)}, u32[]{:S(2)}) copy-start(bf16[2048,1000]{0,1:T(8,128)(2,1)} %get-tuple-element.47) | copy-start | bytes 12288004
  103.2 9.5 %copy-start.1 = (bf16[2048,1000]{0,1:T(8,128)(2,1)S(1)}, bf16[2048,1000]{0,1:T(8,128)(2,1)}, u32[]{:S(2)}) copy-start(bf16[2048,1000]{0,1:T(8,128)(2,1)} %get-tuple-element.48) | copy-start | bytes 12288004
  162.0 17.6 %copy-start.3 = (s32[16]{0:T(128)S(1)}, s32[16]{0:T(128)}, u32[]{:S(2)}) copy-start(s32[16]{0:T(128)} %param.10) | copy-start | bytes 196
  162.0 31.6 %copy-start.2 = (s32[16]{0:T(128)S(1)}, s32[16]{0:T(128)}, u32[]{:S(2)}) copy-start(s32[16]{0:T(128)} %param.11) | copy-start | bytes 196
  163.2 4.2 %collective-permute-start.5 = (f32[4,4,768]{2,1,0:T(4,128)S(1)}, f32[4,4,768]{2,1,0:T(4,128)S(1)}, u32[]{:S(2)}, u32[]{:S(2)}) collective-permute-start(f32[4,4,768]{2,1,0:T(4,128)S(1)} %pad_maximum_fusion.1), channel_id=1, source_target_pairs={{0,2},{2,0},{4,6},{6,4},{8,10},{10,8},{12,14},{14,12},{16,18},{18,... | collective-permute-start | bytes 147464 | tf_op jit(solution)/shard_map/ppermute | solution.py:43
  167.4 5.7 %collective-permute-start.6 = (f32[4,4,768]{2,1,0:T(4,128)S(1)}, f32[4,4,768]{2,1,0:T(4,128)S(1)}, u32[]{:S(2)}, u32[]{:S(2)}) collective-permute-start(f32[4,4,768]{2,1,0:T(4,128)S(1)} %pad_maximum_fusion.2), channel_id=1, source_target_pairs={{0,4},{2,6},{4,0},{6,2},{8,12},{10,14},{12,8},{14,10},{16,20},{18,... | collective-permute-start | bytes 147464 | tf_op jit(solution)/shard_map/ppermute | solution.py:43
  173.2 4.5 %collective-permute-start.7 = (f32[4,4,768]{2,1,0:T(4,128)S(1)}, f32[4,4,768]{2,1,0:T(4,128)S(1)}, u32[]{:S(2)}, u32[]{:S(2)}) collective-permute-start(f32[4,4,768]{2,1,0:T(4,128)S(1)} %pad_maximum_fusion.3), channel_id=1, source_target_pairs={{0,8},{2,10},{4,12},{6,14},{8,0},{10,2},{12,4},{14,6},{16,24},{18,... | collective-permute-start | bytes 147464 | tf_op jit(solution)/shard_map/ppermute | solution.py:43
  177.7 5.7 %collective-permute-start.8 = (f32[4,4,768]{2,1,0:T(4,128)S(1)}, f32[4,4,768]{2,1,0:T(4,128)S(1)}, u32[]{:S(2)}, u32[]{:S(2)}) collective-permute-start(f32[4,4,768]{2,1,0:T(4,128)S(1)} %pad_maximum_fusion.4), channel_id=1, source_target_pairs={{0,16},{2,18},{4,20},{6,22},{8,24},{10,26},{12,28},{14,30},{16,0},... | collective-permute-start | bytes 147464 | tf_op jit(solution)/shard_map/ppermute | solution.py:43
  183.6 1.2 collective-permute-start.9
  184.9 3.6 %collective-permute-start.10 = (f32[16]{0:T(128)S(1)}, f32[16]{0:T(128)S(1)}, u32[]{:S(2)}, u32[]{:S(2)}) collective-permute-start(f32[16]{0:T(128)S(1)} %select_reduce_fusion.8), channel_id=1, source_target_pairs={{0,32},{32,0},{64,96},{96,64},{1,33},{33,1},{65,97},{97,65},{2,34}... | collective-permute-start | bytes 200 | tf_op jit(solution)/shard_map/ppermute | solution.py:43
  188.5 5.1 %collective-permute-start.11 = (f32[16]{0:T(128)S(1)}, f32[16]{0:T(128)S(1)}, u32[]{:S(2)}, u32[]{:S(2)}) collective-permute-start(f32[16]{0:T(128)S(1)} %add.175), channel_id=1, source_target_pairs={{0,64},{32,96},{64,0},{96,32},{1,65},{33,97},{65,1},{97,33},{2,66}... | collective-permute-start | bytes 200 | tf_op jit(solution)/shard_map/ppermute | solution.py:43
Sparse Core Ops, SparseCore 0:
  11.1 92.0 all-gather.1
where the time goes:
time: 204 us; the launch traced here: 202 us
  waiting for transfers between devices  96.1 us (47%)
  matrix products  51 us (25%)
  other arithmetic  21.5 us (11%)
  starting transfers between devices  17.4 us (9%)
  between operations  14.7 us (7%)
    all_gather x1, waiting for transfers between devices, body(): rows = lax.all_gather(normed, 'chip', axis=1, tiled=True)  67 us
    dot_general x8, matrix products, block_stats(): logits = jnp.dot(rows, weight, preferred_element_type=jnp.float32)  51 us
    ppermute x6, waiting for transfers between devices, xor_reduce(): x = combine(x, lax.ppermute(x, axis, [(i, i ^ bit) for i in range(size)]))  17.5 us
    ppermute x4, waiting for transfers between devices, xor_gather(): other = lax.ppermute(x, axis, [(i, i ^ bit) for i in range(size)])  10.5 us
    ppermute x6, starting transfers between devices, xor_reduce(): x = combine(x, lax.ppermute(x, axis, [(i, i ^ bit) for i in range(size)]))  9.72 us
    reduce_sum x8, other arithmetic, block_stats(): exp_total = jnp.sum(exps, axis=1)  8.33 us
    ppermute x4, starting transfers between devices, xor_gather(): other = lax.ppermute(x, axis, [(i, i ^ bit) for i in range(size)])  7.44 us
    select_n x1, other arithmetic, body(): jnp.where(first, head_weight, other)  6.03 us
  transfers between devices with their start and end apart: 13, of which 12 were waited for; matrix products, arithmetic and copies ran while one was open for 4% of the time, Pallas kernels for 0%

commit v1 on v0

--- a/solution.py
+++ b/solution.py
@@ -6,7 +6,7 @@
 from jax.sharding import PartitionSpec as P
 
 norm_eps = 1e-06
-BLOCK = 384
+BLOCK = 768
 
 
 def block_stats(rows, tokens, weight, offset):

time: 204 us -> 195 us (0.956); the launches traced: 202 us -> 195 us
  matrix products: 51 us -> 44.9 us
    dot_general x8 -> x4, matrix products: 51 us -> 44.9 us  [block_stats(): logits = jnp.dot(rows, weight, preferred_element_type=jnp.float32)]
    reduce_sum x8 -> x2, other arithmetic: 8.33 us -> 8.1 us  [block_stats(): exp_total = jnp.sum(exps, axis=1)]
where the time goes in v1:
time: 195 us
  waiting for transfers between devices  96.3 us (49%)
  matrix products  44.9 us (23%)
  other arithmetic  21.1 us (11%)
  starting transfers between devices  17.4 us (9%)
  between operations  14.4 us (7%)
    all_gather x1, waiting for transfers between devices, body(): rows = lax.all_gather(normed, 'chip', axis=1, tiled=True)  67.1 us
    dot_general x4, matrix products, block_stats(): logits = jnp.dot(rows, weight, preferred_element_type=jnp.float32)  44.9 us
    ppermute x6, waiting for transfers between devices, xor_reduce(): x = combine(x, lax.ppermute(x, axis, [(i, i ^ bit) for i in range(size)]))  17.6 us
    ppermute x4, waiting for transfers between devices, xor_gather(): other = lax.ppermute(x, axis, [(i, i ^ bit) for i in range(size)])  10.5 us
    ppermute x6, starting transfers between devices, xor_reduce(): x = combine(x, lax.ppermute(x, axis, [(i, i ^ bit) for i in range(size)]))  9.72 us
    reduce_sum x2, other arithmetic, block_stats(): exp_total = jnp.sum(exps, axis=1)  8.1 us
    ppermute x4, starting transfers between devices, xor_gather(): other = lax.ppermute(x, axis, [(i, i ^ bit) for i in range(size)])  7.44 us
    select_n x1, other arithmetic, body(): jnp.where(first, head_weight, other)  5.88 us
  transfers between devices with their start and end apart: 13, of which 12 were waited for; matrix products, arithmetic and copies ran while one was open for 4% of the time, Pallas kernels for 0%

profile of v1, /device:TPU:2, one launch (start us, length us, event | category | flops | bytes accessed | tf_op | source)
XLA Modules:
  0.0 194.9 jit_solution(4985010969420196370)
XLA Ops:
  7.2 0.0 all-gather.2.cloned.1.call-start
  7.2 1.4 fusion.8
  8.6 2.4 %fusion.10 = bf16[4,48,2048]{2,1,0:T(8,128)(2,1)} fusion(bf16[4,48,2048]{2,1,0:T(8,128)(2,1)} %param.6, f32[2048]{0:T(1024)} %param.7, f32[4,48]{1,0:T(4,128)S(1)} %add_rsqrt_fusion), kind=kLoop, calls=%fused_computation.35 | loop fusion | flops 1572864 | bytes 1581824 | tf_op jit(solution)/shard_map/convert_element_type | solution.py:59
  11.0 0.0 all-gather.2.cloned.1.call-update
  11.0 0.1 collective-permute-start
  11.1 0.5 collective-permute-start.1
  11.6 3.4 %collective-permute-done.1 = s32[48,4]{0,1:T(4,128)S(1)} collective-permute-done((s32[48,4]{0,1:T(4,128)}, s32[48,4]{0,1:T(4,128)S(1)}, u32[]{:S(2)}, u32[]{:S(2)}) %collective-permute-start.1) | collective-permute-done | bytes 800 | tf_op jit(solution)/shard_map/ppermute | solution.py:33
  14.9 0.7 broadcast_select_fusion.7
  15.6 0.1 pad_add_fusion.3
  15.7 2.1 %collective-permute-start.2 = (s32[96,4]{0,1:T(4,128)S(1)}, s32[96,4]{0,1:T(4,128)S(1)}, u32[]{:S(2)}, u32[]{:S(2)}) collective-permute-start(s32[96,4]{0,1:T(4,128)S(1)} %pad_add_fusion.3), channel_id=1, source_target_pairs={{0,4},{2,6},{4,0},{6,2},{8,12},{10,14},{12,8},{14,10},{16,20},{18,... | collective-permute-start | bytes 4616 | tf_op jit(solution)/shard_map/ppermute | solution.py:33
  17.9 3.0 %collective-permute-done.2 = s32[96,4]{0,1:T(4,128)S(1)} collective-permute-done((s32[96,4]{0,1:T(4,128)S(1)}, s32[96,4]{0,1:T(4,128)S(1)}, u32[]{:S(2)}, u32[]{:S(2)}) %collective-permute-start.2) | collective-permute-done | bytes 1568 | tf_op jit(solution)/shard_map/ppermute | solution.py:33
  20.8 0.1 broadcast_select_fusion.9
  20.9 0.1 pad_add_fusion.1
  21.0 1.6 collective-permute-start.3
  22.6 2.0 %collective-permute-done.3 = s32[192,4]{0,1:T(4,128)S(1)} collective-permute-done((s32[192,4]{0,1:T(4,128)S(1)}, s32[192,4]{0,1:T(4,128)S(1)}, u32[]{:S(2)}, u32[]{:S(2)}) %collective-permute-start.3) | collective-permute-done | bytes 3104 | tf_op jit(solution)/shard_map/ppermute | solution.py:33
  24.6 0.1 broadcast_select_fusion.5
  24.7 0.1 pad_add_fusion
  24.7 3.2 %collective-permute-start.4 = (s32[384,4]{0,1:T(4,128)S(1)}, s32[384,4]{0,1:T(4,128)S(1)}, u32[]{:S(2)}, u32[]{:S(2)}) collective-permute-start(s32[384,4]{0,1:T(4,128)S(1)} %pad_add_fusion), channel_id=1, source_target_pairs={{0,16},{2,18},{4,20},{6,22},{8,24},{10,26},{12,28},{14,30},{16,0},... | collective-permute-start | bytes 18440 | tf_op jit(solution)/shard_map/ppermute | solution.py:33
  28.0 2.1 %collective-permute-done.4 = s32[384,4]{0,1:T(4,128)S(1)} collective-permute-done((s32[384,4]{0,1:T(4,128)S(1)}, s32[384,4]{0,1:T(4,128)S(1)}, u32[]{:S(2)}, u32[]{:S(2)}) %collective-permute-start.4) | collective-permute-done | bytes 6176 | tf_op jit(solution)/shard_map/ppermute | solution.py:33
  30.0 0.1 broadcast_select_fusion.3
  30.2 0.0 collective-permute-done
  30.2 5.9 %broadcast_select_fusion.1 = (bf16[2048,1000]{0,1:T(8,128)(2,1)}, bf16[2048,1000]{0,1:T(8,128)(2,1)}) fusion(bf16[2048,1000]{0,1:T(8,128)(2,1)} %param.8, bf16[2048,1000]{0,1:T(8,128)(2,1)} %collective-permute-done, pred[]{:T(512)S(6)} %eq.91), kind=kLoop, calls=%fused_computation.22 | loop fusion | flops 4096000 | bytes 16384001 | tf_op jit(solution)/shard_map/jit(_where)/select_n | solution.py:63
  36.1 67.1 %all-gather.2.cloned.1.call-done = bf16[4,768,2048]{2,1,0:T(8,128)(2,1)} async-done(((bf16[4,48,2048]{2,1,0:T(8,128)(2,1)}), bf16[4,768,2048]{2,1,0:T(8,128)(2,1)}) %all-gather.2.cloned.1.call-update) | async-done | bytes 12582928 | tf_op jit(solution)/shard_map/all_gather | solution.py:60
  103.2 11.2 %fusion.63 = (f32[768]{0:T(1024)S(1)}, f32[768,2000]{0,1:T(8,128)S(1)}) fusion(bf16[2048,1000]{0,1:T(8,128)(2,1)} %get-tuple-element.32, bf16[2048,1000]{0,1:T(8,128)(2,1)} %get-tuple-element.31, bf16[4,768,2048]{2,1,0:T(8,128)(2,1)} %all-gather.2.cloned.1.call-done), kind=kOutput, calls=%fused_computation.179 | convolution fusion | flops 6309374976 | bytes 17484800 | tf_op jit(solution)/shard_map/dot_general | solution.py:13
  114.4 11.2 %fusion.62 = (f32[768]{0:T(1024)S(1)}, f32[768,2000]{0,1:T(8,128)S(1)}) fusion(bf16[2048,1000]{0,1:T(8,128)(2,1)} %get-tuple-element.32, bf16[2048,1000]{0,1:T(8,128)(2,1)} %get-tuple-element.31, bf16[4,768,2048]{2,1,0:T(8,128)(2,1)} %all-gather.2.cloned.1.call-done), kind=kOutput, calls=%fused_computation.178 | convolution fusion | flops 6309374976 | bytes 17484800 | tf_op jit(solution)/shard_map/dot_general | solution.py:13
  125.7 3.9 %fusion.2 = (f32[768]{0:T(1024)S(1)}, f32[768]{0:T(1024)S(1)}, f32[768]{0:T(1024)S(1)}, f32[768]{0:T(1024)S(1)}, f32[768]{0:T(1024)S(1)}, /*index=5*/f32[768]{0:T(1024)S(1)}) fusion(f32[768,2000]{0,1:T(8,128)S(1)} %get-tuple-element.58, f32[768]{0:T(1024)S(1)} %get-tuple-element.57, s32[768]{0:T(1024)S(1)} %get-tuple-element.16, ...), kind=kLoop, calls=%fused_computation.15 | loop fusion | flops 21499392 | bytes 12318720 | tf_op jit(solution)/shard_map/reduce_sum | solution.py:16
  129.8 11.2 %fusion.61 = (f32[768]{0:T(1024)S(1)}, f32[768,2000]{0,1:T(8,128)S(1)}) fusion(bf16[2048,1000]{0,1:T(8,128)(2,1)} %get-tuple-element.32, bf16[2048,1000]{0,1:T(8,128)(2,1)} %get-tuple-element.31, bf16[4,768,2048]{2,1,0:T(8,128)(2,1)} %all-gather.2.cloned.1.call-done), kind=kOutput, calls=%fused_computation.177 | convolution fusion | flops 6309374976 | bytes 17484800 | tf_op jit(solution)/shard_map/dot_general | solution.py:13
  141.0 11.2 %fusion.60 = (f32[768]{0:T(1024)S(1)}, f32[768,2000]{0,1:T(8,128)S(1)}) fusion(bf16[2048,1000]{0,1:T(8,128)(2,1)} %get-tuple-element.32, bf16[2048,1000]{0,1:T(8,128)(2,1)} %get-tuple-element.31, bf16[4,768,2048]{2,1,0:T(8,128)(2,1)} %all-gather.2.cloned.1.call-done), kind=kOutput, calls=%fused_computation.176 | convolution fusion | flops 6309374976 | bytes 17484800 | tf_op jit(solution)/shard_map/dot_general | solution.py:13
  152.3 0.0 copy-start.1
  152.3 0.0 copy-start
  152.3 4.2 %fusion = (f32[768]{0:T(1024)S(1)}, f32[768]{0:T(1024)S(1)}, f32[768]{0:T(1024)S(1)}, f32[768]{0:T(1024)S(1)}, f32[768]{0:T(1024)S(1)}, /*index=5*/f32[768]{0:T(1024)S(1)}) fusion(f32[768,2000]{0,1:T(8,128)S(1)} %get-tuple-element.54, f32[768]{0:T(1024)S(1)} %get-tuple-element.53, s32[768]{0:T(1024)S(1)} %get-tuple-element.17, ...), kind=kLoop, calls=%fused_computation.5 | loop fusion | flops 21499392 | bytes 12318720 | tf_op jit(solution)/shard_map/reduce_sum | solution.py:16
  156.7 0.1 pad_maximum_fusion.1
  156.7 0.6 collective-permute-start.5
  157.4 3.5 %collective-permute-done.5 = f32[4,4,768]{2,1,0:T(4,128)S(1)} collective-permute-done((f32[4,4,768]{2,1,0:T(4,128)S(1)}, f32[4,4,768]{2,1,0:T(4,128)S(1)}, u32[]{:S(2)}, u32[]{:S(2)}) %collective-permute-start.5) | collective-permute-done | bytes 49184 | tf_op jit(solution)/shard_map/ppermute | solution.py:43
  161.0 2.2 %collective-permute-start.6 = (f32[4,4,768]{2,1,0:T(4,128)S(1)}, f32[4,4,768]{2,1,0:T(4,128)S(1)}, u32[]{:S(2)}, u32[]{:S(2)}) collective-permute-start(f32[4,4,768]{2,1,0:T(4,128)S(1)} %pad_maximum_fusion.2), channel_id=1, source_target_pairs={{0,4},{2,6},{4,0},{6,2},{8,12},{10,14},{12,8},{14,10},{16,20},{18,... | collective-permute-start | bytes 147464 | tf_op jit(solution)/shard_map/ppermute | solution.py:43
  163.1 3.5 %collective-permute-done.6 = f32[4,4,768]{2,1,0:T(4,128)S(1)} collective-permute-done((f32[4,4,768]{2,1,0:T(4,128)S(1)}, f32[4,4,768]{2,1,0:T(4,128)S(1)}, u32[]{:S(2)}, u32[]{:S(2)}) %collective-permute-start.6) | collective-permute-done | bytes 49184 | tf_op jit(solution)/shard_map/ppermute | solution.py:43
  166.7 0.3 collective-permute-start.7
  167.1 4.2 %collective-permute-done.7 = f32[4,4,768]{2,1,0:T(4,128)S(1)} collective-permute-done((f32[4,4,768]{2,1,0:T(4,128)S(1)}, f32[4,4,768]{2,1,0:T(4,128)S(1)}, u32[]{:S(2)}, u32[]{:S(2)}) %collective-permute-start.7) | collective-permute-done | bytes 49184 | tf_op jit(solution)/shard_map/ppermute | solution.py:43
  171.3 1.9 collective-permute-start.8
  173.2 0.0 copy-done.1
  173.2 0.1 dynamic_slice.9
  173.2 3.7 %collective-permute-done.8 = f32[4,4,768]{2,1,0:T(4,128)S(1)} collective-permute-done((f32[4,4,768]{2,1,0:T(4,128)S(1)}, f32[4,4,768]{2,1,0:T(4,128)S(1)}, u32[]{:S(2)}, u32[]{:S(2)}) %collective-permute-start.8) | collective-permute-done | bytes 49184 | tf_op jit(solution)/shard_map/ppermute | solution.py:43
  177.0 0.2 fusion.57
  177.1 0.1 collective-permute-start.9
  177.3 1.1 collective-permute-done.9
  178.4 0.1 select_reduce_fusion.4
  178.5 1.6 collective-permute-start.10
  180.1 0.6 constant_dynamic-slice_fusion.8
  180.7 1.4 collective-permute-done.10
  182.1 3.2 %collective-permute-start.11 = (f32[16]{0:T(128)S(1)}, f32[16]{0:T(128)S(1)}, u32[]{:S(2)}, u32[]{:S(2)}) collective-permute-start(f32[16]{0:T(128)S(1)} %add.175), channel_id=1, source_target_pairs={{0,64},{32,96},{64,0},{96,32},{1,65},{33,97},{65,1},{97,33},{2,66}... | collective-permute-start | bytes 200 | tf_op jit(solution)/shard_map/ppermute | solution.py:43
  185.2 0.7 fusion.56
  185.9 1.3 collective-permute-done.11
  187.2 0.0 copy-done
  187.2 0.2 fusion.32
  187.3 0.2 fusion.33
  187.5 0.5 maximum_divide_fusion
  (42 shorter events, 0.5 us)
Async XLA Ops:
  7.2 96.0 %all-gather.2.cloned.1.call-start = ((), (), s32[]{:S(2)}) async-start(), calls=%async_computation | async-start | bytes 13369344 | tf_op jit(solution)/shard_map/all_gather | solution.py:60
  11.0 19.2 %collective-permute-start = (bf16[2048,1000]{0,1:T(8,128)(2,1)}, bf16[2048,1000]{0,1:T(8,128)(2,1)}, u32[]{:S(2)}, u32[]{:S(2)}) collective-permute-start(bf16[2048,1000]{0,1:T(8,128)(2,1)} %param.8), channel_id=1, source_target_pairs={{0,1},{1,0},{2,3},{3,2},{4,5},{5,4},{6,7},{7,6},{8,9},{9,8},{10,11... | collective-permute-start | bytes 12288008 | tf_op jit(solution)/shard_map/ppermute | solution.py:61
  11.1 3.9 %collective-permute-start.1 = (s32[48,4]{0,1:T(4,128)}, s32[48,4]{0,1:T(4,128)S(1)}, u32[]{:S(2)}, u32[]{:S(2)}) collective-permute-start(s32[48,4]{0,1:T(4,128)} %bitcast.171), channel_id=1, source_target_pairs={{0,2},{2,0},{4,6},{6,4},{8,10},{10,8},{12,14},{14,12},{16,18},{18,... | collective-permute-start | bytes 2312 | tf_op jit(solution)/shard_map/ppermute | solution.py:33
  15.7 5.1 %collective-permute-start.2 = (s32[96,4]{0,1:T(4,128)S(1)}, s32[96,4]{0,1:T(4,128)S(1)}, u32[]{:S(2)}, u32[]{:S(2)}) collective-permute-start(s32[96,4]{0,1:T(4,128)S(1)} %pad_add_fusion.3), channel_id=1, source_target_pairs={{0,4},{2,6},{4,0},{6,2},{8,12},{10,14},{12,8},{14,10},{16,20},{18,... | collective-permute-start | bytes 4616 | tf_op jit(solution)/shard_map/ppermute | solution.py:33
  21.0 3.6 %collective-permute-start.3 = (s32[192,4]{0,1:T(4,128)S(1)}, s32[192,4]{0,1:T(4,128)S(1)}, u32[]{:S(2)}, u32[]{:S(2)}) collective-permute-start(s32[192,4]{0,1:T(4,128)S(1)} %pad_add_fusion.1), channel_id=1, source_target_pairs={{0,8},{2,10},{4,12},{6,14},{8,0},{10,2},{12,4},{14,6},{16,24},{18,... | collective-permute-start | bytes 9224 | tf_op jit(solution)/shard_map/ppermute | solution.py:33
  24.7 5.3 %collective-permute-start.4 = (s32[384,4]{0,1:T(4,128)S(1)}, s32[384,4]{0,1:T(4,128)S(1)}, u32[]{:S(2)}, u32[]{:S(2)}) collective-permute-start(s32[384,4]{0,1:T(4,128)S(1)} %pad_add_fusion), channel_id=1, source_target_pairs={{0,16},{2,18},{4,20},{6,22},{8,24},{10,26},{12,28},{14,30},{16,0},... | collective-permute-start | bytes 18440 | tf_op jit(solution)/shard_map/ppermute | solution.py:33
  152.3 20.8 %copy-start.1 = (s32[16]{0:T(128)S(1)}, s32[16]{0:T(128)}, u32[]{:S(2)}) copy-start(s32[16]{0:T(128)} %param.10) | copy-start | bytes 196
  152.3 34.8 %copy-start = (s32[16]{0:T(128)S(1)}, s32[16]{0:T(128)}, u32[]{:S(2)}) copy-start(s32[16]{0:T(128)} %param.11) | copy-start | bytes 196
  156.7 4.2 %collective-permute-start.5 = (f32[4,4,768]{2,1,0:T(4,128)S(1)}, f32[4,4,768]{2,1,0:T(4,128)S(1)}, u32[]{:S(2)}, u32[]{:S(2)}) collective-permute-start(f32[4,4,768]{2,1,0:T(4,128)S(1)} %pad_maximum_fusion.1), channel_id=1, source_target_pairs={{0,2},{2,0},{4,6},{6,4},{8,10},{10,8},{12,14},{14,12},{16,18},{18,... | collective-permute-start | bytes 147464 | tf_op jit(solution)/shard_map/ppermute | solution.py:43
  161.0 5.7 %collective-permute-start.6 = (f32[4,4,768]{2,1,0:T(4,128)S(1)}, f32[4,4,768]{2,1,0:T(4,128)S(1)}, u32[]{:S(2)}, u32[]{:S(2)}) collective-permute-start(f32[4,4,768]{2,1,0:T(4,128)S(1)} %pad_maximum_fusion.2), channel_id=1, source_target_pairs={{0,4},{2,6},{4,0},{6,2},{8,12},{10,14},{12,8},{14,10},{16,20},{18,... | collective-permute-start | bytes 147464 | tf_op jit(solution)/shard_map/ppermute | solution.py:43
  166.7 4.5 %collective-permute-start.7 = (f32[4,4,768]{2,1,0:T(4,128)S(1)}, f32[4,4,768]{2,1,0:T(4,128)S(1)}, u32[]{:S(2)}, u32[]{:S(2)}) collective-permute-start(f32[4,4,768]{2,1,0:T(4,128)S(1)} %pad_maximum_fusion.3), channel_id=1, source_target_pairs={{0,8},{2,10},{4,12},{6,14},{8,0},{10,2},{12,4},{14,6},{16,24},{18,... | collective-permute-start | bytes 147464 | tf_op jit(solution)/shard_map/ppermute | solution.py:43
  171.3 5.7 %collective-permute-start.8 = (f32[4,4,768]{2,1,0:T(4,128)S(1)}, f32[4,4,768]{2,1,0:T(4,128)S(1)}, u32[]{:S(2)}, u32[]{:S(2)}) collective-permute-start(f32[4,4,768]{2,1,0:T(4,128)S(1)} %pad_maximum_fusion.4), channel_id=1, source_target_pairs={{0,16},{2,18},{4,20},{6,22},{8,24},{10,26},{12,28},{14,30},{16,0},... | collective-permute-start | bytes 147464 | tf_op jit(solution)/shard_map/ppermute | solution.py:43
  177.1 1.2 collective-permute-start.9
  178.5 3.6 %collective-permute-start.10 = (f32[16]{0:T(128)S(1)}, f32[16]{0:T(128)S(1)}, u32[]{:S(2)}, u32[]{:S(2)}) collective-permute-start(f32[16]{0:T(128)S(1)} %select_reduce_fusion.4), channel_id=1, source_target_pairs={{0,32},{32,0},{64,96},{96,64},{1,33},{33,1},{65,97},{97,65},{2,34}... | collective-permute-start | bytes 200 | tf_op jit(solution)/shard_map/ppermute | solution.py:43
  182.1 5.1 %collective-permute-start.11 = (f32[16]{0:T(128)S(1)}, f32[16]{0:T(128)S(1)}, u32[]{:S(2)}, u32[]{:S(2)}) collective-permute-start(f32[16]{0:T(128)S(1)} %add.175), channel_id=1, source_target_pairs={{0,64},{32,96},{64,0},{96,32},{1,65},{33,97},{65,1},{97,33},{2,66}... | collective-permute-start | bytes 200 | tf_op jit(solution)/shard_map/ppermute | solution.py:43
Sparse Core Ops, SparseCore 0:
  11.1 92.0 all-gather.1

commit v2 on v1

--- a/solution.py
+++ b/solution.py
@@ -61,6 +61,7 @@
     other = lax.ppermute(head_weight, "core", [(0, 1), (1, 0)])
     first = core == 0
     weight = jnp.concatenate([jnp.where(first, head_weight, other), jnp.where(first, other, head_weight)], axis=1)
+    weight = lax.optimization_barrier(weight)
     offset = chip * (n_core * vocab_dev)
     half_len = rows.shape[1]
     tokens = xor_gather(token_ids.T, "chip", n_chip, chip)

time: 195 us -> 187 us (0.959)
  matrix products: 44.9 us -> 36.5 us
  waiting for transfers between devices: 96.3 us -> 88 us
  other arithmetic: 21.1 us -> 29.2 us
    dot_general x4, matrix products: 44.9 us -> 36.5 us  [block_stats(): logits = jnp.dot(rows, weight, preferred_element_type=jnp.float32)]
    all_gather x1, waiting for transfers between devices: 67.1 us -> 58.9 us  [body(): rows = lax.all_gather(normed, 'chip', axis=1, tiled=True)]
    concatenate x0 -> x1, other arithmetic: none -> 8.24 us  [body(): jnp.concatenate([jnp.where(first, head_weight, other), jnp.where(first, o...]
  transfers between devices with their start and end apart: 13 -> 13, of which waited for: 12 -> 12; matrix products, arithmetic and copies ran while one was open for 4% -> 9% of each run, Pallas kernels for 0% -> 0%
where the time goes in v2:
time: 187 us; the launch traced here: 186 us
  waiting for transfers between devices  88 us (47%)
  matrix products  36.5 us (20%)
  other arithmetic  29.2 us (16%)
  starting transfers between devices  17.4 us (9%)
  between operations  14.4 us (8%)
    all_gather x1, waiting for transfers between devices, body(): rows = lax.all_gather(normed, 'chip', axis=1, tiled=True)  58.9 us
    dot_general x4, matrix products, block_stats(): logits = jnp.dot(rows, weight, preferred_element_type=jnp.float32)  36.5 us
    ppermute x6, waiting for transfers between devices, xor_reduce(): x = combine(x, lax.ppermute(x, axis, [(i, i ^ bit) for i in range(size)]))  17.6 us
    ppermute x4, waiting for transfers between devices, xor_gather(): other = lax.ppermute(x, axis, [(i, i ^ bit) for i in range(size)])  10.5 us
    ppermute x6, starting transfers between devices, xor_reduce(): x = combine(x, lax.ppermute(x, axis, [(i, i ^ bit) for i in range(size)]))  9.71 us
    concatenate x1, other arithmetic, body(): jnp.concatenate([jnp.where(first, head_weight, other), jnp.where(first, o...  8.24 us
    reduce_sum x2, other arithmetic, block_stats(): exp_total = jnp.sum(exps, axis=1)  8.02 us
    ppermute x4, starting transfers between devices, xor_gather(): other = lax.ppermute(x, axis, [(i, i ^ bit) for i in range(size)])  7.44 us
  transfers between devices with their start and end apart: 13, of which 12 were waited for; matrix products, arithmetic and copies ran while one was open for 9% of the time, Pallas kernels for 0%

profile of v2, /device:TPU:2, one launch (start us, length us, event | category | flops | bytes accessed | tf_op | source)
XLA Modules:
  0.0 186.4 jit_solution(1461272241698379592)
XLA Ops:
  7.2 0.0 all-gather.2.cloned.1.call-start
  7.2 1.4 fusion.8
  8.6 2.3 %fusion.10 = bf16[4,48,2048]{2,1,0:T(8,128)(2,1)} fusion(bf16[4,48,2048]{2,1,0:T(8,128)(2,1)} %param.6, f32[2048]{0:T(1024)} %param.7, f32[4,48]{1,0:T(4,128)S(1)} %add_rsqrt_fusion), kind=kLoop, calls=%fused_computation.35 | loop fusion | flops 1572864 | bytes 1581824 | tf_op jit(solution)/shard_map/convert_element_type | solution.py:59
  10.9 0.0 all-gather.2.cloned.1.call-update
  10.9 0.1 collective-permute-start
  11.0 0.5 collective-permute-start.1
  11.5 3.4 %collective-permute-done.1 = s32[48,4]{0,1:T(4,128)S(1)} collective-permute-done((s32[48,4]{0,1:T(4,128)}, s32[48,4]{0,1:T(4,128)S(1)}, u32[]{:S(2)}, u32[]{:S(2)}) %collective-permute-start.1) | collective-permute-done | bytes 800 | tf_op jit(solution)/shard_map/ppermute | solution.py:33
  14.9 0.7 broadcast_select_fusion.7
  15.6 0.1 pad_add_fusion.3
  15.6 2.1 %collective-permute-start.2 = (s32[96,4]{0,1:T(4,128)S(1)}, s32[96,4]{0,1:T(4,128)S(1)}, u32[]{:S(2)}, u32[]{:S(2)}) collective-permute-start(s32[96,4]{0,1:T(4,128)S(1)} %pad_add_fusion.3), channel_id=1, source_target_pairs={{0,4},{2,6},{4,0},{6,2},{8,12},{10,14},{12,8},{14,10},{16,20},{18,... | collective-permute-start | bytes 4616 | tf_op jit(solution)/shard_map/ppermute | solution.py:33
  17.8 3.0 %collective-permute-done.2 = s32[96,4]{0,1:T(4,128)S(1)} collective-permute-done((s32[96,4]{0,1:T(4,128)S(1)}, s32[96,4]{0,1:T(4,128)S(1)}, u32[]{:S(2)}, u32[]{:S(2)}) %collective-permute-start.2) | collective-permute-done | bytes 1568 | tf_op jit(solution)/shard_map/ppermute | solution.py:33
  20.7 0.1 broadcast_select_fusion.9
  20.8 0.1 pad_add_fusion.1
  20.9 1.6 collective-permute-start.3
  22.5 2.0 %collective-permute-done.3 = s32[192,4]{0,1:T(4,128)S(1)} collective-permute-done((s32[192,4]{0,1:T(4,128)S(1)}, s32[192,4]{0,1:T(4,128)S(1)}, u32[]{:S(2)}, u32[]{:S(2)}) %collective-permute-start.3) | collective-permute-done | bytes 3104 | tf_op jit(solution)/shard_map/ppermute | solution.py:33
  24.5 0.1 broadcast_select_fusion.5
  24.6 0.1 pad_add_fusion
  24.7 3.2 %collective-permute-start.4 = (s32[384,4]{0,1:T(4,128)S(1)}, s32[384,4]{0,1:T(4,128)S(1)}, u32[]{:S(2)}, u32[]{:S(2)}) collective-permute-start(s32[384,4]{0,1:T(4,128)S(1)} %pad_add_fusion), channel_id=1, source_target_pairs={{0,16},{2,18},{4,20},{6,22},{8,24},{10,26},{12,28},{14,30},{16,0},... | collective-permute-start | bytes 18440 | tf_op jit(solution)/shard_map/ppermute | solution.py:33
  27.9 2.1 %collective-permute-done.4 = s32[384,4]{0,1:T(4,128)S(1)} collective-permute-done((s32[384,4]{0,1:T(4,128)S(1)}, s32[384,4]{0,1:T(4,128)S(1)}, u32[]{:S(2)}, u32[]{:S(2)}) %collective-permute-start.4) | collective-permute-done | bytes 6176 | tf_op jit(solution)/shard_map/ppermute | solution.py:33
  30.0 0.1 broadcast_select_fusion.3
  30.1 0.0 collective-permute-done
  30.1 5.9 %broadcast_select_fusion.1 = (bf16[2048,1000]{0,1:T(8,128)(2,1)}, bf16[2048,1000]{0,1:T(8,128)(2,1)}) fusion(bf16[2048,1000]{0,1:T(8,128)(2,1)} %param.8, bf16[2048,1000]{0,1:T(8,128)(2,1)} %collective-permute-done, pred[]{:T(512)S(6)} %eq.91), kind=kLoop, calls=%fused_computation.22 | loop fusion | flops 4096000 | bytes 16384001 | tf_op jit(solution)/shard_map/jit(_where)/select_n | solution.py:63
  36.0 8.2 %pad_maximum_fusion = bf16[2048,2000]{0,1:T(8,128)(2,1)} fusion(bf16[2048,1000]{0,1:T(8,128)(2,1)} %get-tuple-element.32, bf16[2048,1000]{0,1:T(8,128)(2,1)} %get-tuple-element.31), kind=kLoop, calls=%fused_computation | loop fusion | flops 16384000 | bytes 16384000 | tf_op jit(solution)/shard_map/concatenate | solution.py:63
  44.3 58.9 %all-gather.2.cloned.1.call-done = bf16[4,768,2048]{2,1,0:T(8,128)(2,1)} async-done(((bf16[4,48,2048]{2,1,0:T(8,128)(2,1)}), bf16[4,768,2048]{2,1,0:T(8,128)(2,1)}) %all-gather.2.cloned.1.call-update) | async-done | bytes 12582928 | tf_op jit(solution)/shard_map/all_gather | solution.py:60
  103.1 0.0 copy-start
  103.1 10.1 %fusion.63 = (f32[768]{0:T(1024)S(1)}, f32[768,2000]{0,1:T(8,128)S(1)}) fusion(bf16[2048,2000]{0,1:T(8,128)(2,1)} %pad_maximum_fusion, bf16[4,768,2048]{2,1,0:T(8,128)(2,1)} %all-gather.2.cloned.1.call-done), kind=kOutput, calls=%fused_computation.179 | convolution fusion | flops 6292990976 | bytes 17484800 | tf_op jit(solution)/shard_map/dot_general | solution.py:13
  113.2 0.0 copy-done
  113.2 8.7 %fusion.62 = (f32[768]{0:T(1024)S(1)}, f32[768,2000]{0,1:T(8,128)S(1)}) fusion(bf16[2048,2000]{0,1:T(8,128)(2,1)S(1)} %copy-done, bf16[4,768,2048]{2,1,0:T(8,128)(2,1)} %all-gather.2.cloned.1.call-done), kind=kOutput, calls=%fused_computation.178 | convolution fusion | flops 6292990976 | bytes 17484800 | tf_op jit(solution)/shard_map/dot_general | solution.py:13
  122.0 4.1 %fusion.2 = (f32[768]{0:T(1024)S(1)}, f32[768]{0:T(1024)S(1)}, f32[768]{0:T(1024)S(1)}, f32[768]{0:T(1024)S(1)}, f32[768]{0:T(1024)S(1)}, /*index=5*/f32[768]{0:T(1024)S(1)}) fusion(f32[768,2000]{0,1:T(8,128)S(1)} %get-tuple-element.58, f32[768]{0:T(1024)S(1)} %get-tuple-element.57, s32[768]{0:T(1024)S(1)} %get-tuple-element.16, ...), kind=kLoop, calls=%fused_computation.15 | loop fusion | flops 21499392 | bytes 12318720 | tf_op jit(solution)/shard_map/reduce_sum | solution.py:16
  126.3 8.7 %fusion.61 = (f32[768]{0:T(1024)S(1)}, f32[768,2000]{0,1:T(8,128)S(1)}) fusion(bf16[2048,2000]{0,1:T(8,128)(2,1)S(1)} %copy-done, bf16[4,768,2048]{2,1,0:T(8,128)(2,1)} %all-gather.2.cloned.1.call-done), kind=kOutput, calls=%fused_computation.177 | convolution fusion | flops 6292990976 | bytes 17484800 | tf_op jit(solution)/shard_map/dot_general | solution.py:13
  135.0 9.0 %fusion.60 = (f32[768]{0:T(1024)S(1)}, f32[768,2000]{0,1:T(8,128)S(1)}) fusion(bf16[2048,2000]{0,1:T(8,128)(2,1)S(1)} %copy-done, bf16[4,768,2048]{2,1,0:T(8,128)(2,1)} %all-gather.2.cloned.1.call-done), kind=kOutput, calls=%fused_computation.176 | convolution fusion | flops 6292990976 | bytes 17484800 | tf_op jit(solution)/shard_map/dot_general | solution.py:13
  144.0 0.0 copy-start.2
  144.0 0.0 copy-start.1
  144.0 3.9 %fusion = (f32[768]{0:T(1024)S(1)}, f32[768]{0:T(1024)S(1)}, f32[768]{0:T(1024)S(1)}, f32[768]{0:T(1024)S(1)}, f32[768]{0:T(1024)S(1)}, /*index=5*/f32[768]{0:T(1024)S(1)}) fusion(f32[768,2000]{0,1:T(8,128)S(1)} %get-tuple-element.54, f32[768]{0:T(1024)S(1)} %get-tuple-element.53, s32[768]{0:T(1024)S(1)} %get-tuple-element.17, ...), kind=kLoop, calls=%fused_computation.5 | loop fusion | flops 21499392 | bytes 12318720 | tf_op jit(solution)/shard_map/reduce_sum | solution.py:16
  148.1 0.1 pad_maximum_fusion.1
  148.2 0.6 collective-permute-start.5
  148.8 3.5 %collective-permute-done.5 = f32[4,4,768]{2,1,0:T(4,128)S(1)} collective-permute-done((f32[4,4,768]{2,1,0:T(4,128)S(1)}, f32[4,4,768]{2,1,0:T(4,128)S(1)}, u32[]{:S(2)}, u32[]{:S(2)}) %collective-permute-start.5) | collective-permute-done | bytes 49184 | tf_op jit(solution)/shard_map/ppermute | solution.py:43
  152.4 2.2 %collective-permute-start.6 = (f32[4,4,768]{2,1,0:T(4,128)S(1)}, f32[4,4,768]{2,1,0:T(4,128)S(1)}, u32[]{:S(2)}, u32[]{:S(2)}) collective-permute-start(f32[4,4,768]{2,1,0:T(4,128)S(1)} %pad_maximum_fusion.2), channel_id=1, source_target_pairs={{0,4},{2,6},{4,0},{6,2},{8,12},{10,14},{12,8},{14,10},{16,20},{18,... | collective-permute-start | bytes 147464 | tf_op jit(solution)/shard_map/ppermute | solution.py:43
  154.6 3.5 %collective-permute-done.6 = f32[4,4,768]{2,1,0:T(4,128)S(1)} collective-permute-done((f32[4,4,768]{2,1,0:T(4,128)S(1)}, f32[4,4,768]{2,1,0:T(4,128)S(1)}, u32[]{:S(2)}, u32[]{:S(2)}) %collective-permute-start.6) | collective-permute-done | bytes 49184 | tf_op jit(solution)/shard_map/ppermute | solution.py:43
  158.2 0.3 collective-permute-start.7
  158.5 4.2 %collective-permute-done.7 = f32[4,4,768]{2,1,0:T(4,128)S(1)} collective-permute-done((f32[4,4,768]{2,1,0:T(4,128)S(1)}, f32[4,4,768]{2,1,0:T(4,128)S(1)}, u32[]{:S(2)}, u32[]{:S(2)}) %collective-permute-start.7) | collective-permute-done | bytes 49184 | tf_op jit(solution)/shard_map/ppermute | solution.py:43
  162.7 1.9 collective-permute-start.8
  164.6 0.0 copy-done.2
  164.6 0.1 dynamic_slice.9
  164.7 3.7 %collective-permute-done.8 = f32[4,4,768]{2,1,0:T(4,128)S(1)} collective-permute-done((f32[4,4,768]{2,1,0:T(4,128)S(1)}, f32[4,4,768]{2,1,0:T(4,128)S(1)}, u32[]{:S(2)}, u32[]{:S(2)}) %collective-permute-start.8) | collective-permute-done | bytes 49184 | tf_op jit(solution)/shard_map/ppermute | solution.py:43
  168.4 0.2 fusion.57
  168.6 0.1 collective-permute-start.9
  168.7 1.1 collective-permute-done.9
  169.8 0.1 select_reduce_fusion.4
  169.9 1.6 collective-permute-start.10
  171.5 0.6 constant_dynamic-slice_fusion.8
  172.2 1.4 collective-permute-done.10
  173.5 3.1 %collective-permute-start.11 = (f32[16]{0:T(128)S(1)}, f32[16]{0:T(128)S(1)}, u32[]{:S(2)}, u32[]{:S(2)}) collective-permute-start(f32[16]{0:T(128)S(1)} %add.175), channel_id=1, source_target_pairs={{0,64},{32,96},{64,0},{96,32},{1,65},{33,97},{65,1},{97,33},{2,66}... | collective-permute-start | bytes 200 | tf_op jit(solution)/shard_map/ppermute | solution.py:43
  176.7 0.7 fusion.56
  177.3 1.3 collective-permute-done.11
  178.6 0.0 copy-done.1
  178.6 0.2 fusion.32
  178.8 0.2 fusion.33
  179.0 0.5 maximum_divide_fusion
  (42 shorter events, 0.5 us)
Async XLA Ops:
  7.2 96.0 %all-gather.2.cloned.1.call-start = ((), (), s32[]{:S(2)}) async-start(), calls=%async_computation | async-start | bytes 13369344 | tf_op jit(solution)/shard_map/all_gather | solution.py:60
  10.9 19.2 %collective-permute-start = (bf16[2048,1000]{0,1:T(8,128)(2,1)}, bf16[2048,1000]{0,1:T(8,128)(2,1)}, u32[]{:S(2)}, u32[]{:S(2)}) collective-permute-start(bf16[2048,1000]{0,1:T(8,128)(2,1)} %param.8), channel_id=1, source_target_pairs={{0,1},{1,0},{2,3},{3,2},{4,5},{5,4},{6,7},{7,6},{8,9},{9,8},{10,11... | collective-permute-start | bytes 12288008 | tf_op jit(solution)/shard_map/ppermute | solution.py:61
  11.0 3.9 %collective-permute-start.1 = (s32[48,4]{0,1:T(4,128)}, s32[48,4]{0,1:T(4,128)S(1)}, u32[]{:S(2)}, u32[]{:S(2)}) collective-permute-start(s32[48,4]{0,1:T(4,128)} %bitcast.175), channel_id=1, source_target_pairs={{0,2},{2,0},{4,6},{6,4},{8,10},{10,8},{12,14},{14,12},{16,18},{18,... | collective-permute-start | bytes 2312 | tf_op jit(solution)/shard_map/ppermute | solution.py:33
  15.6 5.1 %collective-permute-start.2 = (s32[96,4]{0,1:T(4,128)S(1)}, s32[96,4]{0,1:T(4,128)S(1)}, u32[]{:S(2)}, u32[]{:S(2)}) collective-permute-start(s32[96,4]{0,1:T(4,128)S(1)} %pad_add_fusion.3), channel_id=1, source_target_pairs={{0,4},{2,6},{4,0},{6,2},{8,12},{10,14},{12,8},{14,10},{16,20},{18,... | collective-permute-start | bytes 4616 | tf_op jit(solution)/shard_map/ppermute | solution.py:33
  20.9 3.6 %collective-permute-start.3 = (s32[192,4]{0,1:T(4,128)S(1)}, s32[192,4]{0,1:T(4,128)S(1)}, u32[]{:S(2)}, u32[]{:S(2)}) collective-permute-start(s32[192,4]{0,1:T(4,128)S(1)} %pad_add_fusion.1), channel_id=1, source_target_pairs={{0,8},{2,10},{4,12},{6,14},{8,0},{10,2},{12,4},{14,6},{16,24},{18,... | collective-permute-start | bytes 9224 | tf_op jit(solution)/shard_map/ppermute | solution.py:33
  24.7 5.3 %collective-permute-start.4 = (s32[384,4]{0,1:T(4,128)S(1)}, s32[384,4]{0,1:T(4,128)S(1)}, u32[]{:S(2)}, u32[]{:S(2)}) collective-permute-start(s32[384,4]{0,1:T(4,128)S(1)} %pad_add_fusion), channel_id=1, source_target_pairs={{0,16},{2,18},{4,20},{6,22},{8,24},{10,26},{12,28},{14,30},{16,0},... | collective-permute-start | bytes 18440 | tf_op jit(solution)/shard_map/ppermute | solution.py:33
  103.1 10.1 %copy-start = (bf16[2048,2000]{0,1:T(8,128)(2,1)S(1)}, bf16[2048,2000]{0,1:T(8,128)(2,1)}, u32[]{:S(2)}) copy-start(bf16[2048,2000]{0,1:T(8,128)(2,1)} %pad_maximum_fusion) | copy-start | bytes 24576004
  144.0 20.6 %copy-start.2 = (s32[16]{0:T(128)S(1)}, s32[16]{0:T(128)}, u32[]{:S(2)}) copy-start(s32[16]{0:T(128)} %param.10) | copy-start | bytes 196
  144.0 34.6 %copy-start.1 = (s32[16]{0:T(128)S(1)}, s32[16]{0:T(128)}, u32[]{:S(2)}) copy-start(s32[16]{0:T(128)} %param.11) | copy-start | bytes 196
  148.2 4.2 %collective-permute-start.5 = (f32[4,4,768]{2,1,0:T(4,128)S(1)}, f32[4,4,768]{2,1,0:T(4,128)S(1)}, u32[]{:S(2)}, u32[]{:S(2)}) collective-permute-start(f32[4,4,768]{2,1,0:T(4,128)S(1)} %pad_maximum_fusion.1), channel_id=1, source_target_pairs={{0,2},{2,0},{4,6},{6,4},{8,10},{10,8},{12,14},{14,12},{16,18},{18,... | collective-permute-start | bytes 147464 | tf_op jit(solution)/shard_map/ppermute | solution.py:43
  152.4 5.7 %collective-permute-start.6 = (f32[4,4,768]{2,1,0:T(4,128)S(1)}, f32[4,4,768]{2,1,0:T(4,128)S(1)}, u32[]{:S(2)}, u32[]{:S(2)}) collective-permute-start(f32[4,4,768]{2,1,0:T(4,128)S(1)} %pad_maximum_fusion.2), channel_id=1, source_target_pairs={{0,4},{2,6},{4,0},{6,2},{8,12},{10,14},{12,8},{14,10},{16,20},{18,... | collective-permute-start | bytes 147464 | tf_op jit(solution)/shard_map/ppermute | solution.py:43
  158.2 4.5 %collective-permute-start.7 = (f32[4,4,768]{2,1,0:T(4,128)S(1)}, f32[4,4,768]{2,1,0:T(4,128)S(1)}, u32[]{:S(2)}, u32[]{:S(2)}) collective-permute-start(f32[4,4,768]{2,1,0:T(4,128)S(1)} %pad_maximum_fusion.3), channel_id=1, source_target_pairs={{0,8},{2,10},{4,12},{6,14},{8,0},{10,2},{12,4},{14,6},{16,24},{18,... | collective-permute-start | bytes 147464 | tf_op jit(solution)/shard_map/ppermute | solution.py:43
  162.7 5.7 %collective-permute-start.8 = (f32[4,4,768]{2,1,0:T(4,128)S(1)}, f32[4,4,768]{2,1,0:T(4,128)S(1)}, u32[]{:S(2)}, u32[]{:S(2)}) collective-permute-start(f32[4,4,768]{2,1,0:T(4,128)S(1)} %pad_maximum_fusion.4), channel_id=1, source_target_pairs={{0,16},{2,18},{4,20},{6,22},{8,24},{10,26},{12,28},{14,30},{16,0},... | collective-permute-start | bytes 147464 | tf_op jit(solution)/shard_map/ppermute | solution.py:43
  168.6 1.2 collective-permute-start.9
  169.9 3.6 %collective-permute-start.10 = (f32[16]{0:T(128)S(1)}, f32[16]{0:T(128)S(1)}, u32[]{:S(2)}, u32[]{:S(2)}) collective-permute-start(f32[16]{0:T(128)S(1)} %select_reduce_fusion.4), channel_id=1, source_target_pairs={{0,32},{32,0},{64,96},{96,64},{1,33},{33,1},{65,97},{97,65},{2,34}... | collective-permute-start | bytes 200 | tf_op jit(solution)/shard_map/ppermute | solution.py:43
  173.5 5.1 %collective-permute-start.11 = (f32[16]{0:T(128)S(1)}, f32[16]{0:T(128)S(1)}, u32[]{:S(2)}, u32[]{:S(2)}) collective-permute-start(f32[16]{0:T(128)S(1)} %add.175), channel_id=1, source_target_pairs={{0,64},{32,96},{64,0},{96,32},{1,65},{33,97},{65,1},{97,33},{2,66}... | collective-permute-start | bytes 200 | tf_op jit(solution)/shard_map/ppermute | solution.py:43
Sparse Core Ops, SparseCore 0:
  11.0 92.0 all-gather.1

commit v3 on v2

--- a/solution.py
+++ b/solution.py
@@ -6,7 +6,7 @@
 from jax.sharding import PartitionSpec as P
 
 norm_eps = 1e-06
-BLOCK = 768
+BLOCK = 1536
 
 
 def block_stats(rows, tokens, weight, offset):
@@ -66,14 +66,13 @@
     half_len = rows.shape[1]
     tokens = xor_gather(token_ids.T, "chip", n_chip, chip)
     own_lengths = lax.dynamic_slice_in_dim(lengths, req_index * req_dev, req_dev)
-    per_request = []
-    for k in range(req_dev):
-        blocks = []
-        for start in range(0, half_len, BLOCK):
-            size = min(BLOCK, half_len - start)
-            blocks.append(block_stats(rows[k, start : start + size], tokens[start : start + size, k], weight, offset))
-        per_request.append(jnp.concatenate(blocks, axis=1))
-    stats = jnp.stack(per_request, axis=1)
+    flat_rows = rows.reshape(req_dev * half_len, model_width)
+    flat_tokens = tokens.T.reshape(req_dev * half_len)
+    blocks = []
+    for start in range(0, req_dev * half_len, BLOCK):
+        size = min(BLOCK, req_dev * half_len - start)
+        blocks.append(block_stats(flat_rows[start : start + size], flat_tokens[start : start + size], weight, offset))
+    stats = jnp.concatenate(blocks, axis=1).reshape(4, req_dev, half_len)
     stats = xor_reduce(stats, "chip", n_chip, merge)
     row_top, exp_total, moment, token_logit = stats[0], stats[1], stats[2], stats[3]
     log_total = row_top + jnp.log(exp_total)

time: 187 us -> 184 us (0.984)
  matrix products: 36.5 us -> 26.6 us
  local copies, waits for them, and re-layouts: 0.85 us -> 7.41 us
    dot_general x4 -> x2, matrix products: 36.5 us -> 26.6 us  [block_stats(): logits = jnp.dot(rows, weight, preferred_element_type=jnp.float32)]
    slice x0 -> x2, local copies, waits for them, and re-layouts: none -> 5.79 us  [the longest x1 5.65 us: body(): flat_rows[start:start + size]]
where the time goes in v3:
time: 184 us
  waiting for transfers between devices  88.4 us (48%)
  other arithmetic  29.7 us (16%)
  matrix products  26.6 us (14%)
  starting transfers between devices  17.3 us (9%)
  between operations  14.3 us (8%)
  local copies, waits for them, and re-layouts  7.41 us (4%)
    all_gather x1, waiting for transfers between devices, body(): rows = lax.all_gather(normed, 'chip', axis=1, tiled=True)  58.9 us
    dot_general x2, matrix products, block_stats(): logits = jnp.dot(rows, weight, preferred_element_type=jnp.float32)  26.6 us
    ppermute x6, waiting for transfers between devices, xor_reduce(): x = combine(x, lax.ppermute(x, axis, [(i, i ^ bit) for i in range(size)]))  18 us
    ppermute x4, waiting for transfers between devices, xor_gather(): other = lax.ppermute(x, axis, [(i, i ^ bit) for i in range(size)])  10.5 us
    ppermute x6, starting transfers between devices, xor_reduce(): x = combine(x, lax.ppermute(x, axis, [(i, i ^ bit) for i in range(size)]))  9.69 us
    reduce_sum x2, other arithmetic, block_stats(): exp_total = jnp.sum(exps, axis=1)  8.57 us
    concatenate x1, other arithmetic, body(): jnp.concatenate([jnp.where(first, head_weight, other), jnp.where(first, o...  8.24 us
    ppermute x4, starting transfers between devices, xor_gather(): other = lax.ppermute(x, axis, [(i, i ^ bit) for i in range(size)])  7.44 us
  transfers between devices with their start and end apart: 13, of which 12 were waited for; matrix products, arithmetic and copies ran while one was open for 9% of the time, Pallas kernels for 0%

profile of v3, /device:TPU:2, one launch (start us, length us, event | category | flops | bytes accessed | tf_op | source)
XLA Modules:
  0.0 183.8 jit_solution(10465221233232633836)
XLA Ops:
  7.2 0.0 all-gather.2.cloned.1.call-start
  7.2 1.4 fusion.2
  8.6 2.3 %fusion.4 = bf16[4,48,2048]{2,1,0:T(8,128)(2,1)} fusion(bf16[4,48,2048]{2,1,0:T(8,128)(2,1)} %param.6, f32[2048]{0:T(1024)} %param.7, f32[4,48]{1,0:T(4,128)S(1)} %add_rsqrt_fusion), kind=kLoop, calls=%fused_computation.17 | loop fusion | flops 1572864 | bytes 1581824 | tf_op jit(solution)/shard_map/convert_element_type | solution.py:59
  10.9 0.0 all-gather.2.cloned.1.call-update
  10.9 0.1 collective-permute-start
  11.0 0.5 collective-permute-start.1
  11.5 3.4 %collective-permute-done.1 = s32[48,4]{0,1:T(4,128)S(1)} collective-permute-done((s32[48,4]{0,1:T(4,128)}, s32[48,4]{0,1:T(4,128)S(1)}, u32[]{:S(2)}, u32[]{:S(2)}) %collective-permute-start.1) | collective-permute-done | bytes 800 | tf_op jit(solution)/shard_map/ppermute | solution.py:33
  14.9 0.7 broadcast_select_fusion.7
  15.6 0.1 pad_add_fusion.2
  15.6 2.1 %collective-permute-start.2 = (s32[96,4]{0,1:T(4,128)S(1)}, s32[96,4]{0,1:T(4,128)S(1)}, u32[]{:S(2)}, u32[]{:S(2)}) collective-permute-start(s32[96,4]{0,1:T(4,128)S(1)} %pad_add_fusion.2), channel_id=1, source_target_pairs={{0,4},{2,6},{4,0},{6,2},{8,12},{10,14},{12,8},{14,10},{16,20},{18,... | collective-permute-start | bytes 4616 | tf_op jit(solution)/shard_map/ppermute | solution.py:33
  17.8 3.0 %collective-permute-done.2 = s32[96,4]{0,1:T(4,128)S(1)} collective-permute-done((s32[96,4]{0,1:T(4,128)S(1)}, s32[96,4]{0,1:T(4,128)S(1)}, u32[]{:S(2)}, u32[]{:S(2)}) %collective-permute-start.2) | collective-permute-done | bytes 1568 | tf_op jit(solution)/shard_map/ppermute | solution.py:33
  20.7 0.1 broadcast_select_fusion.9
  20.8 0.1 pad_add_fusion.1
  20.9 1.6 collective-permute-start.3
  22.5 2.0 %collective-permute-done.3 = s32[192,4]{0,1:T(4,128)S(1)} collective-permute-done((s32[192,4]{0,1:T(4,128)S(1)}, s32[192,4]{0,1:T(4,128)S(1)}, u32[]{:S(2)}, u32[]{:S(2)}) %collective-permute-start.3) | collective-permute-done | bytes 3104 | tf_op jit(solution)/shard_map/ppermute | solution.py:33
  24.5 0.1 broadcast_select_fusion.5
  24.6 0.1 pad_add_fusion
  24.7 3.2 %collective-permute-start.4 = (s32[384,4]{0,1:T(4,128)S(1)}, s32[384,4]{0,1:T(4,128)S(1)}, u32[]{:S(2)}, u32[]{:S(2)}) collective-permute-start(s32[384,4]{0,1:T(4,128)S(1)} %pad_add_fusion), channel_id=1, source_target_pairs={{0,16},{2,18},{4,20},{6,22},{8,24},{10,26},{12,28},{14,30},{16,0},... | collective-permute-start | bytes 18440 | tf_op jit(solution)/shard_map/ppermute | solution.py:33
  27.9 2.1 %collective-permute-done.4 = s32[384,4]{0,1:T(4,128)S(1)} collective-permute-done((s32[384,4]{0,1:T(4,128)S(1)}, s32[384,4]{0,1:T(4,128)S(1)}, u32[]{:S(2)}, u32[]{:S(2)}) %collective-permute-start.4) | collective-permute-done | bytes 6176 | tf_op jit(solution)/shard_map/ppermute | solution.py:33
  30.0 0.1 broadcast_select_fusion.3
  30.1 0.0 collective-permute-done
  30.1 5.9 %broadcast_select_fusion.1 = (bf16[2048,1000]{0,1:T(8,128)(2,1)}, bf16[2048,1000]{0,1:T(8,128)(2,1)}) fusion(bf16[2048,1000]{0,1:T(8,128)(2,1)} %param.8, bf16[2048,1000]{0,1:T(8,128)(2,1)} %collective-permute-done, pred[]{:T(512)S(6)} %eq.28), kind=kLoop, calls=%fused_computation.12 | loop fusion | flops 4096000 | bytes 16384001 | tf_op jit(solution)/shard_map/jit(_where)/select_n | solution.py:63
  36.0 8.2 %pad_maximum_fusion = bf16[2048,2000]{0,1:T(8,128)(2,1)} fusion(bf16[2048,1000]{0,1:T(8,128)(2,1)} %get-tuple-element.28, bf16[2048,1000]{0,1:T(8,128)(2,1)} %get-tuple-element.27), kind=kLoop, calls=%fused_computation.10 | loop fusion | flops 16384000 | bytes 16384000 | tf_op jit(solution)/shard_map/concatenate | solution.py:63
  44.3 58.9 %all-gather.2.cloned.1.call-done = bf16[4,768,2048]{2,1,0:T(8,128)(2,1)} async-done(((bf16[4,48,2048]{2,1,0:T(8,128)(2,1)}), bf16[4,768,2048]{2,1,0:T(8,128)(2,1)}) %all-gather.2.cloned.1.call-update) | async-done | bytes 12582928 | tf_op jit(solution)/shard_map/all_gather | solution.py:60
  103.1 0.0 copy-start
  103.1 5.7 %fusion.48 = (bf16[2,768,2048]{2,1,0:T(8,128)(2,1)S(1)}, bf16[2,768,2048]{2,1,0:T(8,128)(2,1)S(1)}) fusion(bf16[4,768,2048]{2,1,0:T(8,128)(2,1)} %all-gather.2.cloned.1.call-done), kind=kLoop, calls=%fused_computation.146 | loop fusion | bytes 25165824 | tf_op jit(solution)/shard_map/slice | solution.py:74
  108.8 1.3 copy-done
  110.1 13.3 %fusion.49 = (f32[1536]{0:T(1024)S(1)}, f32[1536,2000]{0,1:T(8,128)S(1)}) fusion(bf16[1536,2048]{1,0:T(8,128)(2,1)S(1)} %bitcast.161, bf16[2048,2000]{0,1:T(8,128)(2,1)S(1)} %copy-done), kind=kOutput, calls=%fused_computation.147 | convolution fusion | flops 12585981952 | bytes 26777600 | tf_op jit(solution)/shard_map/dot_general | solution.py:13
  123.5 4.3 %fusion = (f32[1536]{0:T(1024)S(1)}, f32[1536]{0:T(1024)S(1)}, f32[1536]{0:T(1024)S(1)}) fusion(f32[1536,2000]{0,1:T(8,128)S(1)} %get-tuple-element.56, f32[1536]{0:T(1024)S(1)} %get-tuple-element.55, s32[1536]{0:T(1024)S(1)} %sub.135), kind=kLoop, calls=%fused_computation.4 | loop fusion | flops 21499392 | bytes 12318720 | tf_op jit(solution)/shard_map/reduce_sum | solution.py:16
  127.8 13.3 %fusion.50 = (f32[1536]{0:T(1024)S(1)}, f32[1536,2000]{0,1:T(8,128)S(1)}) fusion(bf16[1536,2048]{1,0:T(8,128)(2,1)S(1)} %bitcast.160, bf16[2048,2000]{0,1:T(8,128)(2,1)S(1)} %copy-done), kind=kOutput, calls=%fused_computation.148 | convolution fusion | flops 12585981952 | bytes 26777600 | tf_op jit(solution)/shard_map/dot_general | solution.py:13
  141.1 0.0 copy-start.2
  141.1 0.0 copy-start.1
  141.1 4.3 %fusion.1 = (f32[1536]{0:T(1024)S(1)}, f32[1536]{0:T(1024)S(1)}, f32[1536]{0:T(1024)S(1)}) fusion(f32[1536,2000]{0,1:T(8,128)S(1)} %get-tuple-element.58, f32[1536]{0:T(1024)S(1)} %get-tuple-element.57, s32[1536]{0:T(1024)S(1)} %sub.131), kind=kLoop, calls=%fused_computation.9 | loop fusion | flops 21499392 | bytes 12318720 | tf_op jit(solution)/shard_map/reduce_sum | solution.py:16
  145.5 0.1 maximum_maximum_fusion
  145.6 0.6 collective-permute-start.5
  146.2 0.1 slice_reduce_fusion.3
  146.4 3.3 %collective-permute-done.5 = f32[4,4,768]{2,1,0:T(4,128)S(1)} collective-permute-done((f32[4,4,768]{2,1,0:T(4,128)S(1)}, f32[4,4,768]{2,1,0:T(4,128)S(1)}, u32[]{:S(2)}, u32[]{:S(2)}) %collective-permute-start.5) | collective-permute-done | bytes 49184 | tf_op jit(solution)/shard_map/ppermute | solution.py:43
  149.8 2.2 %collective-permute-start.6 = (f32[4,4,768]{2,1,0:T(4,128)S(1)}, f32[4,4,768]{2,1,0:T(4,128)S(1)}, u32[]{:S(2)}, u32[]{:S(2)}) collective-permute-start(f32[4,4,768]{2,1,0:T(4,128)S(1)} %pad_maximum_fusion.1), channel_id=1, source_target_pairs={{0,4},{2,6},{4,0},{6,2},{8,12},{10,14},{12,8},{14,10},{16,20},{18,... | collective-permute-start | bytes 147464 | tf_op jit(solution)/shard_map/ppermute | solution.py:43
  152.0 3.5 %collective-permute-done.6 = f32[4,4,768]{2,1,0:T(4,128)S(1)} collective-permute-done((f32[4,4,768]{2,1,0:T(4,128)S(1)}, f32[4,4,768]{2,1,0:T(4,128)S(1)}, u32[]{:S(2)}, u32[]{:S(2)}) %collective-permute-start.6) | collective-permute-done | bytes 49184 | tf_op jit(solution)/shard_map/ppermute | solution.py:43
  155.6 0.3 collective-permute-start.7
  155.9 4.2 %collective-permute-done.7 = f32[4,4,768]{2,1,0:T(4,128)S(1)} collective-permute-done((f32[4,4,768]{2,1,0:T(4,128)S(1)}, f32[4,4,768]{2,1,0:T(4,128)S(1)}, u32[]{:S(2)}, u32[]{:S(2)}) %collective-permute-start.7) | collective-permute-done | bytes 49184 | tf_op jit(solution)/shard_map/ppermute | solution.py:43
  160.1 1.9 %collective-permute-start.8 = (f32[4,4,768]{2,1,0:T(4,128)S(1)}, f32[4,4,768]{2,1,0:T(4,128)S(1)}, u32[]{:S(2)}, u32[]{:S(2)}) collective-permute-start(f32[4,4,768]{2,1,0:T(4,128)S(1)} %pad_maximum_fusion.3), channel_id=1, source_target_pairs={{0,16},{2,18},{4,20},{6,22},{8,24},{10,26},{12,28},{14,30},{16,0},... | collective-permute-start | bytes 147464 | tf_op jit(solution)/shard_map/ppermute | solution.py:43
  162.0 0.0 copy-done.2
  162.0 0.1 dynamic_slice.9
  162.1 3.7 %collective-permute-done.8 = f32[4,4,768]{2,1,0:T(4,128)S(1)} collective-permute-done((f32[4,4,768]{2,1,0:T(4,128)S(1)}, f32[4,4,768]{2,1,0:T(4,128)S(1)}, u32[]{:S(2)}, u32[]{:S(2)}) %collective-permute-start.8) | collective-permute-done | bytes 49184 | tf_op jit(solution)/shard_map/ppermute | solution.py:43
  165.8 0.2 fusion.45
  166.0 0.1 collective-permute-start.9
  166.1 1.1 collective-permute-done.9
  167.2 0.1 select_reduce_fusion.2
  167.3 1.6 collective-permute-start.10
  168.9 2.0 %collective-permute-done.10 = f32[16]{0:T(128)S(1)} collective-permute-done((f32[16]{0:T(128)S(1)}, f32[16]{0:T(128)S(1)}, u32[]{:S(2)}, u32[]{:S(2)}) %collective-permute-start.10) | collective-permute-done | bytes 96 | tf_op jit(solution)/shard_map/ppermute | solution.py:43
  170.9 3.2 %collective-permute-start.11 = (f32[16]{0:T(128)S(1)}, f32[16]{0:T(128)S(1)}, u32[]{:S(2)}, u32[]{:S(2)}) collective-permute-start(f32[16]{0:T(128)S(1)} %add.177), channel_id=1, source_target_pairs={{0,64},{32,96},{64,0},{96,32},{1,65},{33,97},{65,1},{97,33},{2,66}... | collective-permute-start | bytes 200 | tf_op jit(solution)/shard_map/ppermute | solution.py:43
  174.1 0.7 constant_dynamic-slice_fusion.8
  174.7 1.3 collective-permute-done.11
  176.0 0.0 copy-done.1
  176.0 0.2 fusion.25
  176.2 0.2 fusion.26
  176.4 0.5 maximum_divide_fusion
  (38 shorter events, 0.5 us)
Async XLA Ops:
  7.2 96.0 %all-gather.2.cloned.1.call-start = ((), (), s32[]{:S(2)}) async-start(), calls=%async_computation | async-start | bytes 13369344 | tf_op jit(solution)/shard_map/all_gather | solution.py:60
  10.9 19.2 %collective-permute-start = (bf16[2048,1000]{0,1:T(8,128)(2,1)}, bf16[2048,1000]{0,1:T(8,128)(2,1)}, u32[]{:S(2)}, u32[]{:S(2)}) collective-permute-start(bf16[2048,1000]{0,1:T(8,128)(2,1)} %param.8), channel_id=1, source_target_pairs={{0,1},{1,0},{2,3},{3,2},{4,5},{5,4},{6,7},{7,6},{8,9},{9,8},{10,11... | collective-permute-start | bytes 12288008 | tf_op jit(solution)/shard_map/ppermute | solution.py:61
  11.0 3.9 %collective-permute-start.1 = (s32[48,4]{0,1:T(4,128)}, s32[48,4]{0,1:T(4,128)S(1)}, u32[]{:S(2)}, u32[]{:S(2)}) collective-permute-start(s32[48,4]{0,1:T(4,128)} %bitcast.166), channel_id=1, source_target_pairs={{0,2},{2,0},{4,6},{6,4},{8,10},{10,8},{12,14},{14,12},{16,18},{18,... | collective-permute-start | bytes 2312 | tf_op jit(solution)/shard_map/ppermute | solution.py:33
  15.6 5.1 %collective-permute-start.2 = (s32[96,4]{0,1:T(4,128)S(1)}, s32[96,4]{0,1:T(4,128)S(1)}, u32[]{:S(2)}, u32[]{:S(2)}) collective-permute-start(s32[96,4]{0,1:T(4,128)S(1)} %pad_add_fusion.2), channel_id=1, source_target_pairs={{0,4},{2,6},{4,0},{6,2},{8,12},{10,14},{12,8},{14,10},{16,20},{18,... | collective-permute-start | bytes 4616 | tf_op jit(solution)/shard_map/ppermute | solution.py:33
  20.9 3.6 %collective-permute-start.3 = (s32[192,4]{0,1:T(4,128)S(1)}, s32[192,4]{0,1:T(4,128)S(1)}, u32[]{:S(2)}, u32[]{:S(2)}) collective-permute-start(s32[192,4]{0,1:T(4,128)S(1)} %pad_add_fusion.1), channel_id=1, source_target_pairs={{0,8},{2,10},{4,12},{6,14},{8,0},{10,2},{12,4},{14,6},{16,24},{18,... | collective-permute-start | bytes 9224 | tf_op jit(solution)/shard_map/ppermute | solution.py:33
  24.7 5.3 %collective-permute-start.4 = (s32[384,4]{0,1:T(4,128)S(1)}, s32[384,4]{0,1:T(4,128)S(1)}, u32[]{:S(2)}, u32[]{:S(2)}) collective-permute-start(s32[384,4]{0,1:T(4,128)S(1)} %pad_add_fusion), channel_id=1, source_target_pairs={{0,16},{2,18},{4,20},{6,22},{8,24},{10,26},{12,28},{14,30},{16,0},... | collective-permute-start | bytes 18440 | tf_op jit(solution)/shard_map/ppermute | solution.py:33
  103.1 7.0 %copy-start = (bf16[2048,2000]{0,1:T(8,128)(2,1)S(1)}, bf16[2048,2000]{0,1:T(8,128)(2,1)}, u32[]{:S(2)}) copy-start(bf16[2048,2000]{0,1:T(8,128)(2,1)} %pad_maximum_fusion) | copy-start | bytes 24576004
  141.1 20.9 %copy-start.2 = (s32[16]{0:T(128)S(1)}, s32[16]{0:T(128)}, u32[]{:S(2)}) copy-start(s32[16]{0:T(128)} %param.10) | copy-start | bytes 196
  141.1 34.9 %copy-start.1 = (s32[16]{0:T(128)S(1)}, s32[16]{0:T(128)}, u32[]{:S(2)}) copy-start(s32[16]{0:T(128)} %param.11) | copy-start | bytes 196
  145.6 4.2 %collective-permute-start.5 = (f32[4,4,768]{2,1,0:T(4,128)S(1)}, f32[4,4,768]{2,1,0:T(4,128)S(1)}, u32[]{:S(2)}, u32[]{:S(2)}) collective-permute-start(f32[4,4,768]{2,1,0:T(4,128)S(1)} %reshape.101), channel_id=1, source_target_pairs={{0,2},{2,0},{4,6},{6,4},{8,10},{10,8},{12,14},{14,12},{16,18},{18,... | collective-permute-start | bytes 147464 | tf_op jit(solution)/shard_map/ppermute | solution.py:43
  149.8 5.7 %collective-permute-start.6 = (f32[4,4,768]{2,1,0:T(4,128)S(1)}, f32[4,4,768]{2,1,0:T(4,128)S(1)}, u32[]{:S(2)}, u32[]{:S(2)}) collective-permute-start(f32[4,4,768]{2,1,0:T(4,128)S(1)} %pad_maximum_fusion.1), channel_id=1, source_target_pairs={{0,4},{2,6},{4,0},{6,2},{8,12},{10,14},{12,8},{14,10},{16,20},{18,... | collective-permute-start | bytes 147464 | tf_op jit(solution)/shard_map/ppermute | solution.py:43
  155.6 4.5 %collective-permute-start.7 = (f32[4,4,768]{2,1,0:T(4,128)S(1)}, f32[4,4,768]{2,1,0:T(4,128)S(1)}, u32[]{:S(2)}, u32[]{:S(2)}) collective-permute-start(f32[4,4,768]{2,1,0:T(4,128)S(1)} %pad_maximum_fusion.2), channel_id=1, source_target_pairs={{0,8},{2,10},{4,12},{6,14},{8,0},{10,2},{12,4},{14,6},{16,24},{18,... | collective-permute-start | bytes 147464 | tf_op jit(solution)/shard_map/ppermute | solution.py:43
  160.1 5.7 %collective-permute-start.8 = (f32[4,4,768]{2,1,0:T(4,128)S(1)}, f32[4,4,768]{2,1,0:T(4,128)S(1)}, u32[]{:S(2)}, u32[]{:S(2)}) collective-permute-start(f32[4,4,768]{2,1,0:T(4,128)S(1)} %pad_maximum_fusion.3), channel_id=1, source_target_pairs={{0,16},{2,18},{4,20},{6,22},{8,24},{10,26},{12,28},{14,30},{16,0},... | collective-permute-start | bytes 147464 | tf_op jit(solution)/shard_map/ppermute | solution.py:43
  166.0 1.2 collective-permute-start.9
  167.3 3.6 %collective-permute-start.10 = (f32[16]{0:T(128)S(1)}, f32[16]{0:T(128)S(1)}, u32[]{:S(2)}, u32[]{:S(2)}) collective-permute-start(f32[16]{0:T(128)S(1)} %select_reduce_fusion.2), channel_id=1, source_target_pairs={{0,32},{32,0},{64,96},{96,64},{1,33},{33,1},{65,97},{97,65},{2,34}... | collective-permute-start | bytes 200 | tf_op jit(solution)/shard_map/ppermute | solution.py:43
  170.9 5.1 %collective-permute-start.11 = (f32[16]{0:T(128)S(1)}, f32[16]{0:T(128)S(1)}, u32[]{:S(2)}, u32[]{:S(2)}) collective-permute-start(f32[16]{0:T(128)S(1)} %add.177), channel_id=1, source_target_pairs={{0,64},{32,96},{64,0},{96,32},{1,65},{33,97},{65,1},{97,33},{2,66}... | collective-permute-start | bytes 200 | tf_op jit(solution)/shard_map/ppermute | solution.py:43
Sparse Core Ops, SparseCore 0:
  11.0 92.0 all-gather.1

commit v4 on v3

--- a/solution.py
+++ b/solution.py
@@ -57,22 +57,22 @@
     values = hidden.astype(jnp.float32)
     squares = jnp.mean(values * values, axis=-1, keepdims=True)
     normed = (values * lax.rsqrt(squares + norm_eps) * norm_gain).astype(jnp.bfloat16)
-    rows = lax.all_gather(normed, "chip", axis=1, tiled=True)
+    own_rows = req_dev * pos_dev
+    flat_rows = lax.all_gather(normed.reshape(own_rows, model_width), "chip", axis=0, tiled=True)
     other = lax.ppermute(head_weight, "core", [(0, 1), (1, 0)])
     first = core == 0
     weight = jnp.concatenate([jnp.where(first, head_weight, other), jnp.where(first, other, head_weight)], axis=1)
     weight = lax.optimization_barrier(weight)
     offset = chip * (n_core * vocab_dev)
-    half_len = rows.shape[1]
-    tokens = xor_gather(token_ids.T, "chip", n_chip, chip)
+    half_len = n_chip * pos_dev
+    flat_tokens = xor_gather(token_ids, "chip", n_chip, chip).reshape(n_chip * own_rows)
     own_lengths = lax.dynamic_slice_in_dim(lengths, req_index * req_dev, req_dev)
-    flat_rows = rows.reshape(req_dev * half_len, model_width)
-    flat_tokens = tokens.T.reshape(req_dev * half_len)
     blocks = []
     for start in range(0, req_dev * half_len, BLOCK):
         size = min(BLOCK, req_dev * half_len - start)
         blocks.append(block_stats(flat_rows[start : start + size], flat_tokens[start : start + size], weight, offset))
-    stats = jnp.concatenate(blocks, axis=1).reshape(4, req_dev, half_len)
+    stats = jnp.concatenate(blocks, axis=1).reshape(4, n_chip, req_dev, pos_dev)
+    stats = stats.transpose(0, 2, 1, 3).reshape(4, req_dev, half_len)
     stats = xor_reduce(stats, "chip", n_chip, merge)
     row_top, exp_total, moment, token_logit = stats[0], stats[1], stats[2], stats[3]
     log_total = row_top + jnp.log(exp_total)

time: 184 us -> 183 us (level)
  matrix products: 26.6 us -> 33.1 us
  local copies, waits for them, and re-layouts: 7.41 us -> 1.31 us
    dot_general x2, matrix products: 26.6 us -> 33.1 us  [block_stats(): logits = jnp.dot(rows, weight, preferred_element_type=jnp.float32)]
    slice x1 -> x4, local copies, waits for them, and re-layouts: 5.65 us -> 0.02 us  [the longest x2 0.01 us: merge(): a[1] * ea + b[1] * eb]
where the time goes in v4:
time: 183 us
  waiting for transfers between devices  88.1 us (48%)
  matrix products  33.1 us (18%)
  other arithmetic  28.8 us (16%)
  starting transfers between devices  17.6 us (10%)
  between operations  14.3 us (8%)
    all_gather x1, waiting for transfers between devices, body(): lax.all_gather(normed.reshape(own_rows, model_width), 'chip', axis=0, til...  58.7 us
    dot_general x2, matrix products, block_stats(): logits = jnp.dot(rows, weight, preferred_element_type=jnp.float32)  33.1 us
    ppermute x6, waiting for transfers between devices, xor_reduce(): x = combine(x, lax.ppermute(x, axis, [(i, i ^ bit) for i in range(size)]))  17.5 us
    ppermute x4, waiting for transfers between devices, xor_gather(): other = lax.ppermute(x, axis, [(i, i ^ bit) for i in range(size)])  10.8 us
    ppermute x6, starting transfers between devices, xor_reduce(): x = combine(x, lax.ppermute(x, axis, [(i, i ^ bit) for i in range(size)]))  9.72 us
    concatenate x1, other arithmetic, body(): jnp.concatenate([jnp.where(first, head_weight, other), jnp.where(first, o...  8.23 us
    reduce_sum x2, other arithmetic, block_stats(): exp_total = jnp.sum(exps, axis=1)  8.09 us
    ppermute x4, starting transfers between devices, xor_gather(): other = lax.ppermute(x, axis, [(i, i ^ bit) for i in range(size)])  7.63 us
  transfers between devices with their start and end apart: 13, of which 12 were waited for; matrix products, arithmetic and copies ran while one was open for 9% of the time, Pallas kernels for 0%

profile of v4, /device:TPU:2, one launch (start us, length us, event | category | flops | bytes accessed | tf_op | source)
XLA Modules:
  0.0 183.2 jit_solution(359651505106999283)
XLA Ops:
  7.2 0.0 all-gather.2.cloned.1.call-start
  7.2 1.4 fusion.6
  8.6 2.3 %fusion.8 = bf16[4,48,2048]{2,1,0:T(8,128)(2,1)} fusion(bf16[4,48,2048]{2,1,0:T(8,128)(2,1)} %param.6, f32[2048]{0:T(1024)} %param.7, f32[4,48]{1,0:T(4,128)S(1)} %add_rsqrt_fusion), kind=kLoop, calls=%fused_computation.21 | loop fusion | flops 1572864 | bytes 1581824 | tf_op jit(solution)/shard_map/convert_element_type | solution.py:59
  10.9 0.0 all-gather.2.cloned.1.call-update
  10.9 0.1 collective-permute-start
  11.0 0.5 collective-permute-start.1
  11.5 3.4 %collective-permute-done.1 = s32[4,48]{1,0:T(4,128)S(1)} collective-permute-done((s32[4,48]{1,0:T(4,128)}, s32[4,48]{1,0:T(4,128)S(1)}, u32[]{:S(2)}, u32[]{:S(2)}) %collective-permute-start.1) | collective-permute-done | bytes 800 | tf_op jit(solution)/shard_map/ppermute | solution.py:33
  14.9 0.7 broadcast_select_fusion.7
  15.6 2.2 %collective-permute-start.2 = (s32[8,48]{1,0:T(8,128)S(1)}, s32[8,48]{1,0:T(8,128)S(1)}, u32[]{:S(2)}, u32[]{:S(2)}) collective-permute-start(s32[8,48]{1,0:T(8,128)S(1)} %pad_add_fusion.2), channel_id=1, source_target_pairs={{0,4},{2,6},{4,0},{6,2},{8,12},{10,14},{12,8},{14,10},{16,20},{18,... | collective-permute-start | bytes 4616 | tf_op jit(solution)/shard_map/ppermute | solution.py:33
  17.8 3.0 %collective-permute-done.2 = s32[8,48]{1,0:T(8,128)S(1)} collective-permute-done((s32[8,48]{1,0:T(8,128)S(1)}, s32[8,48]{1,0:T(8,128)S(1)}, u32[]{:S(2)}, u32[]{:S(2)}) %collective-permute-start.2) | collective-permute-done | bytes 1568 | tf_op jit(solution)/shard_map/ppermute | solution.py:33
  20.8 1.7 collective-permute-start.3
  22.4 2.1 %collective-permute-done.3 = s32[16,48]{1,0:T(8,128)S(1)} collective-permute-done((s32[16,48]{1,0:T(8,128)S(1)}, s32[16,48]{1,0:T(8,128)S(1)}, u32[]{:S(2)}, u32[]{:S(2)}) %collective-permute-start.3) | collective-permute-done | bytes 3104 | tf_op jit(solution)/shard_map/ppermute | solution.py:33
  24.5 3.3 %collective-permute-start.4 = (s32[32,48]{1,0:T(8,128)S(1)}, s32[32,48]{1,0:T(8,128)S(1)}, u32[]{:S(2)}, u32[]{:S(2)}) collective-permute-start(s32[32,48]{1,0:T(8,128)S(1)} %pad_add_fusion), channel_id=1, source_target_pairs={{0,16},{2,18},{4,20},{6,22},{8,24},{10,26},{12,28},{14,30},{16,0},... | collective-permute-start | bytes 18440 | tf_op jit(solution)/shard_map/ppermute | solution.py:33
  27.8 2.4 %collective-permute-done.4 = s32[32,48]{1,0:T(8,128)S(1)} collective-permute-done((s32[32,48]{1,0:T(8,128)S(1)}, s32[32,48]{1,0:T(8,128)S(1)}, u32[]{:S(2)}, u32[]{:S(2)}) %collective-permute-start.4) | collective-permute-done | bytes 6176 | tf_op jit(solution)/shard_map/ppermute | solution.py:33
  30.2 0.1 sub.131
  30.3 0.1 sub.135
  30.4 0.0 collective-permute-done
  30.4 5.9 %broadcast_select_fusion.1 = (bf16[2048,1000]{0,1:T(8,128)(2,1)}, bf16[2048,1000]{0,1:T(8,128)(2,1)}) fusion(bf16[2048,1000]{0,1:T(8,128)(2,1)} %param.8, bf16[2048,1000]{0,1:T(8,128)(2,1)} %collective-permute-done, pred[]{:T(512)S(6)} %eq.28), kind=kLoop, calls=%fused_computation.16 | loop fusion | flops 4096000 | bytes 16384001 | tf_op jit(solution)/shard_map/jit(_where)/select_n | solution.py:64
  36.3 8.2 %pad_maximum_fusion = bf16[2048,2000]{0,1:T(8,128)(2,1)} fusion(bf16[2048,1000]{0,1:T(8,128)(2,1)} %get-tuple-element.22, bf16[2048,1000]{0,1:T(8,128)(2,1)} %get-tuple-element.21), kind=kLoop, calls=%fused_computation.10 | loop fusion | flops 16384000 | bytes 16384000 | tf_op jit(solution)/shard_map/concatenate | solution.py:64
  44.5 58.7 %all-gather.2.cloned.1.call-done = bf16[3072,2048]{1,0:T(8,128)(2,1)} async-done(((bf16[192,2048]{1,0:T(8,128)(2,1)}), bf16[3072,2048]{1,0:T(8,128)(2,1)}) %all-gather.2.cloned.1.call-update) | async-done | bytes 12582928 | tf_op jit(solution)/shard_map/all_gather | solution.py:61
  103.2 17.2 %fusion.54 = (f32[1536]{0:T(1024)S(1)}, f32[1536,2000]{0,1:T(8,128)S(1)}) fusion(bf16[2048,2000]{0,1:T(8,128)(2,1)} %pad_maximum_fusion, bf16[3072,2048]{1,0:T(8,128)(2,1)} %all-gather.2.cloned.1.call-done), kind=kOutput, calls=%fused_computation.145 | convolution fusion | flops 12585981952 | bytes 26777600 | tf_op jit(solution)/shard_map/dot_general | solution.py:13
  120.4 0.0 copy-start
  120.4 4.0 %fusion.1 = (f32[1536]{0:T(1024)S(1)}, f32[1536]{0:T(1024)S(1)}, f32[1536]{0:T(1024)S(1)}) fusion(f32[1536,2000]{0,1:T(8,128)S(1)} %get-tuple-element.50, f32[1536]{0:T(1024)S(1)} %get-tuple-element.49, s32[1536]{0:T(1024)S(1)} %sub.131), kind=kLoop, calls=%fused_computation.9 | loop fusion | flops 21499392 | bytes 12318720 | tf_op jit(solution)/shard_map/reduce_sum | solution.py:16
  124.5 0.0 copy-done
  124.5 15.9 %fusion.53 = (f32[1536]{0:T(1024)S(1)}, f32[1536,2000]{0,1:T(8,128)S(1)}) fusion(bf16[2048,2000]{0,1:T(8,128)(2,1)S(1)} %copy-done, bf16[3072,2048]{1,0:T(8,128)(2,1)} %all-gather.2.cloned.1.call-done), kind=kOutput, calls=%fused_computation.144 | convolution fusion | flops 12585981952 | bytes 26777600 | tf_op jit(solution)/shard_map/dot_general | solution.py:13
  140.5 0.0 copy-start.2
  140.5 0.0 copy-start.1
  140.5 4.0 %fusion = (f32[1536]{0:T(1024)S(1)}, f32[1536]{0:T(1024)S(1)}, f32[1536]{0:T(1024)S(1)}) fusion(f32[1536,2000]{0,1:T(8,128)S(1)} %get-tuple-element.48, f32[1536]{0:T(1024)S(1)} %get-tuple-element.47, s32[1536]{0:T(1024)S(1)} %sub.135), kind=kLoop, calls=%fused_computation.4 | loop fusion | flops 21499392 | bytes 12318720 | tf_op jit(solution)/shard_map/reduce_sum | solution.py:16
  144.6 0.1 maximum_maximum_fusion
  144.7 0.2 reshape.105
  144.9 0.1 reshape.106
  145.0 0.6 collective-permute-start.5
  145.6 0.1 squeeze.75
  145.7 0.1 squeeze.76
  145.8 0.1 squeeze.77
  145.9 0.1 squeeze.78
  146.0 3.1 %collective-permute-done.5 = f32[4,4,768]{2,1,0:T(4,128)S(1)} collective-permute-done((f32[4,4,768]{2,1,0:T(4,128)S(1)}, f32[4,4,768]{2,1,0:T(4,128)S(1)}, u32[]{:S(2)}, u32[]{:S(2)}) %collective-permute-start.5) | collective-permute-done | bytes 49184 | tf_op jit(solution)/shard_map/ppermute | solution.py:43
  149.2 2.2 %collective-permute-start.6 = (f32[4,4,768]{2,1,0:T(4,128)S(1)}, f32[4,4,768]{2,1,0:T(4,128)S(1)}, u32[]{:S(2)}, u32[]{:S(2)}) collective-permute-start(f32[4,4,768]{2,1,0:T(4,128)S(1)} %pad_maximum_fusion.1), channel_id=1, source_target_pairs={{0,4},{2,6},{4,0},{6,2},{8,12},{10,14},{12,8},{14,10},{16,20},{18,... | collective-permute-start | bytes 147464 | tf_op jit(solution)/shard_map/ppermute | solution.py:43
  151.4 3.5 %collective-permute-done.6 = f32[4,4,768]{2,1,0:T(4,128)S(1)} collective-permute-done((f32[4,4,768]{2,1,0:T(4,128)S(1)}, f32[4,4,768]{2,1,0:T(4,128)S(1)}, u32[]{:S(2)}, u32[]{:S(2)}) %collective-permute-start.6) | collective-permute-done | bytes 49184 | tf_op jit(solution)/shard_map/ppermute | solution.py:43
  155.0 0.3 collective-permute-start.7
  155.3 4.2 %collective-permute-done.7 = f32[4,4,768]{2,1,0:T(4,128)S(1)} collective-permute-done((f32[4,4,768]{2,1,0:T(4,128)S(1)}, f32[4,4,768]{2,1,0:T(4,128)S(1)}, u32[]{:S(2)}, u32[]{:S(2)}) %collective-permute-start.7) | collective-permute-done | bytes 49184 | tf_op jit(solution)/shard_map/ppermute | solution.py:43
  159.5 1.9 %collective-permute-start.8 = (f32[4,4,768]{2,1,0:T(4,128)S(1)}, f32[4,4,768]{2,1,0:T(4,128)S(1)}, u32[]{:S(2)}, u32[]{:S(2)}) collective-permute-start(f32[4,4,768]{2,1,0:T(4,128)S(1)} %pad_maximum_fusion.3), channel_id=1, source_target_pairs={{0,16},{2,18},{4,20},{6,22},{8,24},{10,26},{12,28},{14,30},{16,0},... | collective-permute-start | bytes 147464 | tf_op jit(solution)/shard_map/ppermute | solution.py:43
  161.4 0.0 copy-done.2
  161.4 0.1 dynamic_slice.9
  161.5 0.1 squeeze.73
  161.6 0.1 squeeze.82
  161.7 0.1 squeeze.87
  161.7 0.1 squeeze.92
  161.8 3.4 %collective-permute-done.8 = f32[4,4,768]{2,1,0:T(4,128)S(1)} collective-permute-done((f32[4,4,768]{2,1,0:T(4,128)S(1)}, f32[4,4,768]{2,1,0:T(4,128)S(1)}, u32[]{:S(2)}, u32[]{:S(2)}) %collective-permute-start.8) | collective-permute-done | bytes 49184 | tf_op jit(solution)/shard_map/ppermute | solution.py:43
  165.2 0.2 fusion.49
  165.4 0.1 collective-permute-start.9
  165.5 1.1 collective-permute-done.9
  166.6 0.1 select_reduce_fusion.2
  166.7 1.6 collective-permute-start.10
  168.3 2.0 %collective-permute-done.10 = f32[16]{0:T(128)S(1)} collective-permute-done((f32[16]{0:T(128)S(1)}, f32[16]{0:T(128)S(1)}, u32[]{:S(2)}, u32[]{:S(2)}) %collective-permute-start.10) | collective-permute-done | bytes 96 | tf_op jit(solution)/shard_map/ppermute | solution.py:43
  170.3 3.2 %collective-permute-start.11 = (f32[16]{0:T(128)S(1)}, f32[16]{0:T(128)S(1)}, u32[]{:S(2)}, u32[]{:S(2)}) collective-permute-start(f32[16]{0:T(128)S(1)} %add.177), channel_id=1, source_target_pairs={{0,64},{32,96},{64,0},{96,32},{1,65},{33,97},{65,1},{97,33},{2,66}... | collective-permute-start | bytes 200 | tf_op jit(solution)/shard_map/ppermute | solution.py:43
  173.5 0.7 constant_dynamic-slice_fusion.8
  174.1 1.3 collective-permute-done.11
  175.4 0.0 copy-done.1
  175.4 0.2 fusion.29
  175.6 0.2 fusion.30
  175.8 0.5 maximum_divide_fusion
  (37 shorter events, 0.4 us)
Async XLA Ops:
  7.2 96.1 %all-gather.2.cloned.1.call-start = ((), (), s32[]{:S(2)}) async-start(), calls=%async_computation | async-start | bytes 13369344 | tf_op jit(solution)/shard_map/all_gather | solution.py:61
  10.9 19.5 %collective-permute-start = (bf16[2048,1000]{0,1:T(8,128)(2,1)}, bf16[2048,1000]{0,1:T(8,128)(2,1)}, u32[]{:S(2)}, u32[]{:S(2)}) collective-permute-start(bf16[2048,1000]{0,1:T(8,128)(2,1)} %param.8), channel_id=1, source_target_pairs={{0,1},{1,0},{2,3},{3,2},{4,5},{5,4},{6,7},{7,6},{8,9},{9,8},{10,11... | collective-permute-start | bytes 12288008 | tf_op jit(solution)/shard_map/ppermute | solution.py:62
  11.0 3.9 %collective-permute-start.1 = (s32[4,48]{1,0:T(4,128)}, s32[4,48]{1,0:T(4,128)S(1)}, u32[]{:S(2)}, u32[]{:S(2)}) collective-permute-start(s32[4,48]{1,0:T(4,128)} %param.9), channel_id=1, source_target_pairs={{0,2},{2,0},{4,6},{6,4},{8,10},{10,8},{12,14},{14,12},{16,18},{18,... | collective-permute-start | bytes 2312 | tf_op jit(solution)/shard_map/ppermute | solution.py:33
  15.6 5.2 %collective-permute-start.2 = (s32[8,48]{1,0:T(8,128)S(1)}, s32[8,48]{1,0:T(8,128)S(1)}, u32[]{:S(2)}, u32[]{:S(2)}) collective-permute-start(s32[8,48]{1,0:T(8,128)S(1)} %pad_add_fusion.2), channel_id=1, source_target_pairs={{0,4},{2,6},{4,0},{6,2},{8,12},{10,14},{12,8},{14,10},{16,20},{18,... | collective-permute-start | bytes 4616 | tf_op jit(solution)/shard_map/ppermute | solution.py:33
  20.8 3.7 %collective-permute-start.3 = (s32[16,48]{1,0:T(8,128)S(1)}, s32[16,48]{1,0:T(8,128)S(1)}, u32[]{:S(2)}, u32[]{:S(2)}) collective-permute-start(s32[16,48]{1,0:T(8,128)S(1)} %pad_add_fusion.1), channel_id=1, source_target_pairs={{0,8},{2,10},{4,12},{6,14},{8,0},{10,2},{12,4},{14,6},{16,24},{18,... | collective-permute-start | bytes 9224 | tf_op jit(solution)/shard_map/ppermute | solution.py:33
  24.5 5.7 %collective-permute-start.4 = (s32[32,48]{1,0:T(8,128)S(1)}, s32[32,48]{1,0:T(8,128)S(1)}, u32[]{:S(2)}, u32[]{:S(2)}) collective-permute-start(s32[32,48]{1,0:T(8,128)S(1)} %pad_add_fusion), channel_id=1, source_target_pairs={{0,16},{2,18},{4,20},{6,22},{8,24},{10,26},{12,28},{14,30},{16,0},... | collective-permute-start | bytes 18440 | tf_op jit(solution)/shard_map/ppermute | solution.py:33
  120.4 4.1 %copy-start = (bf16[2048,2000]{0,1:T(8,128)(2,1)S(1)}, bf16[2048,2000]{0,1:T(8,128)(2,1)}, u32[]{:S(2)}) copy-start(bf16[2048,2000]{0,1:T(8,128)(2,1)} %pad_maximum_fusion) | copy-start | bytes 24576004
  140.5 20.9 %copy-start.2 = (s32[16]{0:T(128)S(1)}, s32[16]{0:T(128)}, u32[]{:S(2)}) copy-start(s32[16]{0:T(128)} %param.10) | copy-start | bytes 196
  140.5 34.9 %copy-start.1 = (s32[16]{0:T(128)S(1)}, s32[16]{0:T(128)}, u32[]{:S(2)}) copy-start(s32[16]{0:T(128)} %param.11) | copy-start | bytes 196
  145.0 4.2 %collective-permute-start.5 = (f32[4,4,768]{2,1,0:T(4,128)S(1)}, f32[4,4,768]{2,1,0:T(4,128)S(1)}, u32[]{:S(2)}, u32[]{:S(2)}) collective-permute-start(f32[4,4,768]{2,1,0:T(4,128)S(1)} %reshape.106), channel_id=1, source_target_pairs={{0,2},{2,0},{4,6},{6,4},{8,10},{10,8},{12,14},{14,12},{16,18},{18,... | collective-permute-start | bytes 147464 | tf_op jit(solution)/shard_map/ppermute | solution.py:43
  149.2 5.7 %collective-permute-start.6 = (f32[4,4,768]{2,1,0:T(4,128)S(1)}, f32[4,4,768]{2,1,0:T(4,128)S(1)}, u32[]{:S(2)}, u32[]{:S(2)}) collective-permute-start(f32[4,4,768]{2,1,0:T(4,128)S(1)} %pad_maximum_fusion.1), channel_id=1, source_target_pairs={{0,4},{2,6},{4,0},{6,2},{8,12},{10,14},{12,8},{14,10},{16,20},{18,... | collective-permute-start | bytes 147464 | tf_op jit(solution)/shard_map/ppermute | solution.py:43
  155.0 4.5 %collective-permute-start.7 = (f32[4,4,768]{2,1,0:T(4,128)S(1)}, f32[4,4,768]{2,1,0:T(4,128)S(1)}, u32[]{:S(2)}, u32[]{:S(2)}) collective-permute-start(f32[4,4,768]{2,1,0:T(4,128)S(1)} %pad_maximum_fusion.2), channel_id=1, source_target_pairs={{0,8},{2,10},{4,12},{6,14},{8,0},{10,2},{12,4},{14,6},{16,24},{18,... | collective-permute-start | bytes 147464 | tf_op jit(solution)/shard_map/ppermute | solution.py:43
  159.5 5.7 %collective-permute-start.8 = (f32[4,4,768]{2,1,0:T(4,128)S(1)}, f32[4,4,768]{2,1,0:T(4,128)S(1)}, u32[]{:S(2)}, u32[]{:S(2)}) collective-permute-start(f32[4,4,768]{2,1,0:T(4,128)S(1)} %pad_maximum_fusion.3), channel_id=1, source_target_pairs={{0,16},{2,18},{4,20},{6,22},{8,24},{10,26},{12,28},{14,30},{16,0},... | collective-permute-start | bytes 147464 | tf_op jit(solution)/shard_map/ppermute | solution.py:43
  165.4 1.2 collective-permute-start.9
  166.7 3.6 %collective-permute-start.10 = (f32[16]{0:T(128)S(1)}, f32[16]{0:T(128)S(1)}, u32[]{:S(2)}, u32[]{:S(2)}) collective-permute-start(f32[16]{0:T(128)S(1)} %select_reduce_fusion.2), channel_id=1, source_target_pairs={{0,32},{32,0},{64,96},{96,64},{1,33},{33,1},{65,97},{97,65},{2,34}... | collective-permute-start | bytes 200 | tf_op jit(solution)/shard_map/ppermute | solution.py:43
  170.3 5.1 %collective-permute-start.11 = (f32[16]{0:T(128)S(1)}, f32[16]{0:T(128)S(1)}, u32[]{:S(2)}, u32[]{:S(2)}) collective-permute-start(f32[16]{0:T(128)S(1)} %add.177), channel_id=1, source_target_pairs={{0,64},{32,96},{64,0},{96,32},{1,65},{33,97},{65,1},{97,33},{2,66}... | collective-permute-start | bytes 200 | tf_op jit(solution)/shard_map/ppermute | solution.py:43
Sparse Core Ops, SparseCore 0:
  11.0 92.1 all-gather.1

commit v5 on v4

--- a/solution.py
+++ b/solution.py
@@ -45,35 +45,48 @@
     return x
 
 
+def shift_gather(v, axis, n, index):
+    got = [v] + [lax.ppermute(v, axis, [(i, (i + d) % n) for i in range(n)]) for d in range(1, n)]
+    order = (index - jnp.arange(n, dtype=jnp.int32)) % n
+    return jnp.take(jnp.stack(got), order, axis=0)
+
+
 def body(hidden, norm_gain, head_weight, token_ids, lengths, group_ids):
     req_dev, pos_dev, model_width = hidden.shape
     vocab_dev = head_weight.shape[1]
-    n_chip = lax.axis_size("chip")
+    chips = ("y", "x")
+    n_chip = lax.axis_size(chips)
     n_core = lax.axis_size("core")
     n_req = lax.axis_size("req")
-    chip = lax.axis_index("chip")
+    chip = lax.axis_index(chips)
     core = lax.axis_index("core")
     req_index = lax.axis_index("req")
     values = hidden.astype(jnp.float32)
     squares = jnp.mean(values * values, axis=-1, keepdims=True)
     normed = (values * lax.rsqrt(squares + norm_eps) * norm_gain).astype(jnp.bfloat16)
-    own_rows = req_dev * pos_dev
-    flat_rows = lax.all_gather(normed.reshape(own_rows, model_width), "chip", axis=0, tiled=True)
+    n_y, n_x = lax.axis_size("y"), lax.axis_size("x")
+    y_index, x_index = lax.axis_index("y"), lax.axis_index("x")
+    half_req = req_dev // 2
+    half_rows = half_req * pos_dev
+    rows_a = lax.all_gather(normed[:half_req].reshape(half_rows, model_width), chips, axis=0, tiled=True)
+    part_b = shift_gather(normed[half_req:].reshape(half_rows, model_width), "y", n_y, y_index)
+    rows_b = shift_gather(part_b, "x", n_x, x_index).reshape(n_chip * half_rows, model_width)
     other = lax.ppermute(head_weight, "core", [(0, 1), (1, 0)])
     first = core == 0
     weight = jnp.concatenate([jnp.where(first, head_weight, other), jnp.where(first, other, head_weight)], axis=1)
     weight = lax.optimization_barrier(weight)
     offset = chip * (n_core * vocab_dev)
     half_len = n_chip * pos_dev
-    flat_tokens = xor_gather(token_ids, "chip", n_chip, chip).reshape(n_chip * own_rows)
+    tok = xor_gather(token_ids, chips, n_chip, chip).reshape(n_y, n_x, req_dev, pos_dev)
+    tok_a = tok[:, :, :half_req].reshape(-1)
+    tok_b = tok[:, :, half_req:].transpose(1, 0, 2, 3).reshape(-1)
     own_lengths = lax.dynamic_slice_in_dim(lengths, req_index * req_dev, req_dev)
-    blocks = []
-    for start in range(0, req_dev * half_len, BLOCK):
-        size = min(BLOCK, req_dev * half_len - start)
-        blocks.append(block_stats(flat_rows[start : start + size], flat_tokens[start : start + size], weight, offset))
-    stats = jnp.concatenate(blocks, axis=1).reshape(4, n_chip, req_dev, pos_dev)
+    stats_b = block_stats(rows_b, tok_b, weight, offset).reshape(4, n_x, n_y, half_req, pos_dev)
+    stats_b = stats_b.transpose(0, 2, 1, 3, 4).reshape(4, n_chip, half_req, pos_dev)
+    stats_a = block_stats(rows_a, tok_a, weight, offset).reshape(4, n_chip, half_req, pos_dev)
+    stats = jnp.concatenate([stats_a, stats_b], axis=2)
     stats = stats.transpose(0, 2, 1, 3).reshape(4, req_dev, half_len)
-    stats = xor_reduce(stats, "chip", n_chip, merge)
+    stats = xor_reduce(stats, chips, n_chip, merge)
     row_top, exp_total, moment, token_logit = stats[0], stats[1], stats[2], stats[3]
     log_total = row_top + jnp.log(exp_total)
     raw_logprob = token_logit - log_total
@@ -106,8 +119,9 @@
 
 def solution(mesh):
     n_req, n_vocab = mesh.devices.shape
-    split = Mesh(np.asarray(mesh.devices).reshape(n_req, n_vocab // 2, 2), ("req", "chip", "core"))
-    vocab = ("chip", "core")
+    side = int(round((n_vocab // 2) ** 0.5))
+    split = Mesh(np.asarray(mesh.devices).reshape(n_req, side, n_vocab // 2 // side, 2), ("req", "y", "x", "core"))
+    vocab = ("y", "x", "core")
     return jax.shard_map(
         body,
         mesh=split,

time: 183 us -> 265 us (1.45)
  waiting for transfers between devices: 88.1 us -> 126 us
  other arithmetic: 28.8 us -> 46.4 us
  starting transfers between devices: 17.6 us -> 28.3 us
  local copies, waits for them, and re-layouts: 1.31 us -> 10.5 us
  matrix products: 33.1 us -> 38 us
    ppermute x0 -> x6, waiting for transfers between devices: none -> 99.4 us  [shift_gather(): lax.ppermute(v, axis, [(i, (i + d) % n) for i in range(n)])]
    all_gather x1, waiting for transfers between devices: 58.7 us -> 0.02 us  [body(): lax.all_gather(normed[:half_req].reshape(half_rows, model_width), chips,...]
    ppermute x0 -> x6, starting transfers between devices: none -> 9.44 us  [shift_gather(): lax.ppermute(v, axis, [(i, (i + d) % n) for i in range(n)])]
    select_n x0 -> x6, other arithmetic: none -> 8.48 us  [the longest x5 7.82 us: shift_gather(): return jnp.take(jnp.stack(got), order, axis=0)]
    gather x0 -> x2, local copies, waits for them, and re-layouts: none -> 7.03 us  [shift_gather(): return jnp.take(jnp.stack(got), order, axis=0)]
    reduce_sum x2, other arithmetic: 8.09 us -> 14.3 us  [block_stats(): exp_total = jnp.sum(exps, axis=1)]
    another operation x0 -> x2, other arithmetic: none -> 5.28 us  [shift_gather(): return jnp.take(jnp.stack(got), order, axis=0)]
    dot_general x2, matrix products: 33.1 us -> 38 us  [block_stats(): logits = jnp.dot(rows, weight, preferred_element_type=jnp.float32)]
  transfers between devices with their start and end apart: 13 -> 19, of which waited for: 12 -> 15; matrix products, arithmetic and copies ran while one was open for 9% -> 24% of each run, Pallas kernels for 0% -> 0%
where the time goes in v5:
time: 265 us; the launch traced here: 263 us
  waiting for transfers between devices  126 us (48%)
  other arithmetic  46.4 us (18%)
  matrix products  38 us (14%)
  starting transfers between devices  28.3 us (11%)
  between operations  14.4 us (5%)
  local copies, waits for them, and re-layouts  10.5 us (4%)
    ppermute x6, waiting for transfers between devices, shift_gather(): lax.ppermute(v, axis, [(i, (i + d) % n) for i in range(n)])  99.4 us
    dot_general x2, matrix products, block_stats(): logits = jnp.dot(rows, weight, preferred_element_type=jnp.float32)  38 us
    ppermute x6, waiting for transfers between devices, xor_reduce(): x = combine(x, lax.ppermute(x, axis, [(i, i ^ bit) for i in range(size)]))  15.3 us
    reduce_sum x2, other arithmetic, block_stats(): exp_total = jnp.sum(exps, axis=1)  14.3 us
    ppermute x6, starting transfers between devices, xor_reduce(): x = combine(x, lax.ppermute(x, axis, [(i, i ^ bit) for i in range(size)]))  12.3 us
    ppermute x4, waiting for transfers between devices, xor_gather(): other = lax.ppermute(x, axis, [(i, i ^ bit) for i in range(size)])  9.83 us
    ppermute x6, starting transfers between devices, shift_gather(): lax.ppermute(v, axis, [(i, (i + d) % n) for i in range(n)])  9.44 us
    concatenate x1, other arithmetic, body(): jnp.concatenate([jnp.where(first, head_weight, other), jnp.where(first, o...  8.17 us
  transfers between devices with their start and end apart: 19, of which 15 were waited for; matrix products, arithmetic and copies ran while one was open for 24% of the time, Pallas kernels for 0%

profile of v5, /device:TPU:2, one launch (start us, length us, event | category | flops | bytes accessed | tf_op | source)
XLA Modules:
  0.0 263.2 jit_solution(2216589061402577775)
XLA Ops:
  7.2 1.4 fusion.2
  8.6 1.4 fusion.4
  10.0 0.8 fusion.55
  10.8 3.1 %collective-permute-start.7 = (bf16[96,2048]{1,0:T(8,128)(2,1)S(1)}, bf16[96,2048]{1,0:T(8,128)(2,1)S(1)}, u32[]{:S(2)}, u32[]{:S(2)}) collective-permute-start(bf16[96,2048]{1,0:T(8,128)(2,1)S(1)} %bitcast.193), channel_id=1, source_target_pairs={{0,24},{8,0},{16,8},{24,16},{1,25},{9,1},{17,9},{25,17},{2,26},{10... | collective-permute-start | bytes 1179656 | tf_op jit(solution)/shard_map/ppermute | solution.py:49
  13.9 0.6 collective-permute-start.6
  14.6 1.0 collective-permute-start.5
  15.5 0.5 collective-permute-start.1
  16.1 3.2 %collective-permute-done.1 = s32[4,48]{1,0:T(4,128)S(1)} collective-permute-done((s32[4,48]{1,0:T(4,128)}, s32[4,48]{1,0:T(4,128)S(1)}, u32[]{:S(2)}, u32[]{:S(2)}) %collective-permute-start.1) | collective-permute-done | bytes 800 | tf_op jit(solution)/shard_map/ppermute | solution.py:33
  19.3 0.7 broadcast_select_fusion.10
  20.0 2.2 collective-permute-start.2
  22.2 3.0 %collective-permute-done.2 = s32[8,48]{1,0:T(8,128)S(1)} collective-permute-done((s32[8,48]{1,0:T(8,128)S(1)}, s32[8,48]{1,0:T(8,128)S(1)}, u32[]{:S(2)}, u32[]{:S(2)}) %collective-permute-start.2) | collective-permute-done | bytes 1568 | tf_op jit(solution)/shard_map/ppermute | solution.py:33
  25.2 2.0 collective-permute-start.3
  27.2 5.5 %collective-permute-done.7 = bf16[96,2048]{1,0:T(8,128)(2,1)S(1)} collective-permute-done((bf16[96,2048]{1,0:T(8,128)(2,1)S(1)}, bf16[96,2048]{1,0:T(8,128)(2,1)S(1)}, u32[]{:S(2)}, u32[]{:S(2)}) %collective-permute-start.7) | collective-permute-done | bytes 393248 | tf_op jit(solution)/shard_map/ppermute | solution.py:49
  32.7 7.2 %collective-permute-done.5 = bf16[96,2048]{1,0:T(8,128)(2,1)S(1)} collective-permute-done((bf16[96,2048]{1,0:T(8,128)(2,1)S(1)}, bf16[96,2048]{1,0:T(8,128)(2,1)S(1)}, u32[]{:S(2)}, u32[]{:S(2)}) %collective-permute-start.5) | collective-permute-done | bytes 393248 | tf_op jit(solution)/shard_map/ppermute | solution.py:49
  40.0 0.2 pad_maximum_fusion.2
  40.2 0.6 gather_fusion
  40.8 1.4 broadcast_select_fusion.2
  42.2 0.7 collective-permute-start.10
  42.9 2.3 collective-permute-start.9
  45.2 1.8 collective-permute-start.8
  47.0 1.7 collective-permute-start.4
  48.7 0.1 broadcast_in_dim.70
  48.8 3.7 %collective-permute-done.4 = s32[32,48]{1,0:T(8,128)S(1)} collective-permute-done((s32[32,48]{1,0:T(8,128)S(1)}, s32[32,48]{1,0:T(8,128)S(1)}, u32[]{:S(2)}, u32[]{:S(2)}) %collective-permute-start.4) | collective-permute-done | bytes 6176 | tf_op jit(solution)/shard_map/ppermute | solution.py:33
  52.7 0.2 bitcast_select_fusion.1
  53.0 46.1 %collective-permute-done.10 = bf16[4,96,2048]{2,1,0:T(8,128)(2,1)S(1)} collective-permute-done((bf16[4,96,2048]{2,1,0:T(8,128)(2,1)}, bf16[4,96,2048]{2,1,0:T(8,128)(2,1)S(1)}, u32[]{:S(2)}, u32[]{:S(2)}) %collective-permute-start.10) | collective-permute-done | bytes 1572896 | tf_op jit(solution)/shard_map/ppermute | solution.py:49
  99.0 39.6 %collective-permute-done.9 = bf16[4,96,2048]{2,1,0:T(8,128)(2,1)} collective-permute-done((bf16[4,96,2048]{2,1,0:T(8,128)(2,1)}, bf16[4,96,2048]{2,1,0:T(8,128)(2,1)}, u32[]{:S(2)}, u32[]{:S(2)}) %collective-permute-start.9) | collective-permute-done | bytes 1572896 | tf_op jit(solution)/shard_map/ppermute | solution.py:49
  138.7 0.9 collective-permute-done.8
  139.6 5.1 %pad_maximum_fusion.1 = bf16[4,4,96,2048]{3,2,1,0:T(8,128)(2,1)} fusion(bf16[1,4,96,2048]{3,2,1,0:T(8,128)(2,1)S(1)} %bitcast.192, bf16[1,4,96,2048]{3,2,1,0:T(8,128)(2,1)} %bitcast.10, bf16[1,4,96,2048]{3,2,1,0:T(8,128)(2,1)} %bitcast.9, bf16[1,4,96,2048]{3,2,1,0:T(8,128)(2,1)S(1)} %bitcast_select_fusion.1), kind=kLoop, calls=%fused_computation.13 | loop fusion | flops 9437184 | bytes 12582912 | tf_op jit(solution)/shard_map/stack | solution.py:51
  144.6 6.4 %gather_fusion.1 = bf16[4,4,96,2048]{3,2,1,0:T(8,128)(2,1)} fusion(bf16[4,4,96,2048]{3,2,1,0:T(8,128)(2,1)} %pad_maximum_fusion.1, s32[1024]{0:T(1024)S(1)} %pad_clamp_fusion), kind=kCustom, calls=%fused_computation.1 | custom fusion | bytes 12582928 | tf_op jit(solution)/shard_map/jit(_take)/gather | solution.py:51
  151.0 6.2 %bitcast_select_fusion = bf16[1536,2048]{1,0:T(8,128)(2,1)} fusion(bf16[4,4,96,2048]{3,2,1,0:T(8,128)(2,1)} %gather_fusion.1, pred[1536]{0:T(1024)(128)(4,1)S(1)} %broadcast_in_dim.70), kind=kLoop, calls=%fused_computation.14 | loop fusion | flops 3145728 | bytes 12584448 | tf_op jit(solution)/shard_map/jit(_take)/select_n | solution.py:51
  157.2 5.1 %broadcast_select_fusion.1 = (bf16[2048,1000]{0,1:T(8,128)(2,1)}, bf16[2048,1000]{0,1:T(8,128)(2,1)}) fusion(bf16[2048,1000]{0,1:T(8,128)(2,1)S(1)} %copy-done, bf16[2048,1000]{0,1:T(8,128)(2,1)} %collective-permute-done, pred[]{:T(512)S(6)} %eq.31), kind=kLoop, calls=%fused_computation.16 | loop fusion | flops 4096000 | bytes 16384001 | tf_op jit(solution)/shard_map/jit(_where)/select_n | solution.py:76
  162.3 8.2 %pad_maximum_fusion = bf16[2048,2000]{0,1:T(8,128)(2,1)} fusion(bf16[2048,1000]{0,1:T(8,128)(2,1)} %get-tuple-element.22, bf16[2048,1000]{0,1:T(8,128)(2,1)} %get-tuple-element.21), kind=kLoop, calls=%fused_computation.12 | loop fusion | flops 16384000 | bytes 16384000 | tf_op jit(solution)/shard_map/concatenate | solution.py:76
  170.5 19.0 %fusion.58 = (f32[1536]{0:T(1024)S(1)}, f32[1536,2000]{0,1:T(8,128)}) fusion(bf16[1536,2048]{1,0:T(8,128)(2,1)} %bitcast_select_fusion, bf16[2048,2000]{0,1:T(8,128)(2,1)} %pad_maximum_fusion), kind=kOutput, calls=%fused_computation.180 | convolution fusion | flops 12585981952 | bytes 26777600 | tf_op jit(solution)/shard_map/dot_general | solution.py:13
  189.6 7.1 %fusion = (f32[1536]{0:T(1024)S(1)}, f32[1536]{0:T(1024)S(1)}, f32[1536]{0:T(1024)S(1)}) fusion(f32[1536,2000]{0,1:T(8,128)} %get-tuple-element.52, f32[1536]{0:T(1024)S(1)} %get-tuple-element.51, s32[1536]{0:T(1024)S(1)} %sub.185), kind=kLoop, calls=%fused_computation.6 | loop fusion | flops 21499392 | bytes 12318720 | tf_op jit(solution)/shard_map/reduce_sum | solution.py:16
  196.6 0.1 stack.92
  196.7 0.1 stack.91
  196.8 0.1 stack.90
  197.0 19.0 %fusion.59 = (f32[1536]{0:T(1024)S(1)}, f32[1536,2000]{0,1:T(8,128)}) fusion(bf16[1536,2048]{1,0:T(8,128)(2,1)} %all-gather.2.cloned.1.call-done, bf16[2048,2000]{0,1:T(8,128)(2,1)} %pad_maximum_fusion), kind=kOutput, calls=%fused_computation.181 | convolution fusion | flops 12585981952 | bytes 26777600 | tf_op jit(solution)/shard_map/dot_general | solution.py:13
  216.2 7.3 %fusion.1 = (f32[1536]{0:T(1024)S(1)}, f32[1536]{0:T(1024)S(1)}, f32[1536]{0:T(1024)S(1)}) fusion(f32[1536,2000]{0,1:T(8,128)} %get-tuple-element.54, f32[1536]{0:T(1024)S(1)} %get-tuple-element.53, s32[1536]{0:T(1024)S(1)} %sub.172), kind=kLoop, calls=%fused_computation.11 | loop fusion | flops 21499392 | bytes 12318720 | tf_op jit(solution)/shard_map/reduce_sum | solution.py:16
  223.4 0.1 stack.79
  223.5 0.1 stack.78
  223.6 0.1 stack.77
  223.8 0.1 reshape.249
  223.9 2.8 %collective-permute-start.11 = (f32[4,4,768]{2,1,0:T(4,128)S(1)}, f32[4,4,768]{2,1,0:T(4,128)S(1)}, u32[]{:S(2)}, u32[]{:S(2)}) collective-permute-start(f32[4,4,768]{2,1,0:T(4,128)S(1)} %reshape.249), channel_id=1, source_target_pairs={{0,2},{2,0},{4,6},{6,4},{8,10},{10,8},{12,14},{14,12},{16,18},{18,... | collective-permute-start | bytes 147464 | tf_op jit(solution)/shard_map/ppermute | solution.py:43
  226.7 0.1 squeeze.76
  226.8 0.1 squeeze.75
  227.1 1.7 collective-permute-done.11
  228.8 1.5 collective-permute-start.12
  230.4 4.1 %collective-permute-done.12 = f32[4,4,768]{2,1,0:T(4,128)S(1)} collective-permute-done((f32[4,4,768]{2,1,0:T(4,128)S(1)}, f32[4,4,768]{2,1,0:T(4,128)S(1)}, u32[]{:S(2)}, u32[]{:S(2)}) %collective-permute-start.12) | collective-permute-done | bytes 49184 | tf_op jit(solution)/shard_map/ppermute | solution.py:43
  234.7 4.1 %collective-permute-done.13 = f32[4,4,768]{2,1,0:T(4,128)S(1)} collective-permute-done((f32[4,4,768]{2,1,0:T(4,128)S(1)}, f32[4,4,768]{2,1,0:T(4,128)S(1)}, u32[]{:S(2)}, u32[]{:S(2)}) %collective-permute-start.13) | collective-permute-done | bytes 49184 | tf_op jit(solution)/shard_map/ppermute | solution.py:43
  238.8 1.7 collective-permute-start.14
  240.9 3.6 %collective-permute-done.14 = f32[4,4,768]{2,1,0:T(4,128)S(1)} collective-permute-done((f32[4,4,768]{2,1,0:T(4,128)S(1)}, f32[4,4,768]{2,1,0:T(4,128)S(1)}, u32[]{:S(2)}, u32[]{:S(2)}) %collective-permute-start.14) | collective-permute-done | bytes 49184 | tf_op jit(solution)/shard_map/ppermute | solution.py:43
  244.5 0.2 fusion.52
  244.8 1.1 collective-permute-done.15
  245.9 0.1 select_reduce_fusion.2
  246.0 2.0 collective-permute-start.16
  248.0 0.6 constant_dynamic-slice_fusion.8
  248.6 1.0 collective-permute-done.16
  249.6 4.3 %collective-permute-start.17 = (f32[16]{0:T(128)S(1)}, f32[16]{0:T(128)S(1)}, u32[]{:S(2)}, u32[]{:S(2)}) collective-permute-start(f32[16]{0:T(128)S(1)} %add.251), channel_id=1, source_target_pairs={{0,64},{32,96},{64,0},{96,32},{1,65},{33,97},{65,1},{97,33},{2,66}... | collective-permute-start | bytes 200 | tf_op jit(solution)/shard_map/ppermute | solution.py:43
  253.9 0.7 fusion.40
  254.6 0.9 collective-permute-done.17
  255.5 0.2 fusion.26
  255.7 0.2 fusion.27
  255.9 0.5 maximum_divide_fusion
  (68 shorter events, 1.8 us)
Async XLA Ops:
  7.2 189.8 %all-gather.2.cloned.1.call-start = ((), (), s32[]{:S(2)}) async-start(), calls=%async_computation | async-start | bytes 6684672 | tf_op jit(solution)/shard_map/all_gather | solution.py:71
  10.8 21.9 %collective-permute-start.7 = (bf16[96,2048]{1,0:T(8,128)(2,1)S(1)}, bf16[96,2048]{1,0:T(8,128)(2,1)S(1)}, u32[]{:S(2)}, u32[]{:S(2)}) collective-permute-start(bf16[96,2048]{1,0:T(8,128)(2,1)S(1)} %bitcast.193), channel_id=1, source_target_pairs={{0,24},{8,0},{16,8},{24,16},{1,25},{9,1},{17,9},{25,17},{2,26},{10... | collective-permute-start | bytes 1179656 | tf_op jit(solution)/shard_map/ppermute | solution.py:49
  13.9 18.8 %collective-permute-start.6 = (bf16[96,2048]{1,0:T(8,128)(2,1)S(1)}, bf16[96,2048]{1,0:T(8,128)(2,1)S(1)}, u32[]{:S(2)}, u32[]{:S(2)}) collective-permute-start(bf16[96,2048]{1,0:T(8,128)(2,1)S(1)} %bitcast.194), channel_id=1, source_target_pairs={{0,16},{8,24},{16,0},{24,8},{1,17},{9,25},{17,1},{25,9},{2,18},{10... | collective-permute-start | bytes 1179656 | tf_op jit(solution)/shard_map/ppermute | solution.py:49
  14.6 25.4 %collective-permute-start.5 = (bf16[96,2048]{1,0:T(8,128)(2,1)S(1)}, bf16[96,2048]{1,0:T(8,128)(2,1)S(1)}, u32[]{:S(2)}, u32[]{:S(2)}) collective-permute-start(bf16[96,2048]{1,0:T(8,128)(2,1)S(1)} %bitcast.195), channel_id=1, source_target_pairs={{0,8},{8,16},{16,24},{24,0},{1,9},{9,17},{17,25},{25,1},{2,10},{10... | collective-permute-start | bytes 1179656 | tf_op jit(solution)/shard_map/ppermute | solution.py:49
  15.5 141.7 %collective-permute-start = (bf16[2048,1000]{0,1:T(8,128)(2,1)}, bf16[2048,1000]{0,1:T(8,128)(2,1)}, u32[]{:S(2)}, u32[]{:S(2)}) collective-permute-start(bf16[2048,1000]{0,1:T(8,128)(2,1)} %param.8), channel_id=1, source_target_pairs={{0,1},{1,0},{2,3},{3,2},{4,5},{5,4},{6,7},{7,6},{8,9},{9,8},{10,11... | collective-permute-start | bytes 12288008 | tf_op jit(solution)/shard_map/ppermute | solution.py:74
  15.5 3.8 %collective-permute-start.1 = (s32[4,48]{1,0:T(4,128)}, s32[4,48]{1,0:T(4,128)S(1)}, u32[]{:S(2)}, u32[]{:S(2)}) collective-permute-start(s32[4,48]{1,0:T(4,128)} %param.9), channel_id=1, source_target_pairs={{0,2},{2,0},{4,6},{6,4},{8,10},{10,8},{12,14},{14,12},{16,18},{18,... | collective-permute-start | bytes 2312 | tf_op jit(solution)/shard_map/ppermute | solution.py:33
  20.0 5.2 %collective-permute-start.2 = (s32[8,48]{1,0:T(8,128)S(1)}, s32[8,48]{1,0:T(8,128)S(1)}, u32[]{:S(2)}, u32[]{:S(2)}) collective-permute-start(s32[8,48]{1,0:T(8,128)S(1)} %pad_add_fusion.3), channel_id=1, source_target_pairs={{0,4},{2,6},{4,0},{6,2},{8,12},{10,14},{12,8},{14,10},{16,20},{18,... | collective-permute-start | bytes 4616 | tf_op jit(solution)/shard_map/ppermute | solution.py:33
  25.2 21.7 %collective-permute-start.3 = (s32[16,48]{1,0:T(8,128)S(1)}, s32[16,48]{1,0:T(8,128)S(1)}, u32[]{:S(2)}, u32[]{:S(2)}) collective-permute-start(s32[16,48]{1,0:T(8,128)S(1)} %pad_add_fusion.2), channel_id=1, source_target_pairs={{0,8},{2,10},{4,12},{6,14},{8,0},{10,2},{12,4},{14,6},{16,24},{18,... | collective-permute-start | bytes 9224 | tf_op jit(solution)/shard_map/ppermute | solution.py:33
  42.2 56.8 %collective-permute-start.10 = (bf16[4,96,2048]{2,1,0:T(8,128)(2,1)}, bf16[4,96,2048]{2,1,0:T(8,128)(2,1)S(1)}, u32[]{:S(2)}, u32[]{:S(2)}) collective-permute-start(bf16[4,96,2048]{2,1,0:T(8,128)(2,1)} %broadcast_select_fusion.2), channel_id=1, source_target_pairs={{0,6},{2,0},{4,2},{6,4},{1,7},{3,1},{5,3},{7,5},{8,14},{10,8},{12,... | collective-permute-start | bytes 4718600 | tf_op jit(solution)/shard_map/ppermute | solution.py:49
  42.9 95.8 %collective-permute-start.9 = (bf16[4,96,2048]{2,1,0:T(8,128)(2,1)}, bf16[4,96,2048]{2,1,0:T(8,128)(2,1)}, u32[]{:S(2)}, u32[]{:S(2)}) collective-permute-start(bf16[4,96,2048]{2,1,0:T(8,128)(2,1)} %broadcast_select_fusion.2), channel_id=1, source_target_pairs={{0,4},{2,6},{4,0},{6,2},{1,5},{3,7},{5,1},{7,3},{8,12},{10,14},{12... | collective-permute-start | bytes 4718600 | tf_op jit(solution)/shard_map/ppermute | solution.py:49
  45.2 94.4 %collective-permute-start.8 = (bf16[4,96,2048]{2,1,0:T(8,128)(2,1)}, bf16[4,96,2048]{2,1,0:T(8,128)(2,1)}, u32[]{:S(2)}, u32[]{:S(2)}) collective-permute-start(bf16[4,96,2048]{2,1,0:T(8,128)(2,1)} %broadcast_select_fusion.2), channel_id=1, source_target_pairs={{0,2},{2,4},{4,6},{6,0},{1,3},{3,5},{5,7},{7,1},{8,10},{10,12},{12... | collective-permute-start | bytes 4718600 | tf_op jit(solution)/shard_map/ppermute | solution.py:49
  47.0 5.5 %collective-permute-start.4 = (s32[32,48]{1,0:T(8,128)S(1)}, s32[32,48]{1,0:T(8,128)S(1)}, u32[]{:S(2)}, u32[]{:S(2)}) collective-permute-start(s32[32,48]{1,0:T(8,128)S(1)} %pad_add_fusion.1), channel_id=1, source_target_pairs={{0,16},{2,18},{4,20},{6,22},{8,24},{10,26},{12,28},{14,30},{16,0},... | collective-permute-start | bytes 18440 | tf_op jit(solution)/shard_map/ppermute | solution.py:33
  151.0 6.2 %copy-start = (bf16[2048,1000]{0,1:T(8,128)(2,1)S(1)}, bf16[2048,1000]{0,1:T(8,128)(2,1)}, u32[]{:S(2)}) copy-start(bf16[2048,1000]{0,1:T(8,128)(2,1)} %param.8) | copy-start | bytes 12288004
  216.1 24.3 %copy-start.2 = (s32[16]{0:T(128)S(1)}, s32[16]{0:T(128)}, u32[]{:S(2)}) copy-start(s32[16]{0:T(128)} %param.10) | copy-start | bytes 196
  216.1 39.3 %copy-start.1 = (s32[16]{0:T(128)S(1)}, s32[16]{0:T(128)}, u32[]{:S(2)}) copy-start(s32[16]{0:T(128)} %param.11) | copy-start | bytes 196
  223.9 4.8 %collective-permute-start.11 = (f32[4,4,768]{2,1,0:T(4,128)S(1)}, f32[4,4,768]{2,1,0:T(4,128)S(1)}, u32[]{:S(2)}, u32[]{:S(2)}) collective-permute-start(f32[4,4,768]{2,1,0:T(4,128)S(1)} %reshape.249), channel_id=1, source_target_pairs={{0,2},{2,0},{4,6},{6,4},{8,10},{10,8},{12,14},{14,12},{16,18},{18,... | collective-permute-start | bytes 147464 | tf_op jit(solution)/shard_map/ppermute | solution.py:43
  228.8 5.7 %collective-permute-start.12 = (f32[4,4,768]{2,1,0:T(4,128)S(1)}, f32[4,4,768]{2,1,0:T(4,128)S(1)}, u32[]{:S(2)}, u32[]{:S(2)}) collective-permute-start(f32[4,4,768]{2,1,0:T(4,128)S(1)} %pad_maximum_fusion.3), channel_id=1, source_target_pairs={{0,4},{2,6},{4,0},{6,2},{8,12},{10,14},{12,8},{14,10},{16,20},{18,... | collective-permute-start | bytes 147464 | tf_op jit(solution)/shard_map/ppermute | solution.py:43
  234.6 4.2 %collective-permute-start.13 = (f32[4,4,768]{2,1,0:T(4,128)S(1)}, f32[4,4,768]{2,1,0:T(4,128)S(1)}, u32[]{:S(2)}, u32[]{:S(2)}) collective-permute-start(f32[4,4,768]{2,1,0:T(4,128)S(1)} %pad_maximum_fusion.4), channel_id=1, source_target_pairs={{0,8},{2,10},{4,12},{6,14},{8,0},{10,2},{12,4},{14,6},{16,24},{18,... | collective-permute-start | bytes 147464 | tf_op jit(solution)/shard_map/ppermute | solution.py:43
  238.8 5.7 %collective-permute-start.14 = (f32[4,4,768]{2,1,0:T(4,128)S(1)}, f32[4,4,768]{2,1,0:T(4,128)S(1)}, u32[]{:S(2)}, u32[]{:S(2)}) collective-permute-start(f32[4,4,768]{2,1,0:T(4,128)S(1)} %pad_maximum_fusion.5), channel_id=1, source_target_pairs={{0,16},{2,18},{4,20},{6,22},{8,24},{10,26},{12,28},{14,30},{16,0},... | collective-permute-start | bytes 147464 | tf_op jit(solution)/shard_map/ppermute | solution.py:43
  244.7 1.2 collective-permute-start.15
  246.0 3.6 %collective-permute-start.16 = (f32[16]{0:T(128)S(1)}, f32[16]{0:T(128)S(1)}, u32[]{:S(2)}, u32[]{:S(2)}) collective-permute-start(f32[16]{0:T(128)S(1)} %select_reduce_fusion.2), channel_id=1, source_target_pairs={{0,32},{32,0},{64,96},{96,64},{1,33},{33,1},{65,97},{97,65},{2,34}... | collective-permute-start | bytes 200 | tf_op jit(solution)/shard_map/ppermute | solution.py:43
  249.6 5.9 %collective-permute-start.17 = (f32[16]{0:T(128)S(1)}, f32[16]{0:T(128)S(1)}, u32[]{:S(2)}, u32[]{:S(2)}) collective-permute-start(f32[16]{0:T(128)S(1)} %add.251), channel_id=1, source_target_pairs={{0,64},{32,96},{64,0},{96,32},{1,65},{33,97},{65,1},{97,33},{2,66}... | collective-permute-start | bytes 200 | tf_op jit(solution)/shard_map/ppermute | solution.py:43
Sparse Core Ops, SparseCore 0:
  11.0 133.5 all-gather.1

commit v6 on v4

--- a/solution.py
+++ b/solution.py
@@ -1,23 +1,46 @@
+import functools
+
 import jax
 import jax.numpy as jnp
 import numpy as np
 from jax import lax
+from jax.experimental import pallas as pl
+from jax.experimental.pallas import tpu as pltpu
 from jax.sharding import Mesh
 from jax.sharding import PartitionSpec as P
 
 norm_eps = 1e-06
-BLOCK = 1536
+TILE = 256
 
 
-def block_stats(rows, tokens, weight, offset):
-    logits = jnp.dot(rows, weight, preferred_element_type=jnp.float32)
-    row_top = jnp.max(logits, axis=1)
-    exps = jnp.exp(logits - row_top[:, None])
-    exp_total = jnp.sum(exps, axis=1)
-    moment = jnp.sum(exps * logits, axis=1)
-    columns = jnp.arange(weight.shape[1], dtype=jnp.int32)
-    picked = jnp.sum(jnp.where(columns[None, :] == (tokens - offset)[:, None], logits, 0.0), axis=1)
-    return jnp.stack([row_top, exp_total, moment, picked])
+def stats_kernel(real_cols, rows_ref, w_ref, ids_ref, out_ref):
+    raw = jnp.dot(rows_ref[...], w_ref[...], preferred_element_type=jnp.float32)
+    cols = lax.broadcasted_iota(jnp.int32, raw.shape, 1)
+    masked = jnp.where(cols < real_cols, raw, -jnp.inf)
+    top = jnp.max(masked, axis=1, keepdims=True)
+    exps = jnp.exp(masked - top)
+    out_ref[:, 0:1] = top
+    out_ref[:, 1:2] = jnp.sum(exps, axis=1, keepdims=True)
+    out_ref[:, 2:3] = jnp.sum(exps * raw, axis=1, keepdims=True)
+    out_ref[:, 3:4] = jnp.sum(jnp.where(cols == ids_ref[...], raw, 0.0), axis=1, keepdims=True)
+
+
+def kernel_stats(rows, weight, local_ids, real_cols):
+    n, d = rows.shape
+    c = weight.shape[1]
+    return pl.pallas_call(
+        functools.partial(stats_kernel, real_cols),
+        grid=(n // TILE,),
+        in_specs=[
+            pl.BlockSpec((TILE, d), lambda i: (i, 0)),
+            pl.BlockSpec((d, c), lambda i: (0, 0)),
+            pl.BlockSpec((TILE, 1), lambda i: (i, 0)),
+        ],
+        out_specs=pl.BlockSpec((TILE, 4), lambda i: (i, 0)),
+        out_shape=jax.ShapeDtypeStruct((n, 4), jnp.float32),
+        compiler_params=pltpu.CompilerParams(vmem_limit_bytes=48 * 1024 * 1024),
+        cost_estimate=pl.CostEstimate(flops=2 * n * d * c, transcendentals=n * c, bytes_accessed=2 * (n * d + d * c) + 20 * n),
+    )(rows, weight, local_ids)
 
 
 def merge(a, b):
@@ -62,16 +85,15 @@
     other = lax.ppermute(head_weight, "core", [(0, 1), (1, 0)])
     first = core == 0
     weight = jnp.concatenate([jnp.where(first, head_weight, other), jnp.where(first, other, head_weight)], axis=1)
+    cols = weight.shape[1]
+    weight = jnp.pad(weight, ((0, 0), (0, -cols % 128)))
     weight = lax.optimization_barrier(weight)
     offset = chip * (n_core * vocab_dev)
     half_len = n_chip * pos_dev
     flat_tokens = xor_gather(token_ids, "chip", n_chip, chip).reshape(n_chip * own_rows)
     own_lengths = lax.dynamic_slice_in_dim(lengths, req_index * req_dev, req_dev)
-    blocks = []
-    for start in range(0, req_dev * half_len, BLOCK):
-        size = min(BLOCK, req_dev * half_len - start)
-        blocks.append(block_stats(flat_rows[start : start + size], flat_tokens[start : start + size], weight, offset))
-    stats = jnp.concatenate(blocks, axis=1).reshape(4, n_chip, req_dev, pos_dev)
+    local_ids = (flat_tokens - offset).reshape(-1, 1)
+    stats = kernel_stats(flat_rows, weight, local_ids, cols).T.reshape(4, n_chip, req_dev, pos_dev)
     stats = stats.transpose(0, 2, 1, 3).reshape(4, req_dev, half_len)
     stats = xor_reduce(stats, "chip", n_chip, merge)
     row_top, exp_total, moment, token_logit = stats[0], stats[1], stats[2], stats[3]

time: 183 us -> 188 us (1.027)
  Pallas kernels: 0 us -> 39.1 us
  matrix products: 33.1 us -> 0 us
  local copies, waits for them, and re-layouts: 1.31 us -> 23.7 us
  waiting for transfers between devices: 88.1 us -> 72.9 us
  other arithmetic: 28.8 us -> 16.4 us
  starting transfers between devices: 17.6 us -> 20.2 us
    pallas_call x0 -> x1, Pallas kernels: none -> 39.1 us  [kernel_stats(): pl.pallas_call(functools.partial(stats_kernel, real_cols), grid=(n // TIL...]
    dot_general x2 -> x0, matrix products: 33.1 us -> none  [block_stats(): logits = jnp.dot(rows, weight, preferred_element_type=jnp.float32)]
    reduce_sum x2 -> x0, other arithmetic: 8.09 us -> none  [block_stats(): exp_total = jnp.sum(exps, axis=1)]
    all_gather x1, waiting for transfers between devices: 58.7 us -> 52 us  [body(): lax.all_gather(normed.reshape(own_rows, model_width), 'chip', axis=0, til...]
    ppermute x0 -> x1, local copies, waits for them, and re-layouts: none -> 6.43 us  [body(): other = lax.ppermute(head_weight, 'core', [(0, 1), (1, 0)])]
    unnamed x6 -> x7, local copies, waits for them, and re-layouts: 0.02 us -> 6.34 us
    ppermute x6, waiting for transfers between devices: 17.5 us -> 11.3 us  [xor_reduce(): x = combine(x, lax.ppermute(x, axis, [(i, i ^ bit) for i in range(size)]))]
    slice x2, local copies, waits for them, and re-layouts: 0.01 us -> 5.4 us  [merge(): a[1] * ea + b[1] * eb]
  transfers between devices with their start and end apart: 13 -> 13, of which waited for: 12 -> 10; matrix products, arithmetic and copies ran while one was open for 9% -> 18% of each run, Pallas kernels for 0% -> 0%
where the time goes in v6:
time: 188 us; the launch traced here: 186 us
  waiting for transfers between devices  72.9 us (39%)
  Pallas kernels  39.1 us (21%)
  local copies, waits for them, and re-layouts  23.7 us (13%)
  starting transfers between devices  20.2 us (11%)
  other arithmetic  16.4 us (9%)
  between operations  14.2 us (8%)
    all_gather x1, waiting for transfers between devices, body(): lax.all_gather(normed.reshape(own_rows, model_width), 'chip', axis=0, til...  52 us
    pallas_call x1, Pallas kernels, kernel_stats(): pl.pallas_call(functools.partial(stats_kernel, real_cols), grid=(n // TIL...  39.1 us
    ppermute x6, starting transfers between devices, xor_reduce(): x = combine(x, lax.ppermute(x, axis, [(i, i ^ bit) for i in range(size)]))  12.4 us
    ppermute x6, waiting for transfers between devices, xor_reduce(): x = combine(x, lax.ppermute(x, axis, [(i, i ^ bit) for i in range(size)]))  11.3 us
    ppermute x4, waiting for transfers between devices, xor_gather(): other = lax.ppermute(x, axis, [(i, i ^ bit) for i in range(size)])  8.44 us
    ppermute x4, starting transfers between devices, xor_gather(): other = lax.ppermute(x, axis, [(i, i ^ bit) for i in range(size)])  7.63 us
    ppermute x1, local copies, waits for them, and re-layouts, body(): other = lax.ppermute(head_weight, 'core', [(0, 1), (1, 0)])  6.43 us
    unnamed x7, local copies, waits for them, and re-layouts  6.34 us
  transfers between devices with their start and end apart: 13, of which 10 were waited for; matrix products, arithmetic and copies ran while one was open for 18% of the time, Pallas kernels for 0%

profile of v6, /device:TPU:2, one launch (start us, length us, event | category | flops | bytes accessed | tf_op | source)
XLA Modules:
  0.0 186.5 jit_solution(4532593211756224966)
XLA Ops:
  7.2 0.0 all-gather.2.cloned.1.call-start
  7.2 1.4 fusion.3
  8.6 2.3 %fusion.5 = bf16[4,48,2048]{2,1,0:T(8,128)(2,1)} fusion(bf16[4,48,2048]{2,1,0:T(8,128)(2,1)} %param.6, f32[2048]{0:T(1024)} %param.7, f32[4,48]{1,0:T(4,128)S(1)} %add_rsqrt_fusion), kind=kLoop, calls=%fused_computation.10 | loop fusion | flops 1572864 | bytes 1581824 | tf_op jit(solution)/shard_map/convert_element_type | solution.py:82
  10.9 0.0 all-gather.2.cloned.1.call-update
  10.9 0.1 collective-permute-start
  11.0 0.5 collective-permute-start.1
  11.5 3.4 %collective-permute-done.1 = s32[4,48]{1,0:T(4,128)S(1)} collective-permute-done((s32[4,48]{1,0:T(4,128)}, s32[4,48]{1,0:T(4,128)S(1)}, u32[]{:S(2)}, u32[]{:S(2)}) %collective-permute-start.1) | collective-permute-done | bytes 800 | tf_op jit(solution)/shard_map/ppermute | solution.py:56
  14.9 0.7 broadcast_select_fusion.9
  15.6 2.2 %collective-permute-start.2 = (s32[8,48]{1,0:T(8,128)S(1)}, s32[8,48]{1,0:T(8,128)S(1)}, u32[]{:S(2)}, u32[]{:S(2)}) collective-permute-start(s32[8,48]{1,0:T(8,128)S(1)} %pad_add_fusion.2), channel_id=1, source_target_pairs={{0,4},{2,6},{4,0},{6,2},{8,12},{10,14},{12,8},{14,10},{16,20},{18,... | collective-permute-start | bytes 4616 | tf_op jit(solution)/shard_map/ppermute | solution.py:56
  17.8 3.0 %collective-permute-done.2 = s32[8,48]{1,0:T(8,128)S(1)} collective-permute-done((s32[8,48]{1,0:T(8,128)S(1)}, s32[8,48]{1,0:T(8,128)S(1)}, u32[]{:S(2)}, u32[]{:S(2)}) %collective-permute-start.2) | collective-permute-done | bytes 1568 | tf_op jit(solution)/shard_map/ppermute | solution.py:56
  20.8 1.7 collective-permute-start.3
  22.5 2.1 %collective-permute-done.3 = s32[16,48]{1,0:T(8,128)S(1)} collective-permute-done((s32[16,48]{1,0:T(8,128)S(1)}, s32[16,48]{1,0:T(8,128)S(1)}, u32[]{:S(2)}, u32[]{:S(2)}) %collective-permute-start.3) | collective-permute-done | bytes 3104 | tf_op jit(solution)/shard_map/ppermute | solution.py:56
  24.6 3.3 %collective-permute-start.4 = (s32[32,48]{1,0:T(8,128)S(1)}, s32[32,48]{1,0:T(8,128)S(1)}, u32[]{:S(2)}, u32[]{:S(2)}) collective-permute-start(s32[32,48]{1,0:T(8,128)S(1)} %pad_add_fusion), channel_id=1, source_target_pairs={{0,16},{2,18},{4,20},{6,22},{8,24},{10,26},{12,28},{14,30},{16,0},... | collective-permute-start | bytes 18440 | tf_op jit(solution)/shard_map/ppermute | solution.py:56
  27.9 6.3 %copy.48 = bf16[2048,1000]{1,0:T(8,128)(2,1)} copy(bf16[2048,1000]{0,1:T(8,128)(2,1)} %param.8) | data formatting | bytes 8192000 | tf_op args[2]
  34.2 0.0 collective-permute-done.4
  34.2 0.8 sub.125.ids_ref
  35.0 0.0 collective-permute-done
  35.0 6.4 %copy.49 = bf16[2048,1000]{1,0:T(8,128)(2,1)} copy(bf16[2048,1000]{0,1:T(8,128)(2,1)} %collective-permute-done) | data formatting | bytes 8192000 | tf_op jit(solution)/shard_map/ppermute | solution.py:85
  41.4 3.8 %broadcast_select_fusion.1 = (bf16[2048,1000]{1,0:T(8,128)(2,1)S(1)}, bf16[2048,1000]{1,0:T(8,128)(2,1)S(1)}) fusion(bf16[2048,1000]{1,0:T(8,128)(2,1)} %copy.48, bf16[2048,1000]{1,0:T(8,128)(2,1)} %copy.49, pred[]{:T(512)S(6)} %eq.16), kind=kLoop, calls=%fused_computation.5 | loop fusion | flops 4096000 | bytes 16384001 | tf_op jit(solution)/shard_map/jit(_where)/select_n | solution.py:87
  45.2 6.1 %fusion.2.w_ref = bf16[2048,2048]{1,0:T(8,128)(2,1)} fusion(bf16[2048,1000]{1,0:T(8,128)(2,1)S(1)} %get-tuple-element.16, bf16[2048,1000]{1,0:T(8,128)(2,1)S(1)} %get-tuple-element.15), kind=kLoop, calls=%fused_computation.3 | loop fusion | flops 29360128 | bytes 16580608 | tf_op jit(solution)/shard_map/concatenate | solution.py:87
  51.3 52.0 %all-gather.2.cloned.1.call-done.rows_ref = bf16[3072,2048]{1,0:T(8,128)(2,1)} async-done(((bf16[192,2048]{1,0:T(8,128)(2,1)}), bf16[3072,2048]{1,0:T(8,128)(2,1)}) %all-gather.2.cloned.1.call-update) | async-done | bytes 12582928 | tf_op jit(solution)/shard_map/all_gather | solution.py:84
  103.3 39.1 %shard_map.85 = f32[3072,4]{1,0:T(8,128)S(1)} custom-call(bf16[3072,2048]{1,0:T(8,128)(2,1)} %all-gather.2.cloned.1.call-done.rows_ref, bf16[2048,2048]{1,0:T(8,128)(2,1)} %fusion.2.w_ref, s32[3072,1]{1,0:T(8,128)S(1)} %sub.125.ids_ref), custom_call_target="tpu_custom_call" | custom-call | flops 25769803776 | bytes 21032960 | tf_op jit(solution)/shard_map/pallas_call | solution.py:31
  142.4 0.6 copy.54
  143.0 0.1 reshape.101
  143.1 0.6 collective-permute-start.5
  143.7 3.4 %fusion.49 = (f32[1,4,16,48]{0,3,1,2:T(8,128)}, f32[1,4,16,48]{0,3,1,2:T(8,128)}, f32[1,4,16,48]{0,3,1,2:T(8,128)}, f32[1,4,16,48]{0,3,1,2:T(8,128)S(1)}) fusion(f32[4,4,16,48]{0,3,1,2:T(8,128)S(1)} %bitcast.170), kind=kLoop, calls=%fused_computation.132 | loop fusion | bytes 98304 | tf_op jit(solution)/shard_map/slice | solution.py:50
  147.2 0.0 copy-start
  147.2 0.0 copy-start.2
  147.2 0.0 copy-start.1
  147.2 2.1 %copy.55 = f32[1,4,16,48]{3,2,1,0:T(8,128)S(1)} copy(f32[1,4,16,48]{0,3,1,2:T(8,128)} %get-tuple-element.19) | data formatting | bytes 24576 | tf_op jit(solution)/shard_map/slice | solution.py:47
  149.3 0.1 squeeze.75
  149.4 2.0 %copy.56 = f32[1,4,16,48]{3,2,1,0:T(8,128)S(1)} copy(f32[1,4,16,48]{0,3,1,2:T(8,128)} %get-tuple-element.17) | data formatting | bytes 24576 | tf_op jit(solution)/shard_map/slice | solution.py:50
  151.3 0.1 squeeze.76
  151.4 0.0 copy-done
  151.4 0.6 copy.57
  152.0 0.1 squeeze.77
  152.1 0.6 copy.53
  152.7 0.1 squeeze.78
  152.8 0.0 collective-permute-done.5
  152.9 2.5 %collective-permute-start.6 = (f32[4,4,768]{2,1,0:T(4,128)S(1)}, f32[4,4,768]{2,1,0:T(4,128)S(1)}, u32[]{:S(2)}, u32[]{:S(2)}) collective-permute-start(f32[4,4,768]{2,1,0:T(4,128)S(1)} %pad_maximum_fusion), channel_id=1, source_target_pairs={{0,4},{2,6},{4,0},{6,2},{8,12},{10,14},{12,8},{14,10},{16,20},{18,... | collective-permute-start | bytes 147464 | tf_op jit(solution)/shard_map/ppermute | solution.py:66
  155.3 3.2 %collective-permute-done.6 = f32[4,4,768]{2,1,0:T(4,128)S(1)} collective-permute-done((f32[4,4,768]{2,1,0:T(4,128)S(1)}, f32[4,4,768]{2,1,0:T(4,128)S(1)}, u32[]{:S(2)}, u32[]{:S(2)}) %collective-permute-start.6) | collective-permute-done | bytes 49184 | tf_op jit(solution)/shard_map/ppermute | solution.py:66
  158.6 1.5 collective-permute-start.7
  160.1 2.6 %collective-permute-done.7 = f32[4,4,768]{2,1,0:T(4,128)S(1)} collective-permute-done((f32[4,4,768]{2,1,0:T(4,128)S(1)}, f32[4,4,768]{2,1,0:T(4,128)S(1)}, u32[]{:S(2)}, u32[]{:S(2)}) %collective-permute-start.7) | collective-permute-done | bytes 49184 | tf_op jit(solution)/shard_map/ppermute | solution.py:66
  162.8 3.0 %collective-permute-start.8 = (f32[4,4,768]{2,1,0:T(4,128)S(1)}, f32[4,4,768]{2,1,0:T(4,128)S(1)}, u32[]{:S(2)}, u32[]{:S(2)}) collective-permute-start(f32[4,4,768]{2,1,0:T(4,128)S(1)} %pad_maximum_fusion.2), channel_id=1, source_target_pairs={{0,16},{2,18},{4,20},{6,22},{8,24},{10,26},{12,28},{14,30},{16,0},... | collective-permute-start | bytes 147464 | tf_op jit(solution)/shard_map/ppermute | solution.py:66
  165.9 0.0 copy-done.2
  165.9 0.1 dynamic_slice.9
  166.0 0.1 squeeze.73
  166.0 0.1 squeeze.82
  166.1 0.1 squeeze.87
  166.2 0.1 squeeze.92
  166.3 2.2 %collective-permute-done.8 = f32[4,4,768]{2,1,0:T(4,128)S(1)} collective-permute-done((f32[4,4,768]{2,1,0:T(4,128)S(1)}, f32[4,4,768]{2,1,0:T(4,128)S(1)}, u32[]{:S(2)}, u32[]{:S(2)}) %collective-permute-start.8) | collective-permute-done | bytes 49184 | tf_op jit(solution)/shard_map/ppermute | solution.py:66
  168.5 0.2 fusion.46
  168.7 0.1 collective-permute-start.9
  168.8 1.1 collective-permute-done.9
  169.9 0.1 select_reduce_fusion
  170.0 1.6 collective-permute-start.10
  171.6 2.0 %collective-permute-done.10 = f32[16]{0:T(128)S(1)} collective-permute-done((f32[16]{0:T(128)S(1)}, f32[16]{0:T(128)S(1)}, u32[]{:S(2)}, u32[]{:S(2)}) %collective-permute-start.10) | collective-permute-done | bytes 96 | tf_op jit(solution)/shard_map/ppermute | solution.py:66
  173.6 3.2 %collective-permute-start.11 = (f32[16]{0:T(128)S(1)}, f32[16]{0:T(128)S(1)}, u32[]{:S(2)}, u32[]{:S(2)}) collective-permute-start(f32[16]{0:T(128)S(1)} %add.179), channel_id=1, source_target_pairs={{0,64},{32,96},{64,0},{96,32},{1,65},{33,97},{65,1},{97,33},{2,66}... | collective-permute-start | bytes 200 | tf_op jit(solution)/shard_map/ppermute | solution.py:66
  176.8 0.7 constant_dynamic-slice_fusion.8
  177.4 1.3 collective-permute-done.11
  178.7 0.0 copy-done.1
  178.7 0.2 fusion.26
  178.9 0.2 fusion.27
  179.1 0.5 maximum_divide_fusion
  (24 shorter events, 0.3 us)
Async XLA Ops:
  7.2 96.1 %all-gather.2.cloned.1.call-start = ((), (), s32[]{:S(2)}) async-start(), calls=%async_computation | async-start | bytes 13369344 | tf_op jit(solution)/shard_map/all_gather | solution.py:84
  10.9 24.1 %collective-permute-start = (bf16[2048,1000]{0,1:T(8,128)(2,1)}, bf16[2048,1000]{0,1:T(8,128)(2,1)}, u32[]{:S(2)}, u32[]{:S(2)}) collective-permute-start(bf16[2048,1000]{0,1:T(8,128)(2,1)} %param.8), channel_id=1, source_target_pairs={{0,1},{1,0},{2,3},{3,2},{4,5},{5,4},{6,7},{7,6},{8,9},{9,8},{10,11... | collective-permute-start | bytes 12288008 | tf_op jit(solution)/shard_map/ppermute | solution.py:85
  11.0 3.9 %collective-permute-start.1 = (s32[4,48]{1,0:T(4,128)}, s32[4,48]{1,0:T(4,128)S(1)}, u32[]{:S(2)}, u32[]{:S(2)}) collective-permute-start(s32[4,48]{1,0:T(4,128)} %param.9), channel_id=1, source_target_pairs={{0,2},{2,0},{4,6},{6,4},{8,10},{10,8},{12,14},{14,12},{16,18},{18,... | collective-permute-start | bytes 2312 | tf_op jit(solution)/shard_map/ppermute | solution.py:56
  15.6 5.2 %collective-permute-start.2 = (s32[8,48]{1,0:T(8,128)S(1)}, s32[8,48]{1,0:T(8,128)S(1)}, u32[]{:S(2)}, u32[]{:S(2)}) collective-permute-start(s32[8,48]{1,0:T(8,128)S(1)} %pad_add_fusion.2), channel_id=1, source_target_pairs={{0,4},{2,6},{4,0},{6,2},{8,12},{10,14},{12,8},{14,10},{16,20},{18,... | collective-permute-start | bytes 4616 | tf_op jit(solution)/shard_map/ppermute | solution.py:56
  20.8 3.7 %collective-permute-start.3 = (s32[16,48]{1,0:T(8,128)S(1)}, s32[16,48]{1,0:T(8,128)S(1)}, u32[]{:S(2)}, u32[]{:S(2)}) collective-permute-start(s32[16,48]{1,0:T(8,128)S(1)} %pad_add_fusion.1), channel_id=1, source_target_pairs={{0,8},{2,10},{4,12},{6,14},{8,0},{10,2},{12,4},{14,6},{16,24},{18,... | collective-permute-start | bytes 9224 | tf_op jit(solution)/shard_map/ppermute | solution.py:56
  24.6 9.6 %collective-permute-start.4 = (s32[32,48]{1,0:T(8,128)S(1)}, s32[32,48]{1,0:T(8,128)S(1)}, u32[]{:S(2)}, u32[]{:S(2)}) collective-permute-start(s32[32,48]{1,0:T(8,128)S(1)} %pad_add_fusion), channel_id=1, source_target_pairs={{0,16},{2,18},{4,20},{6,22},{8,24},{10,26},{12,28},{14,30},{16,0},... | collective-permute-start | bytes 18440 | tf_op jit(solution)/shard_map/ppermute | solution.py:56
  143.1 9.7 %collective-permute-start.5 = (f32[4,4,768]{2,1,0:T(4,128)S(1)}, f32[4,4,768]{2,1,0:T(4,128)S(1)}, u32[]{:S(2)}, u32[]{:S(2)}) collective-permute-start(f32[4,4,768]{2,1,0:T(4,128)S(1)} %reshape.101), channel_id=1, source_target_pairs={{0,2},{2,0},{4,6},{6,4},{8,10},{10,8},{12,14},{14,12},{16,18},{18,... | collective-permute-start | bytes 147464 | tf_op jit(solution)/shard_map/ppermute | solution.py:66
  147.2 4.3 %copy-start = (f32[1,4,16,48]{0,3,1,2:T(8,128)S(1)}, f32[1,4,16,48]{0,3,1,2:T(8,128)}, u32[]{:S(2)}) copy-start(f32[1,4,16,48]{0,3,1,2:T(8,128)} %get-tuple-element.18) | copy-start | bytes 36868
  147.2 18.7 %copy-start.2 = (s32[16]{0:T(128)S(1)}, s32[16]{0:T(128)}, u32[]{:S(2)}) copy-start(s32[16]{0:T(128)} %param.10) | copy-start | bytes 196
  147.2 31.5 %copy-start.1 = (s32[16]{0:T(128)S(1)}, s32[16]{0:T(128)}, u32[]{:S(2)}) copy-start(s32[16]{0:T(128)} %param.11) | copy-start | bytes 196
  152.9 5.7 %collective-permute-start.6 = (f32[4,4,768]{2,1,0:T(4,128)S(1)}, f32[4,4,768]{2,1,0:T(4,128)S(1)}, u32[]{:S(2)}, u32[]{:S(2)}) collective-permute-start(f32[4,4,768]{2,1,0:T(4,128)S(1)} %pad_maximum_fusion), channel_id=1, source_target_pairs={{0,4},{2,6},{4,0},{6,2},{8,12},{10,14},{12,8},{14,10},{16,20},{18,... | collective-permute-start | bytes 147464 | tf_op jit(solution)/shard_map/ppermute | solution.py:66
  158.6 4.2 %collective-permute-start.7 = (f32[4,4,768]{2,1,0:T(4,128)S(1)}, f32[4,4,768]{2,1,0:T(4,128)S(1)}, u32[]{:S(2)}, u32[]{:S(2)}) collective-permute-start(f32[4,4,768]{2,1,0:T(4,128)S(1)} %pad_maximum_fusion.1), channel_id=1, source_target_pairs={{0,8},{2,10},{4,12},{6,14},{8,0},{10,2},{12,4},{14,6},{16,24},{18,... | collective-permute-start | bytes 147464 | tf_op jit(solution)/shard_map/ppermute | solution.py:66
  162.8 5.7 %collective-permute-start.8 = (f32[4,4,768]{2,1,0:T(4,128)S(1)}, f32[4,4,768]{2,1,0:T(4,128)S(1)}, u32[]{:S(2)}, u32[]{:S(2)}) collective-permute-start(f32[4,4,768]{2,1,0:T(4,128)S(1)} %pad_maximum_fusion.2), channel_id=1, source_target_pairs={{0,16},{2,18},{4,20},{6,22},{8,24},{10,26},{12,28},{14,30},{16,0},... | collective-permute-start | bytes 147464 | tf_op jit(solution)/shard_map/ppermute | solution.py:66
  168.7 1.2 collective-permute-start.9
  170.0 3.6 %collective-permute-start.10 = (f32[16]{0:T(128)S(1)}, f32[16]{0:T(128)S(1)}, u32[]{:S(2)}, u32[]{:S(2)}) collective-permute-start(f32[16]{0:T(128)S(1)} %select_reduce_fusion), channel_id=1, source_target_pairs={{0,32},{32,0},{64,96},{96,64},{1,33},{33,1},{65,97},{97,65},{2,34}... | collective-permute-start | bytes 200 | tf_op jit(solution)/shard_map/ppermute | solution.py:66
  173.6 5.1 %collective-permute-start.11 = (f32[16]{0:T(128)S(1)}, f32[16]{0:T(128)S(1)}, u32[]{:S(2)}, u32[]{:S(2)}) collective-permute-start(f32[16]{0:T(128)S(1)} %add.179), channel_id=1, source_target_pairs={{0,64},{32,96},{64,0},{96,32},{1,65},{33,97},{65,1},{97,33},{2,66}... | collective-permute-start | bytes 200 | tf_op jit(solution)/shard_map/ppermute | solution.py:66
Sparse Core Ops, SparseCore 0:
  11.1 92.1 all-gather.1

commit v7 on v6

--- a/solution.py
+++ b/solution.py
@@ -14,15 +14,15 @@
 
 
 def stats_kernel(real_cols, rows_ref, w_ref, ids_ref, out_ref):
-    raw = jnp.dot(rows_ref[...], w_ref[...], preferred_element_type=jnp.float32)
-    cols = lax.broadcasted_iota(jnp.int32, raw.shape, 1)
+    raw = lax.dot_general(w_ref[...], rows_ref[...], (((0,), (1,)), ((), ())), preferred_element_type=jnp.float32)
+    cols = lax.broadcasted_iota(jnp.int32, raw.shape, 0)
     masked = jnp.where(cols < real_cols, raw, -jnp.inf)
-    top = jnp.max(masked, axis=1, keepdims=True)
+    top = jnp.max(masked, axis=0, keepdims=True)
     exps = jnp.exp(masked - top)
-    out_ref[:, 0:1] = top
-    out_ref[:, 1:2] = jnp.sum(exps, axis=1, keepdims=True)
-    out_ref[:, 2:3] = jnp.sum(exps * raw, axis=1, keepdims=True)
-    out_ref[:, 3:4] = jnp.sum(jnp.where(cols == ids_ref[...], raw, 0.0), axis=1, keepdims=True)
+    out_ref[0:1, :] = top
+    out_ref[1:2, :] = jnp.sum(exps, axis=0, keepdims=True)
+    out_ref[2:3, :] = jnp.sum(exps * raw, axis=0, keepdims=True)
+    out_ref[3:4, :] = jnp.sum(jnp.where(cols == ids_ref[...], raw, 0.0), axis=0, keepdims=True)
 
 
 def kernel_stats(rows, weight, local_ids, real_cols):
@@ -34,10 +34,10 @@
         in_specs=[
             pl.BlockSpec((TILE, d), lambda i: (i, 0)),
             pl.BlockSpec((d, c), lambda i: (0, 0)),
-            pl.BlockSpec((TILE, 1), lambda i: (i, 0)),
+            pl.BlockSpec((1, TILE), lambda i: (0, i)),
         ],
-        out_specs=pl.BlockSpec((TILE, 4), lambda i: (i, 0)),
-        out_shape=jax.ShapeDtypeStruct((n, 4), jnp.float32),
+        out_specs=pl.BlockSpec((4, TILE), lambda i: (0, i)),
+        out_shape=jax.ShapeDtypeStruct((4, n), jnp.float32),
         compiler_params=pltpu.CompilerParams(vmem_limit_bytes=48 * 1024 * 1024),
         cost_estimate=pl.CostEstimate(flops=2 * n * d * c, transcendentals=n * c, bytes_accessed=2 * (n * d + d * c) + 20 * n),
     )(rows, weight, local_ids)
@@ -92,8 +92,8 @@
     half_len = n_chip * pos_dev
     flat_tokens = xor_gather(token_ids, "chip", n_chip, chip).reshape(n_chip * own_rows)
     own_lengths = lax.dynamic_slice_in_dim(lengths, req_index * req_dev, req_dev)
-    local_ids = (flat_tokens - offset).reshape(-1, 1)
-    stats = kernel_stats(flat_rows, weight, local_ids, cols).T.reshape(4, n_chip, req_dev, pos_dev)
+    local_ids = (flat_tokens - offset).reshape(1, -1)
+    stats = kernel_stats(flat_rows, weight, local_ids, cols).reshape(4, n_chip, req_dev, pos_dev)
     stats = stats.transpose(0, 2, 1, 3).reshape(4, req_dev, half_len)
     stats = xor_reduce(stats, "chip", n_chip, merge)
     row_top, exp_total, moment, token_logit = stats[0], stats[1], stats[2], stats[3]

time: 188 us -> 186 us (0.989)
  local copies, waits for them, and re-layouts: 23.7 us -> 14 us
  waiting for transfers between devices: 72.9 us -> 79.7 us
  Pallas kernels: 39.1 us -> 43.6 us
  starting transfers between devices: 20.2 us -> 17.6 us
    ppermute x6, waiting for transfers between devices: 11.3 us -> 17.5 us  [xor_reduce(): x = combine(x, lax.ppermute(x, axis, [(i, i ^ bit) for i in range(size)]))]
    slice x2, local copies, waits for them, and re-layouts: 5.4 us -> 0.01 us  [merge(): a[1] * ea + b[1] * eb]
    pallas_call x1, Pallas kernels: 39.1 us -> 43.6 us  [kernel_stats(): pl.pallas_call(functools.partial(stats_kernel, real_cols), grid=(n // TIL...]
    ppermute x6, starting transfers between devices: 12.4 us -> 9.71 us  [xor_reduce(): x = combine(x, lax.ppermute(x, axis, [(i, i ^ bit) for i in range(size)]))]
    slice x1, local copies, waits for them, and re-layouts: 2.08 us -> 0.01 us  [merge(): top = jnp.maximum(a[0], b[0])]
    unnamed x7 -> x5, local copies, waits for them, and re-layouts: 6.34 us -> 6.34 us
  transfers between devices with their start and end apart: 13 -> 13, of which waited for: 10 -> 11; matrix products, arithmetic and copies ran while one was open for 18% -> 13% of each run, Pallas kernels for 0% -> 0%
where the time goes in v7:
time: 186 us; the launch traced here: 185 us
  waiting for transfers between devices  79.7 us (43%)
  Pallas kernels  43.6 us (23%)
  starting transfers between devices  17.6 us (9%)
  other arithmetic  16.4 us (9%)
  between operations  14.2 us (8%)
  local copies, waits for them, and re-layouts  14 us (8%)
    all_gather x1, waiting for transfers between devices, body(): lax.all_gather(normed.reshape(own_rows, model_width), 'chip', axis=0, til...  52.6 us
    pallas_call x1, Pallas kernels, kernel_stats(): pl.pallas_call(functools.partial(stats_kernel, real_cols), grid=(n // TIL...  43.6 us
    ppermute x6, waiting for transfers between devices, xor_reduce(): x = combine(x, lax.ppermute(x, axis, [(i, i ^ bit) for i in range(size)]))  17.5 us
    ppermute x6, starting transfers between devices, xor_reduce(): x = combine(x, lax.ppermute(x, axis, [(i, i ^ bit) for i in range(size)]))  9.71 us
    ppermute x4, waiting for transfers between devices, xor_gather(): other = lax.ppermute(x, axis, [(i, i ^ bit) for i in range(size)])  8.44 us
    ppermute x4, starting transfers between devices, xor_gather(): other = lax.ppermute(x, axis, [(i, i ^ bit) for i in range(size)])  7.63 us
    ppermute x1, local copies, waits for them, and re-layouts, body(): other = lax.ppermute(head_weight, 'core', [(0, 1), (1, 0)])  6.43 us
    unnamed x5, local copies, waits for them, and re-layouts  6.34 us
  transfers between devices with their start and end apart: 13, of which 11 were waited for; matrix products, arithmetic and copies ran while one was open for 13% of the time, Pallas kernels for 0%

profile of v7, /device:TPU:2, one launch (start us, length us, event | category | flops | bytes accessed | tf_op | source)
XLA Modules:
  0.0 185.4 jit_solution(2668116264806843303)
XLA Ops:
  7.2 0.0 all-gather.2.cloned.1.call-start
  7.2 1.4 fusion.3
  8.6 2.3 %fusion.5 = bf16[4,48,2048]{2,1,0:T(8,128)(2,1)} fusion(bf16[4,48,2048]{2,1,0:T(8,128)(2,1)} %param.6, f32[2048]{0:T(1024)} %param.7, f32[4,48]{1,0:T(4,128)S(1)} %add_rsqrt_fusion), kind=kLoop, calls=%fused_computation.10 | loop fusion | flops 1572864 | bytes 1581824 | tf_op jit(solution)/shard_map/convert_element_type | solution.py:82
  10.9 0.0 all-gather.2.cloned.1.call-update
  11.0 0.1 collective-permute-start
  11.1 0.5 collective-permute-start.1
  11.6 3.4 %collective-permute-done.1 = s32[4,48]{1,0:T(4,128)S(1)} collective-permute-done((s32[4,48]{1,0:T(4,128)}, s32[4,48]{1,0:T(4,128)S(1)}, u32[]{:S(2)}, u32[]{:S(2)}) %collective-permute-start.1) | collective-permute-done | bytes 800 | tf_op jit(solution)/shard_map/ppermute | solution.py:56
  14.9 0.7 broadcast_select_fusion.9
  15.6 2.2 %collective-permute-start.2 = (s32[8,48]{1,0:T(8,128)S(1)}, s32[8,48]{1,0:T(8,128)S(1)}, u32[]{:S(2)}, u32[]{:S(2)}) collective-permute-start(s32[8,48]{1,0:T(8,128)S(1)} %pad_add_fusion.2), channel_id=1, source_target_pairs={{0,4},{2,6},{4,0},{6,2},{8,12},{10,14},{12,8},{14,10},{16,20},{18,... | collective-permute-start | bytes 4616 | tf_op jit(solution)/shard_map/ppermute | solution.py:56
  17.8 3.0 %collective-permute-done.2 = s32[8,48]{1,0:T(8,128)S(1)} collective-permute-done((s32[8,48]{1,0:T(8,128)S(1)}, s32[8,48]{1,0:T(8,128)S(1)}, u32[]{:S(2)}, u32[]{:S(2)}) %collective-permute-start.2) | collective-permute-done | bytes 1568 | tf_op jit(solution)/shard_map/ppermute | solution.py:56
  20.8 1.7 collective-permute-start.3
  22.5 2.1 %collective-permute-done.3 = s32[16,48]{1,0:T(8,128)S(1)} collective-permute-done((s32[16,48]{1,0:T(8,128)S(1)}, s32[16,48]{1,0:T(8,128)S(1)}, u32[]{:S(2)}, u32[]{:S(2)}) %collective-permute-start.3) | collective-permute-done | bytes 3104 | tf_op jit(solution)/shard_map/ppermute | solution.py:56
  24.6 3.3 %collective-permute-start.4 = (s32[32,48]{1,0:T(8,128)S(1)}, s32[32,48]{1,0:T(8,128)S(1)}, u32[]{:S(2)}, u32[]{:S(2)}) collective-permute-start(s32[32,48]{1,0:T(8,128)S(1)} %pad_add_fusion), channel_id=1, source_target_pairs={{0,16},{2,18},{4,20},{6,22},{8,24},{10,26},{12,28},{14,30},{16,0},... | collective-permute-start | bytes 18440 | tf_op jit(solution)/shard_map/ppermute | solution.py:56
  27.9 6.3 %copy.46 = bf16[2048,1000]{1,0:T(8,128)(2,1)} copy(bf16[2048,1000]{0,1:T(8,128)(2,1)} %param.8) | data formatting | bytes 8192000 | tf_op args[2]
  34.2 0.0 collective-permute-done.4
  34.2 0.1 sub.105.ids_ref
  34.3 0.0 collective-permute-done
  34.3 6.4 %copy.47 = bf16[2048,1000]{1,0:T(8,128)(2,1)} copy(bf16[2048,1000]{0,1:T(8,128)(2,1)} %collective-permute-done) | data formatting | bytes 8192000 | tf_op jit(solution)/shard_map/ppermute | solution.py:85
  40.8 3.8 %broadcast_select_fusion.1 = (bf16[2048,1000]{1,0:T(8,128)(2,1)S(1)}, bf16[2048,1000]{1,0:T(8,128)(2,1)S(1)}) fusion(bf16[2048,1000]{1,0:T(8,128)(2,1)} %copy.46, bf16[2048,1000]{1,0:T(8,128)(2,1)} %copy.47, pred[]{:T(512)S(6)} %eq.16), kind=kLoop, calls=%fused_computation.5 | loop fusion | flops 4096000 | bytes 16384001 | tf_op jit(solution)/shard_map/jit(_where)/select_n | solution.py:87
  44.5 6.1 %fusion.2.w_ref = bf16[2048,2048]{1,0:T(8,128)(2,1)} fusion(bf16[2048,1000]{1,0:T(8,128)(2,1)S(1)} %get-tuple-element.16, bf16[2048,1000]{1,0:T(8,128)(2,1)S(1)} %get-tuple-element.15), kind=kLoop, calls=%fused_computation.3 | loop fusion | flops 29360128 | bytes 16580608 | tf_op jit(solution)/shard_map/concatenate | solution.py:87
  50.7 0.0 copy-start.1
  50.7 0.0 copy-start
  50.7 52.6 %all-gather.2.cloned.1.call-done.rows_ref = bf16[3072,2048]{1,0:T(8,128)(2,1)} async-done(((bf16[192,2048]{1,0:T(8,128)(2,1)}), bf16[3072,2048]{1,0:T(8,128)(2,1)}) %all-gather.2.cloned.1.call-update) | async-done | bytes 12582928 | tf_op jit(solution)/shard_map/all_gather | solution.py:84
  103.3 43.6 %shard_map.85 = f32[4,3072]{1,0:T(4,128)S(1)} custom-call(bf16[3072,2048]{1,0:T(8,128)(2,1)} %all-gather.2.cloned.1.call-done.rows_ref, bf16[2048,2048]{1,0:T(8,128)(2,1)} %fusion.2.w_ref, s32[1,3072]{1,0:T(1,128)S(1)} %sub.105.ids_ref), custom_call_target="tpu_custom_call" | custom-call | flops 25769803776 | bytes 21032960 | tf_op jit(solution)/shard_map/pallas_call | solution.py:31
  146.9 0.2 reshape.100
  147.1 0.1 reshape.101
  147.2 0.6 collective-permute-start.5
  147.9 0.1 squeeze.75
  148.0 0.1 squeeze.76
  148.1 0.1 squeeze.77
  148.2 0.1 squeeze.78
  148.3 3.1 %collective-permute-done.5 = f32[4,4,768]{2,1,0:T(4,128)S(1)} collective-permute-done((f32[4,4,768]{2,1,0:T(4,128)S(1)}, f32[4,4,768]{2,1,0:T(4,128)S(1)}, u32[]{:S(2)}, u32[]{:S(2)}) %collective-permute-start.5) | collective-permute-done | bytes 49184 | tf_op jit(solution)/shard_map/ppermute | solution.py:66
  151.5 2.2 %collective-permute-start.6 = (f32[4,4,768]{2,1,0:T(4,128)S(1)}, f32[4,4,768]{2,1,0:T(4,128)S(1)}, u32[]{:S(2)}, u32[]{:S(2)}) collective-permute-start(f32[4,4,768]{2,1,0:T(4,128)S(1)} %pad_maximum_fusion), channel_id=1, source_target_pairs={{0,4},{2,6},{4,0},{6,2},{8,12},{10,14},{12,8},{14,10},{16,20},{18,... | collective-permute-start | bytes 147464 | tf_op jit(solution)/shard_map/ppermute | solution.py:66
  153.6 3.5 %collective-permute-done.6 = f32[4,4,768]{2,1,0:T(4,128)S(1)} collective-permute-done((f32[4,4,768]{2,1,0:T(4,128)S(1)}, f32[4,4,768]{2,1,0:T(4,128)S(1)}, u32[]{:S(2)}, u32[]{:S(2)}) %collective-permute-start.6) | collective-permute-done | bytes 49184 | tf_op jit(solution)/shard_map/ppermute | solution.py:66
  157.2 0.3 collective-permute-start.7
  157.5 4.2 %collective-permute-done.7 = f32[4,4,768]{2,1,0:T(4,128)S(1)} collective-permute-done((f32[4,4,768]{2,1,0:T(4,128)S(1)}, f32[4,4,768]{2,1,0:T(4,128)S(1)}, u32[]{:S(2)}, u32[]{:S(2)}) %collective-permute-start.7) | collective-permute-done | bytes 49184 | tf_op jit(solution)/shard_map/ppermute | solution.py:66
  161.8 1.9 %collective-permute-start.8 = (f32[4,4,768]{2,1,0:T(4,128)S(1)}, f32[4,4,768]{2,1,0:T(4,128)S(1)}, u32[]{:S(2)}, u32[]{:S(2)}) collective-permute-start(f32[4,4,768]{2,1,0:T(4,128)S(1)} %pad_maximum_fusion.2), channel_id=1, source_target_pairs={{0,16},{2,18},{4,20},{6,22},{8,24},{10,26},{12,28},{14,30},{16,0},... | collective-permute-start | bytes 147464 | tf_op jit(solution)/shard_map/ppermute | solution.py:66
  163.6 0.0 copy-done.1
  163.6 0.1 dynamic_slice.9
  163.7 0.1 squeeze.73
  163.8 0.1 squeeze.82
  163.9 0.1 squeeze.87
  164.0 0.1 squeeze.92
  164.0 3.4 %collective-permute-done.8 = f32[4,4,768]{2,1,0:T(4,128)S(1)} collective-permute-done((f32[4,4,768]{2,1,0:T(4,128)S(1)}, f32[4,4,768]{2,1,0:T(4,128)S(1)}, u32[]{:S(2)}, u32[]{:S(2)}) %collective-permute-start.8) | collective-permute-done | bytes 49184 | tf_op jit(solution)/shard_map/ppermute | solution.py:66
  167.4 0.2 fusion.46
  167.6 0.1 collective-permute-start.9
  167.7 1.1 collective-permute-done.9
  168.9 0.1 select_reduce_fusion
  168.9 1.6 collective-permute-start.10
  170.5 2.0 %collective-permute-done.10 = f32[16]{0:T(128)S(1)} collective-permute-done((f32[16]{0:T(128)S(1)}, f32[16]{0:T(128)S(1)}, u32[]{:S(2)}, u32[]{:S(2)}) %collective-permute-start.10) | collective-permute-done | bytes 96 | tf_op jit(solution)/shard_map/ppermute | solution.py:66
  172.6 3.1 %collective-permute-start.11 = (f32[16]{0:T(128)S(1)}, f32[16]{0:T(128)S(1)}, u32[]{:S(2)}, u32[]{:S(2)}) collective-permute-start(f32[16]{0:T(128)S(1)} %add.179), channel_id=1, source_target_pairs={{0,64},{32,96},{64,0},{96,32},{1,65},{33,97},{65,1},{97,33},{2,66}... | collective-permute-start | bytes 200 | tf_op jit(solution)/shard_map/ppermute | solution.py:66
  175.7 0.7 constant_dynamic-slice_fusion.8
  176.4 1.3 collective-permute-done.11
  177.6 0.0 copy-done
  177.6 0.2 fusion.26
  177.8 0.2 fusion.27
  178.0 0.5 maximum_divide_fusion
  (30 shorter events, 0.3 us)
Async XLA Ops:
  7.2 96.1 %all-gather.2.cloned.1.call-start = ((), (), s32[]{:S(2)}) async-start(), calls=%async_computation | async-start | bytes 13369344 | tf_op jit(solution)/shard_map/all_gather | solution.py:84
  11.0 23.4 %collective-permute-start = (bf16[2048,1000]{0,1:T(8,128)(2,1)}, bf16[2048,1000]{0,1:T(8,128)(2,1)}, u32[]{:S(2)}, u32[]{:S(2)}) collective-permute-start(bf16[2048,1000]{0,1:T(8,128)(2,1)} %param.8), channel_id=1, source_target_pairs={{0,1},{1,0},{2,3},{3,2},{4,5},{5,4},{6,7},{7,6},{8,9},{9,8},{10,11... | collective-permute-start | bytes 12288008 | tf_op jit(solution)/shard_map/ppermute | solution.py:85
  11.1 3.9 %collective-permute-start.1 = (s32[4,48]{1,0:T(4,128)}, s32[4,48]{1,0:T(4,128)S(1)}, u32[]{:S(2)}, u32[]{:S(2)}) collective-permute-start(s32[4,48]{1,0:T(4,128)} %param.9), channel_id=1, source_target_pairs={{0,2},{2,0},{4,6},{6,4},{8,10},{10,8},{12,14},{14,12},{16,18},{18,... | collective-permute-start | bytes 2312 | tf_op jit(solution)/shard_map/ppermute | solution.py:56
  15.6 5.2 %collective-permute-start.2 = (s32[8,48]{1,0:T(8,128)S(1)}, s32[8,48]{1,0:T(8,128)S(1)}, u32[]{:S(2)}, u32[]{:S(2)}) collective-permute-start(s32[8,48]{1,0:T(8,128)S(1)} %pad_add_fusion.2), channel_id=1, source_target_pairs={{0,4},{2,6},{4,0},{6,2},{8,12},{10,14},{12,8},{14,10},{16,20},{18,... | collective-permute-start | bytes 4616 | tf_op jit(solution)/shard_map/ppermute | solution.py:56
  20.8 3.7 %collective-permute-start.3 = (s32[16,48]{1,0:T(8,128)S(1)}, s32[16,48]{1,0:T(8,128)S(1)}, u32[]{:S(2)}, u32[]{:S(2)}) collective-permute-start(s32[16,48]{1,0:T(8,128)S(1)} %pad_add_fusion.1), channel_id=1, source_target_pairs={{0,8},{2,10},{4,12},{6,14},{8,0},{10,2},{12,4},{14,6},{16,24},{18,... | collective-permute-start | bytes 9224 | tf_op jit(solution)/shard_map/ppermute | solution.py:56
  24.6 9.6 %collective-permute-start.4 = (s32[32,48]{1,0:T(8,128)S(1)}, s32[32,48]{1,0:T(8,128)S(1)}, u32[]{:S(2)}, u32[]{:S(2)}) collective-permute-start(s32[32,48]{1,0:T(8,128)S(1)} %pad_add_fusion), channel_id=1, source_target_pairs={{0,16},{2,18},{4,20},{6,22},{8,24},{10,26},{12,28},{14,30},{16,0},... | collective-permute-start | bytes 18440 | tf_op jit(solution)/shard_map/ppermute | solution.py:56
  50.7 113.0 %copy-start.1 = (s32[16]{0:T(128)S(1)}, s32[16]{0:T(128)}, u32[]{:S(2)}) copy-start(s32[16]{0:T(128)} %param.10) | copy-start | bytes 196
  50.7 127.0 %copy-start = (s32[16]{0:T(128)S(1)}, s32[16]{0:T(128)}, u32[]{:S(2)}) copy-start(s32[16]{0:T(128)} %param.11) | copy-start | bytes 196
  147.2 4.2 %collective-permute-start.5 = (f32[4,4,768]{2,1,0:T(4,128)S(1)}, f32[4,4,768]{2,1,0:T(4,128)S(1)}, u32[]{:S(2)}, u32[]{:S(2)}) collective-permute-start(f32[4,4,768]{2,1,0:T(4,128)S(1)} %reshape.101), channel_id=1, source_target_pairs={{0,2},{2,0},{4,6},{6,4},{8,10},{10,8},{12,14},{14,12},{16,18},{18,... | collective-permute-start | bytes 147464 | tf_op jit(solution)/shard_map/ppermute | solution.py:66
  151.5 5.7 %collective-permute-start.6 = (f32[4,4,768]{2,1,0:T(4,128)S(1)}, f32[4,4,768]{2,1,0:T(4,128)S(1)}, u32[]{:S(2)}, u32[]{:S(2)}) collective-permute-start(f32[4,4,768]{2,1,0:T(4,128)S(1)} %pad_maximum_fusion), channel_id=1, source_target_pairs={{0,4},{2,6},{4,0},{6,2},{8,12},{10,14},{12,8},{14,10},{16,20},{18,... | collective-permute-start | bytes 147464 | tf_op jit(solution)/shard_map/ppermute | solution.py:66
  157.2 4.5 %collective-permute-start.7 = (f32[4,4,768]{2,1,0:T(4,128)S(1)}, f32[4,4,768]{2,1,0:T(4,128)S(1)}, u32[]{:S(2)}, u32[]{:S(2)}) collective-permute-start(f32[4,4,768]{2,1,0:T(4,128)S(1)} %pad_maximum_fusion.1), channel_id=1, source_target_pairs={{0,8},{2,10},{4,12},{6,14},{8,0},{10,2},{12,4},{14,6},{16,24},{18,... | collective-permute-start | bytes 147464 | tf_op jit(solution)/shard_map/ppermute | solution.py:66
  161.8 5.7 %collective-permute-start.8 = (f32[4,4,768]{2,1,0:T(4,128)S(1)}, f32[4,4,768]{2,1,0:T(4,128)S(1)}, u32[]{:S(2)}, u32[]{:S(2)}) collective-permute-start(f32[4,4,768]{2,1,0:T(4,128)S(1)} %pad_maximum_fusion.2), channel_id=1, source_target_pairs={{0,16},{2,18},{4,20},{6,22},{8,24},{10,26},{12,28},{14,30},{16,0},... | collective-permute-start | bytes 147464 | tf_op jit(solution)/shard_map/ppermute | solution.py:66
  167.6 1.2 collective-permute-start.9
  168.9 3.6 %collective-permute-start.10 = (f32[16]{0:T(128)S(1)}, f32[16]{0:T(128)S(1)}, u32[]{:S(2)}, u32[]{:S(2)}) collective-permute-start(f32[16]{0:T(128)S(1)} %select_reduce_fusion), channel_id=1, source_target_pairs={{0,32},{32,0},{64,96},{96,64},{1,33},{33,1},{65,97},{97,65},{2,34}... | collective-permute-start | bytes 200 | tf_op jit(solution)/shard_map/ppermute | solution.py:66
  172.6 5.1 %collective-permute-start.11 = (f32[16]{0:T(128)S(1)}, f32[16]{0:T(128)S(1)}, u32[]{:S(2)}, u32[]{:S(2)}) collective-permute-start(f32[16]{0:T(128)S(1)} %add.179), channel_id=1, source_target_pairs={{0,64},{32,96},{64,0},{96,32},{1,65},{33,97},{65,1},{97,33},{2,66}... | collective-permute-start | bytes 200 | tf_op jit(solution)/shard_map/ppermute | solution.py:66
Sparse Core Ops, SparseCore 0:
  11.1 92.1 all-gather.1

commit v8 on v7

--- a/solution.py
+++ b/solution.py
@@ -10,7 +10,7 @@
 from jax.sharding import PartitionSpec as P
 
 norm_eps = 1e-06
-TILE = 256
+TILE = 512
 
 
 def stats_kernel(real_cols, rows_ref, w_ref, ids_ref, out_ref):

time: 186 us -> 184 us (0.989)
  Pallas kernels: 43.6 us -> 41.5 us
    pallas_call x1, Pallas kernels: 43.6 us -> 41.5 us  [kernel_stats(): pl.pallas_call(functools.partial(stats_kernel, real_cols), grid=(n // TIL...]
  transfers between devices with their start and end apart: 13 -> 13, of which waited for: 11 -> 11; matrix products, arithmetic and copies ran while one was open for 13% -> 14% of each run, Pallas kernels for 0% -> 0%
where the time goes in v8:
time: 184 us; the launch traced here: 183 us
  waiting for transfers between devices  79.7 us (43%)
  Pallas kernels  41.5 us (23%)
  starting transfers between devices  17.5 us (10%)
  other arithmetic  16.4 us (9%)
  between operations  14.2 us (8%)
  local copies, waits for them, and re-layouts  14 us (8%)
    all_gather x1, waiting for transfers between devices, body(): lax.all_gather(normed.reshape(own_rows, model_width), 'chip', axis=0, til...  52.6 us
    pallas_call x1, Pallas kernels, kernel_stats(): pl.pallas_call(functools.partial(stats_kernel, real_cols), grid=(n // TIL...  41.5 us
    ppermute x6, waiting for transfers between devices, xor_reduce(): x = combine(x, lax.ppermute(x, axis, [(i, i ^ bit) for i in range(size)]))  17.5 us
    ppermute x6, starting transfers between devices, xor_reduce(): x = combine(x, lax.ppermute(x, axis, [(i, i ^ bit) for i in range(size)]))  9.7 us
    ppermute x4, waiting for transfers between devices, xor_gather(): other = lax.ppermute(x, axis, [(i, i ^ bit) for i in range(size)])  8.44 us
    ppermute x4, starting transfers between devices, xor_gather(): other = lax.ppermute(x, axis, [(i, i ^ bit) for i in range(size)])  7.63 us
    ppermute x1, local copies, waits for them, and re-layouts, body(): other = lax.ppermute(head_weight, 'core', [(0, 1), (1, 0)])  6.43 us
    unnamed x5, local copies, waits for them, and re-layouts  6.34 us
  transfers between devices with their start and end apart: 13, of which 11 were waited for; matrix products, arithmetic and copies ran while one was open for 14% of the time, Pallas kernels for 0%

profile of v8, /device:TPU:2, one launch (start us, length us, event | category | flops | bytes accessed | tf_op | source)
XLA Modules:
  0.0 183.3 jit_solution(17240004034429981515)
XLA Ops:
  7.2 0.0 all-gather.2.cloned.1.call-start
  7.2 1.4 fusion.3
  8.6 2.3 %fusion.5 = bf16[4,48,2048]{2,1,0:T(8,128)(2,1)} fusion(bf16[4,48,2048]{2,1,0:T(8,128)(2,1)} %param.6, f32[2048]{0:T(1024)} %param.7, f32[4,48]{1,0:T(4,128)S(1)} %add_rsqrt_fusion), kind=kLoop, calls=%fused_computation.10 | loop fusion | flops 1572864 | bytes 1581824 | tf_op jit(solution)/shard_map/convert_element_type | solution.py:82
  10.9 0.0 all-gather.2.cloned.1.call-update
  11.0 0.1 collective-permute-start
  11.1 0.5 collective-permute-start.1
  11.6 3.4 %collective-permute-done.1 = s32[4,48]{1,0:T(4,128)S(1)} collective-permute-done((s32[4,48]{1,0:T(4,128)}, s32[4,48]{1,0:T(4,128)S(1)}, u32[]{:S(2)}, u32[]{:S(2)}) %collective-permute-start.1) | collective-permute-done | bytes 800 | tf_op jit(solution)/shard_map/ppermute | solution.py:56
  14.9 0.7 broadcast_select_fusion.9
  15.6 2.2 %collective-permute-start.2 = (s32[8,48]{1,0:T(8,128)S(1)}, s32[8,48]{1,0:T(8,128)S(1)}, u32[]{:S(2)}, u32[]{:S(2)}) collective-permute-start(s32[8,48]{1,0:T(8,128)S(1)} %pad_add_fusion.2), channel_id=1, source_target_pairs={{0,4},{2,6},{4,0},{6,2},{8,12},{10,14},{12,8},{14,10},{16,20},{18,... | collective-permute-start | bytes 4616 | tf_op jit(solution)/shard_map/ppermute | solution.py:56
  17.8 3.0 %collective-permute-done.2 = s32[8,48]{1,0:T(8,128)S(1)} collective-permute-done((s32[8,48]{1,0:T(8,128)S(1)}, s32[8,48]{1,0:T(8,128)S(1)}, u32[]{:S(2)}, u32[]{:S(2)}) %collective-permute-start.2) | collective-permute-done | bytes 1568 | tf_op jit(solution)/shard_map/ppermute | solution.py:56
  20.8 1.7 collective-permute-start.3
  22.5 2.1 %collective-permute-done.3 = s32[16,48]{1,0:T(8,128)S(1)} collective-permute-done((s32[16,48]{1,0:T(8,128)S(1)}, s32[16,48]{1,0:T(8,128)S(1)}, u32[]{:S(2)}, u32[]{:S(2)}) %collective-permute-start.3) | collective-permute-done | bytes 3104 | tf_op jit(solution)/shard_map/ppermute | solution.py:56
  24.6 3.3 %collective-permute-start.4 = (s32[32,48]{1,0:T(8,128)S(1)}, s32[32,48]{1,0:T(8,128)S(1)}, u32[]{:S(2)}, u32[]{:S(2)}) collective-permute-start(s32[32,48]{1,0:T(8,128)S(1)} %pad_add_fusion), channel_id=1, source_target_pairs={{0,16},{2,18},{4,20},{6,22},{8,24},{10,26},{12,28},{14,30},{16,0},... | collective-permute-start | bytes 18440 | tf_op jit(solution)/shard_map/ppermute | solution.py:56
  27.9 6.3 %copy.46 = bf16[2048,1000]{1,0:T(8,128)(2,1)} copy(bf16[2048,1000]{0,1:T(8,128)(2,1)} %param.8) | data formatting | bytes 8192000 | tf_op args[2]
  34.2 0.0 collective-permute-done.4
  34.2 0.1 sub.105.ids_ref
  34.3 0.0 collective-permute-done
  34.3 6.4 %copy.47 = bf16[2048,1000]{1,0:T(8,128)(2,1)} copy(bf16[2048,1000]{0,1:T(8,128)(2,1)} %collective-permute-done) | data formatting | bytes 8192000 | tf_op jit(solution)/shard_map/ppermute | solution.py:85
  40.8 3.8 %broadcast_select_fusion.1 = (bf16[2048,1000]{1,0:T(8,128)(2,1)S(1)}, bf16[2048,1000]{1,0:T(8,128)(2,1)S(1)}) fusion(bf16[2048,1000]{1,0:T(8,128)(2,1)} %copy.46, bf16[2048,1000]{1,0:T(8,128)(2,1)} %copy.47, pred[]{:T(512)S(6)} %eq.16), kind=kLoop, calls=%fused_computation.5 | loop fusion | flops 4096000 | bytes 16384001 | tf_op jit(solution)/shard_map/jit(_where)/select_n | solution.py:87
  44.5 6.1 %fusion.2.w_ref = bf16[2048,2048]{1,0:T(8,128)(2,1)} fusion(bf16[2048,1000]{1,0:T(8,128)(2,1)S(1)} %get-tuple-element.16, bf16[2048,1000]{1,0:T(8,128)(2,1)S(1)} %get-tuple-element.15), kind=kLoop, calls=%fused_computation.3 | loop fusion | flops 29360128 | bytes 16580608 | tf_op jit(solution)/shard_map/concatenate | solution.py:87
  50.7 0.0 copy-start.1
  50.7 0.0 copy-start
  50.7 52.6 %all-gather.2.cloned.1.call-done.rows_ref = bf16[3072,2048]{1,0:T(8,128)(2,1)} async-done(((bf16[192,2048]{1,0:T(8,128)(2,1)}), bf16[3072,2048]{1,0:T(8,128)(2,1)}) %all-gather.2.cloned.1.call-update) | async-done | bytes 12582928 | tf_op jit(solution)/shard_map/all_gather | solution.py:84
  103.3 41.5 %shard_map.85 = f32[4,3072]{1,0:T(4,128)S(1)} custom-call(bf16[3072,2048]{1,0:T(8,128)(2,1)} %all-gather.2.cloned.1.call-done.rows_ref, bf16[2048,2048]{1,0:T(8,128)(2,1)} %fusion.2.w_ref, s32[1,3072]{1,0:T(1,128)S(1)} %sub.105.ids_ref), custom_call_target="tpu_custom_call" | custom-call | flops 25769803776 | bytes 21032960 | tf_op jit(solution)/shard_map/pallas_call | solution.py:31
  144.8 0.2 reshape.100
  145.0 0.1 reshape.101
  145.1 0.6 collective-permute-start.5
  145.8 0.1 squeeze.75
  145.9 0.1 squeeze.76
  146.0 0.1 squeeze.77
  146.1 0.1 squeeze.78
  146.2 3.1 %collective-permute-done.5 = f32[4,4,768]{2,1,0:T(4,128)S(1)} collective-permute-done((f32[4,4,768]{2,1,0:T(4,128)S(1)}, f32[4,4,768]{2,1,0:T(4,128)S(1)}, u32[]{:S(2)}, u32[]{:S(2)}) %collective-permute-start.5) | collective-permute-done | bytes 49184 | tf_op jit(solution)/shard_map/ppermute | solution.py:66
  149.4 2.2 %collective-permute-start.6 = (f32[4,4,768]{2,1,0:T(4,128)S(1)}, f32[4,4,768]{2,1,0:T(4,128)S(1)}, u32[]{:S(2)}, u32[]{:S(2)}) collective-permute-start(f32[4,4,768]{2,1,0:T(4,128)S(1)} %pad_maximum_fusion), channel_id=1, source_target_pairs={{0,4},{2,6},{4,0},{6,2},{8,12},{10,14},{12,8},{14,10},{16,20},{18,... | collective-permute-start | bytes 147464 | tf_op jit(solution)/shard_map/ppermute | solution.py:66
  151.5 3.5 %collective-permute-done.6 = f32[4,4,768]{2,1,0:T(4,128)S(1)} collective-permute-done((f32[4,4,768]{2,1,0:T(4,128)S(1)}, f32[4,4,768]{2,1,0:T(4,128)S(1)}, u32[]{:S(2)}, u32[]{:S(2)}) %collective-permute-start.6) | collective-permute-done | bytes 49184 | tf_op jit(solution)/shard_map/ppermute | solution.py:66
  155.1 0.3 collective-permute-start.7
  155.4 4.2 %collective-permute-done.7 = f32[4,4,768]{2,1,0:T(4,128)S(1)} collective-permute-done((f32[4,4,768]{2,1,0:T(4,128)S(1)}, f32[4,4,768]{2,1,0:T(4,128)S(1)}, u32[]{:S(2)}, u32[]{:S(2)}) %collective-permute-start.7) | collective-permute-done | bytes 49184 | tf_op jit(solution)/shard_map/ppermute | solution.py:66
  159.7 1.9 %collective-permute-start.8 = (f32[4,4,768]{2,1,0:T(4,128)S(1)}, f32[4,4,768]{2,1,0:T(4,128)S(1)}, u32[]{:S(2)}, u32[]{:S(2)}) collective-permute-start(f32[4,4,768]{2,1,0:T(4,128)S(1)} %pad_maximum_fusion.2), channel_id=1, source_target_pairs={{0,16},{2,18},{4,20},{6,22},{8,24},{10,26},{12,28},{14,30},{16,0},... | collective-permute-start | bytes 147464 | tf_op jit(solution)/shard_map/ppermute | solution.py:66
  161.5 0.0 copy-done.1
  161.5 0.1 dynamic_slice.9
  161.6 0.1 squeeze.73
  161.7 0.1 squeeze.82
  161.8 0.1 squeeze.87
  161.9 0.1 squeeze.92
  162.0 3.4 %collective-permute-done.8 = f32[4,4,768]{2,1,0:T(4,128)S(1)} collective-permute-done((f32[4,4,768]{2,1,0:T(4,128)S(1)}, f32[4,4,768]{2,1,0:T(4,128)S(1)}, u32[]{:S(2)}, u32[]{:S(2)}) %collective-permute-start.8) | collective-permute-done | bytes 49184 | tf_op jit(solution)/shard_map/ppermute | solution.py:66
  165.3 0.2 fusion.46
  165.5 0.1 collective-permute-start.9
  165.6 1.1 collective-permute-done.9
  166.7 0.1 select_reduce_fusion
  166.8 1.6 collective-permute-start.10
  168.4 2.0 %collective-permute-done.10 = f32[16]{0:T(128)S(1)} collective-permute-done((f32[16]{0:T(128)S(1)}, f32[16]{0:T(128)S(1)}, u32[]{:S(2)}, u32[]{:S(2)}) %collective-permute-start.10) | collective-permute-done | bytes 96 | tf_op jit(solution)/shard_map/ppermute | solution.py:66
  170.4 3.1 %collective-permute-start.11 = (f32[16]{0:T(128)S(1)}, f32[16]{0:T(128)S(1)}, u32[]{:S(2)}, u32[]{:S(2)}) collective-permute-start(f32[16]{0:T(128)S(1)} %add.179), channel_id=1, source_target_pairs={{0,64},{32,96},{64,0},{96,32},{1,65},{33,97},{65,1},{97,33},{2,66}... | collective-permute-start | bytes 200 | tf_op jit(solution)/shard_map/ppermute | solution.py:66
  173.6 0.7 constant_dynamic-slice_fusion.8
  174.3 1.3 collective-permute-done.11
  175.5 0.0 copy-done
  175.5 0.2 fusion.26
  175.7 0.2 fusion.27
  175.9 0.5 maximum_divide_fusion
  (30 shorter events, 0.3 us)
Async XLA Ops:
  7.2 96.1 %all-gather.2.cloned.1.call-start = ((), (), s32[]{:S(2)}) async-start(), calls=%async_computation | async-start | bytes 13369344 | tf_op jit(solution)/shard_map/all_gather | solution.py:84
  11.0 23.4 %collective-permute-start = (bf16[2048,1000]{0,1:T(8,128)(2,1)}, bf16[2048,1000]{0,1:T(8,128)(2,1)}, u32[]{:S(2)}, u32[]{:S(2)}) collective-permute-start(bf16[2048,1000]{0,1:T(8,128)(2,1)} %param.8), channel_id=1, source_target_pairs={{0,1},{1,0},{2,3},{3,2},{4,5},{5,4},{6,7},{7,6},{8,9},{9,8},{10,11... | collective-permute-start | bytes 12288008 | tf_op jit(solution)/shard_map/ppermute | solution.py:85
  11.1 3.9 %collective-permute-start.1 = (s32[4,48]{1,0:T(4,128)}, s32[4,48]{1,0:T(4,128)S(1)}, u32[]{:S(2)}, u32[]{:S(2)}) collective-permute-start(s32[4,48]{1,0:T(4,128)} %param.9), channel_id=1, source_target_pairs={{0,2},{2,0},{4,6},{6,4},{8,10},{10,8},{12,14},{14,12},{16,18},{18,... | collective-permute-start | bytes 2312 | tf_op jit(solution)/shard_map/ppermute | solution.py:56
  15.6 5.2 %collective-permute-start.2 = (s32[8,48]{1,0:T(8,128)S(1)}, s32[8,48]{1,0:T(8,128)S(1)}, u32[]{:S(2)}, u32[]{:S(2)}) collective-permute-start(s32[8,48]{1,0:T(8,128)S(1)} %pad_add_fusion.2), channel_id=1, source_target_pairs={{0,4},{2,6},{4,0},{6,2},{8,12},{10,14},{12,8},{14,10},{16,20},{18,... | collective-permute-start | bytes 4616 | tf_op jit(solution)/shard_map/ppermute | solution.py:56
  20.8 3.7 %collective-permute-start.3 = (s32[16,48]{1,0:T(8,128)S(1)}, s32[16,48]{1,0:T(8,128)S(1)}, u32[]{:S(2)}, u32[]{:S(2)}) collective-permute-start(s32[16,48]{1,0:T(8,128)S(1)} %pad_add_fusion.1), channel_id=1, source_target_pairs={{0,8},{2,10},{4,12},{6,14},{8,0},{10,2},{12,4},{14,6},{16,24},{18,... | collective-permute-start | bytes 9224 | tf_op jit(solution)/shard_map/ppermute | solution.py:56
  24.6 9.6 %collective-permute-start.4 = (s32[32,48]{1,0:T(8,128)S(1)}, s32[32,48]{1,0:T(8,128)S(1)}, u32[]{:S(2)}, u32[]{:S(2)}) collective-permute-start(s32[32,48]{1,0:T(8,128)S(1)} %pad_add_fusion), channel_id=1, source_target_pairs={{0,16},{2,18},{4,20},{6,22},{8,24},{10,26},{12,28},{14,30},{16,0},... | collective-permute-start | bytes 18440 | tf_op jit(solution)/shard_map/ppermute | solution.py:56
  50.7 110.9 %copy-start.1 = (s32[16]{0:T(128)S(1)}, s32[16]{0:T(128)}, u32[]{:S(2)}) copy-start(s32[16]{0:T(128)} %param.10) | copy-start | bytes 196
  50.7 124.9 %copy-start = (s32[16]{0:T(128)S(1)}, s32[16]{0:T(128)}, u32[]{:S(2)}) copy-start(s32[16]{0:T(128)} %param.11) | copy-start | bytes 196
  145.1 4.2 %collective-permute-start.5 = (f32[4,4,768]{2,1,0:T(4,128)S(1)}, f32[4,4,768]{2,1,0:T(4,128)S(1)}, u32[]{:S(2)}, u32[]{:S(2)}) collective-permute-start(f32[4,4,768]{2,1,0:T(4,128)S(1)} %reshape.101), channel_id=1, source_target_pairs={{0,2},{2,0},{4,6},{6,4},{8,10},{10,8},{12,14},{14,12},{16,18},{18,... | collective-permute-start | bytes 147464 | tf_op jit(solution)/shard_map/ppermute | solution.py:66
  149.4 5.7 %collective-permute-start.6 = (f32[4,4,768]{2,1,0:T(4,128)S(1)}, f32[4,4,768]{2,1,0:T(4,128)S(1)}, u32[]{:S(2)}, u32[]{:S(2)}) collective-permute-start(f32[4,4,768]{2,1,0:T(4,128)S(1)} %pad_maximum_fusion), channel_id=1, source_target_pairs={{0,4},{2,6},{4,0},{6,2},{8,12},{10,14},{12,8},{14,10},{16,20},{18,... | collective-permute-start | bytes 147464 | tf_op jit(solution)/shard_map/ppermute | solution.py:66
  155.1 4.5 %collective-permute-start.7 = (f32[4,4,768]{2,1,0:T(4,128)S(1)}, f32[4,4,768]{2,1,0:T(4,128)S(1)}, u32[]{:S(2)}, u32[]{:S(2)}) collective-permute-start(f32[4,4,768]{2,1,0:T(4,128)S(1)} %pad_maximum_fusion.1), channel_id=1, source_target_pairs={{0,8},{2,10},{4,12},{6,14},{8,0},{10,2},{12,4},{14,6},{16,24},{18,... | collective-permute-start | bytes 147464 | tf_op jit(solution)/shard_map/ppermute | solution.py:66
  159.7 5.7 %collective-permute-start.8 = (f32[4,4,768]{2,1,0:T(4,128)S(1)}, f32[4,4,768]{2,1,0:T(4,128)S(1)}, u32[]{:S(2)}, u32[]{:S(2)}) collective-permute-start(f32[4,4,768]{2,1,0:T(4,128)S(1)} %pad_maximum_fusion.2), channel_id=1, source_target_pairs={{0,16},{2,18},{4,20},{6,22},{8,24},{10,26},{12,28},{14,30},{16,0},... | collective-permute-start | bytes 147464 | tf_op jit(solution)/shard_map/ppermute | solution.py:66
  165.5 1.2 collective-permute-start.9
  166.8 3.6 %collective-permute-start.10 = (f32[16]{0:T(128)S(1)}, f32[16]{0:T(128)S(1)}, u32[]{:S(2)}, u32[]{:S(2)}) collective-permute-start(f32[16]{0:T(128)S(1)} %select_reduce_fusion), channel_id=1, source_target_pairs={{0,32},{32,0},{64,96},{96,64},{1,33},{33,1},{65,97},{97,65},{2,34}... | collective-permute-start | bytes 200 | tf_op jit(solution)/shard_map/ppermute | solution.py:66
  170.4 5.1 %collective-permute-start.11 = (f32[16]{0:T(128)S(1)}, f32[16]{0:T(128)S(1)}, u32[]{:S(2)}, u32[]{:S(2)}) collective-permute-start(f32[16]{0:T(128)S(1)} %add.179), channel_id=1, source_target_pairs={{0,64},{32,96},{64,0},{96,32},{1,65},{33,97},{65,1},{97,33},{2,66}... | collective-permute-start | bytes 200 | tf_op jit(solution)/shard_map/ppermute | solution.py:66
Sparse Core Ops, SparseCore 0:
  11.1 92.1 all-gather.1

commit v9 on v8

--- a/solution.py
+++ b/solution.py
@@ -10,7 +10,7 @@
 from jax.sharding import PartitionSpec as P
 
 norm_eps = 1e-06
-TILE = 512
+TILE = 1024
 
 
 def stats_kernel(real_cols, rows_ref, w_ref, ids_ref, out_ref):
@@ -38,7 +38,7 @@
         ],
         out_specs=pl.BlockSpec((4, TILE), lambda i: (0, i)),
         out_shape=jax.ShapeDtypeStruct((4, n), jnp.float32),
-        compiler_params=pltpu.CompilerParams(vmem_limit_bytes=48 * 1024 * 1024),
+        compiler_params=pltpu.CompilerParams(vmem_limit_bytes=60 * 1024 * 1024),
         cost_estimate=pl.CostEstimate(flops=2 * n * d * c, transcendentals=n * c, bytes_accessed=2 * (n * d + d * c) + 20 * n),
     )(rows, weight, local_ids)
 

time: 184 us -> 185 us (level)
  no operation moved by 1% of the time
where the time goes in v9:
time: 185 us; the launch traced here: 184 us
  waiting for transfers between devices  79.2 us (43%)
  Pallas kernels  41.4 us (22%)
  starting transfers between devices  17.8 us (10%)
  other arithmetic  16.4 us (9%)
  local copies, waits for them, and re-layouts  15.3 us (8%)
  between operations  14.2 us (8%)
    all_gather x1, waiting for transfers between devices, body(): lax.all_gather(normed.reshape(own_rows, model_width), 'chip', axis=0, til...  52.2 us
    pallas_call x1, Pallas kernels, kernel_stats(): pl.pallas_call(functools.partial(stats_kernel, real_cols), grid=(n // TIL...  41.4 us
    ppermute x6, waiting for transfers between devices, xor_reduce(): x = combine(x, lax.ppermute(x, axis, [(i, i ^ bit) for i in range(size)]))  17.5 us
    ppermute x6, starting transfers between devices, xor_reduce(): x = combine(x, lax.ppermute(x, axis, [(i, i ^ bit) for i in range(size)]))  9.93 us
    ppermute x4, waiting for transfers between devices, xor_gather(): other = lax.ppermute(x, axis, [(i, i ^ bit) for i in range(size)])  8.44 us
    ppermute x4, starting transfers between devices, xor_gather(): other = lax.ppermute(x, axis, [(i, i ^ bit) for i in range(size)])  7.63 us
    ppermute x1, local copies, waits for them, and re-layouts, body(): other = lax.ppermute(head_weight, 'core', [(0, 1), (1, 0)])  6.39 us
    unnamed x5, local copies, waits for them, and re-layouts  6.34 us
  transfers between devices with their start and end apart: 13, of which 11 were waited for; matrix products, arithmetic and copies ran while one was open for 14% of the time, Pallas kernels for 0%

profile of v9, /device:TPU:2, one launch (start us, length us, event | category | flops | bytes accessed | tf_op | source)
XLA Modules:
  0.0 184.2 jit_solution(16125099627622496693)
XLA Ops:
  7.2 0.0 all-gather.2.cloned.1.call-start
  7.2 1.4 fusion.3
  8.6 2.3 %fusion.5 = bf16[4,48,2048]{2,1,0:T(8,128)(2,1)} fusion(bf16[4,48,2048]{2,1,0:T(8,128)(2,1)} %param.6, f32[2048]{0:T(1024)} %param.7, f32[4,48]{1,0:T(4,128)S(1)} %add_rsqrt_fusion), kind=kLoop, calls=%fused_computation.10 | loop fusion | flops 1572864 | bytes 1581824 | tf_op jit(solution)/shard_map/convert_element_type | solution.py:82
  10.9 0.0 all-gather.2.cloned.1.call-update
  11.0 0.1 collective-permute-start
  11.1 0.5 collective-permute-start.1
  11.6 3.4 %collective-permute-done.1 = s32[4,48]{1,0:T(4,128)S(1)} collective-permute-done((s32[4,48]{1,0:T(4,128)}, s32[4,48]{1,0:T(4,128)S(1)}, u32[]{:S(2)}, u32[]{:S(2)}) %collective-permute-start.1) | collective-permute-done | bytes 800 | tf_op jit(solution)/shard_map/ppermute | solution.py:56
  14.9 0.7 broadcast_select_fusion.9
  15.6 2.2 %collective-permute-start.2 = (s32[8,48]{1,0:T(8,128)S(1)}, s32[8,48]{1,0:T(8,128)S(1)}, u32[]{:S(2)}, u32[]{:S(2)}) collective-permute-start(s32[8,48]{1,0:T(8,128)S(1)} %pad_add_fusion.2), channel_id=1, source_target_pairs={{0,4},{2,6},{4,0},{6,2},{8,12},{10,14},{12,8},{14,10},{16,20},{18,... | collective-permute-start | bytes 4616 | tf_op jit(solution)/shard_map/ppermute | solution.py:56
  17.8 3.0 %collective-permute-done.2 = s32[8,48]{1,0:T(8,128)S(1)} collective-permute-done((s32[8,48]{1,0:T(8,128)S(1)}, s32[8,48]{1,0:T(8,128)S(1)}, u32[]{:S(2)}, u32[]{:S(2)}) %collective-permute-start.2) | collective-permute-done | bytes 1568 | tf_op jit(solution)/shard_map/ppermute | solution.py:56
  20.8 1.7 collective-permute-start.3
  22.5 2.1 %collective-permute-done.3 = s32[16,48]{1,0:T(8,128)S(1)} collective-permute-done((s32[16,48]{1,0:T(8,128)S(1)}, s32[16,48]{1,0:T(8,128)S(1)}, u32[]{:S(2)}, u32[]{:S(2)}) %collective-permute-start.3) | collective-permute-done | bytes 3104 | tf_op jit(solution)/shard_map/ppermute | solution.py:56
  24.6 3.3 %collective-permute-start.4 = (s32[32,48]{1,0:T(8,128)S(1)}, s32[32,48]{1,0:T(8,128)S(1)}, u32[]{:S(2)}, u32[]{:S(2)}) collective-permute-start(s32[32,48]{1,0:T(8,128)S(1)} %pad_add_fusion), channel_id=1, source_target_pairs={{0,16},{2,18},{4,20},{6,22},{8,24},{10,26},{12,28},{14,30},{16,0},... | collective-permute-start | bytes 18440 | tf_op jit(solution)/shard_map/ppermute | solution.py:56
  27.9 6.3 %copy.46 = bf16[2048,1000]{1,0:T(8,128)(2,1)} copy(bf16[2048,1000]{0,1:T(8,128)(2,1)} %param.8) | data formatting | bytes 8192000 | tf_op args[2]
  34.2 0.0 collective-permute-done.4
  34.2 0.7 sub.105.ids_ref
  34.9 0.0 collective-permute-done
  34.9 6.4 %copy.47 = bf16[2048,1000]{1,0:T(8,128)(2,1)} copy(bf16[2048,1000]{0,1:T(8,128)(2,1)} %collective-permute-done) | data formatting | bytes 8192000 | tf_op jit(solution)/shard_map/ppermute | solution.py:85
  41.3 3.8 %broadcast_select_fusion.1 = (bf16[2048,1000]{1,0:T(8,128)(2,1)S(1)}, bf16[2048,1000]{1,0:T(8,128)(2,1)S(1)}) fusion(bf16[2048,1000]{1,0:T(8,128)(2,1)} %copy.46, bf16[2048,1000]{1,0:T(8,128)(2,1)} %copy.47, pred[]{:T(512)S(6)} %eq.16), kind=kLoop, calls=%fused_computation.5 | loop fusion | flops 4096000 | bytes 16384001 | tf_op jit(solution)/shard_map/jit(_where)/select_n | solution.py:87
  45.1 6.1 %fusion.2.w_ref = bf16[2048,2048]{1,0:T(8,128)(2,1)} fusion(bf16[2048,1000]{1,0:T(8,128)(2,1)S(1)} %get-tuple-element.16, bf16[2048,1000]{1,0:T(8,128)(2,1)S(1)} %get-tuple-element.15), kind=kLoop, calls=%fused_computation.3 | loop fusion | flops 29360128 | bytes 16580608 | tf_op jit(solution)/shard_map/concatenate | solution.py:87
  51.1 0.0 copy-start.1
  51.1 0.0 copy-start
  51.1 52.2 %all-gather.2.cloned.1.call-done.rows_ref = bf16[3072,2048]{1,0:T(8,128)(2,1)} async-done(((bf16[192,2048]{1,0:T(8,128)(2,1)}), bf16[3072,2048]{1,0:T(8,128)(2,1)}) %all-gather.2.cloned.1.call-update) | async-done | bytes 12582928 | tf_op jit(solution)/shard_map/all_gather | solution.py:84
  103.3 41.4 %shard_map.85 = f32[4,3072]{1,0:T(4,128)} custom-call(bf16[3072,2048]{1,0:T(8,128)(2,1)} %all-gather.2.cloned.1.call-done.rows_ref, bf16[2048,2048]{1,0:T(8,128)(2,1)} %fusion.2.w_ref, s32[1,3072]{1,0:T(1,128)} %sub.105.ids_ref), custom_call_target="tpu_custom_call" | custom-call | flops 25769803776 | bytes 21032960 | tf_op jit(solution)/shard_map/pallas_call | solution.py:31
  144.7 1.0 reshape.100
  145.7 0.1 reshape.101
  145.8 0.9 collective-permute-start.5
  146.7 0.1 squeeze.75
  146.8 0.1 squeeze.76
  146.9 0.1 squeeze.77
  147.0 0.1 squeeze.78
  147.1 3.1 %collective-permute-done.5 = f32[4,4,768]{2,1,0:T(4,128)S(1)} collective-permute-done((f32[4,4,768]{2,1,0:T(4,128)S(1)}, f32[4,4,768]{2,1,0:T(4,128)S(1)}, u32[]{:S(2)}, u32[]{:S(2)}) %collective-permute-start.5) | collective-permute-done | bytes 49184 | tf_op jit(solution)/shard_map/ppermute | solution.py:66
  150.3 2.2 %collective-permute-start.6 = (f32[4,4,768]{2,1,0:T(4,128)S(1)}, f32[4,4,768]{2,1,0:T(4,128)S(1)}, u32[]{:S(2)}, u32[]{:S(2)}) collective-permute-start(f32[4,4,768]{2,1,0:T(4,128)S(1)} %pad_maximum_fusion), channel_id=1, source_target_pairs={{0,4},{2,6},{4,0},{6,2},{8,12},{10,14},{12,8},{14,10},{16,20},{18,... | collective-permute-start | bytes 147464 | tf_op jit(solution)/shard_map/ppermute | solution.py:66
  152.4 3.5 %collective-permute-done.6 = f32[4,4,768]{2,1,0:T(4,128)S(1)} collective-permute-done((f32[4,4,768]{2,1,0:T(4,128)S(1)}, f32[4,4,768]{2,1,0:T(4,128)S(1)}, u32[]{:S(2)}, u32[]{:S(2)}) %collective-permute-start.6) | collective-permute-done | bytes 49184 | tf_op jit(solution)/shard_map/ppermute | solution.py:66
  156.0 0.3 collective-permute-start.7
  156.3 4.2 %collective-permute-done.7 = f32[4,4,768]{2,1,0:T(4,128)S(1)} collective-permute-done((f32[4,4,768]{2,1,0:T(4,128)S(1)}, f32[4,4,768]{2,1,0:T(4,128)S(1)}, u32[]{:S(2)}, u32[]{:S(2)}) %collective-permute-start.7) | collective-permute-done | bytes 49184 | tf_op jit(solution)/shard_map/ppermute | solution.py:66
  160.6 1.9 %collective-permute-start.8 = (f32[4,4,768]{2,1,0:T(4,128)S(1)}, f32[4,4,768]{2,1,0:T(4,128)S(1)}, u32[]{:S(2)}, u32[]{:S(2)}) collective-permute-start(f32[4,4,768]{2,1,0:T(4,128)S(1)} %pad_maximum_fusion.2), channel_id=1, source_target_pairs={{0,16},{2,18},{4,20},{6,22},{8,24},{10,26},{12,28},{14,30},{16,0},... | collective-permute-start | bytes 147464 | tf_op jit(solution)/shard_map/ppermute | solution.py:66
  162.4 0.0 copy-done.1
  162.4 0.1 dynamic_slice.9
  162.5 0.1 squeeze.73
  162.6 0.1 squeeze.82
  162.7 0.1 squeeze.87
  162.8 0.1 squeeze.92
  162.9 3.4 %collective-permute-done.8 = f32[4,4,768]{2,1,0:T(4,128)S(1)} collective-permute-done((f32[4,4,768]{2,1,0:T(4,128)S(1)}, f32[4,4,768]{2,1,0:T(4,128)S(1)}, u32[]{:S(2)}, u32[]{:S(2)}) %collective-permute-start.8) | collective-permute-done | bytes 49184 | tf_op jit(solution)/shard_map/ppermute | solution.py:66
  166.2 0.2 fusion.46
  166.4 0.1 collective-permute-start.9
  166.6 1.1 collective-permute-done.9
  167.7 0.1 select_reduce_fusion
  167.8 1.6 collective-permute-start.10
  169.3 2.0 %collective-permute-done.10 = f32[16]{0:T(128)S(1)} collective-permute-done((f32[16]{0:T(128)S(1)}, f32[16]{0:T(128)S(1)}, u32[]{:S(2)}, u32[]{:S(2)}) %collective-permute-start.10) | collective-permute-done | bytes 96 | tf_op jit(solution)/shard_map/ppermute | solution.py:66
  171.4 3.1 %collective-permute-start.11 = (f32[16]{0:T(128)S(1)}, f32[16]{0:T(128)S(1)}, u32[]{:S(2)}, u32[]{:S(2)}) collective-permute-start(f32[16]{0:T(128)S(1)} %add.179), channel_id=1, source_target_pairs={{0,64},{32,96},{64,0},{96,32},{1,65},{33,97},{65,1},{97,33},{2,66}... | collective-permute-start | bytes 200 | tf_op jit(solution)/shard_map/ppermute | solution.py:66
  174.5 0.7 constant_dynamic-slice_fusion.8
  175.2 1.3 collective-permute-done.11
  176.4 0.0 copy-done
  176.4 0.2 fusion.26
  176.6 0.2 fusion.27
  176.8 0.5 maximum_divide_fusion
  (30 shorter events, 0.3 us)
Async XLA Ops:
  7.2 96.1 %all-gather.2.cloned.1.call-start = ((), (), s32[]{:S(2)}) async-start(), calls=%async_computation | async-start | bytes 13369344 | tf_op jit(solution)/shard_map/all_gather | solution.py:84
  11.0 24.0 %collective-permute-start = (bf16[2048,1000]{0,1:T(8,128)(2,1)}, bf16[2048,1000]{0,1:T(8,128)(2,1)}, u32[]{:S(2)}, u32[]{:S(2)}) collective-permute-start(bf16[2048,1000]{0,1:T(8,128)(2,1)} %param.8), channel_id=1, source_target_pairs={{0,1},{1,0},{2,3},{3,2},{4,5},{5,4},{6,7},{7,6},{8,9},{9,8},{10,11... | collective-permute-start | bytes 12288008 | tf_op jit(solution)/shard_map/ppermute | solution.py:85
  11.1 3.9 %collective-permute-start.1 = (s32[4,48]{1,0:T(4,128)}, s32[4,48]{1,0:T(4,128)S(1)}, u32[]{:S(2)}, u32[]{:S(2)}) collective-permute-start(s32[4,48]{1,0:T(4,128)} %param.9), channel_id=1, source_target_pairs={{0,2},{2,0},{4,6},{6,4},{8,10},{10,8},{12,14},{14,12},{16,18},{18,... | collective-permute-start | bytes 2312 | tf_op jit(solution)/shard_map/ppermute | solution.py:56
  15.6 5.2 %collective-permute-start.2 = (s32[8,48]{1,0:T(8,128)S(1)}, s32[8,48]{1,0:T(8,128)S(1)}, u32[]{:S(2)}, u32[]{:S(2)}) collective-permute-start(s32[8,48]{1,0:T(8,128)S(1)} %pad_add_fusion.2), channel_id=1, source_target_pairs={{0,4},{2,6},{4,0},{6,2},{8,12},{10,14},{12,8},{14,10},{16,20},{18,... | collective-permute-start | bytes 4616 | tf_op jit(solution)/shard_map/ppermute | solution.py:56
  20.8 3.7 %collective-permute-start.3 = (s32[16,48]{1,0:T(8,128)S(1)}, s32[16,48]{1,0:T(8,128)S(1)}, u32[]{:S(2)}, u32[]{:S(2)}) collective-permute-start(s32[16,48]{1,0:T(8,128)S(1)} %pad_add_fusion.1), channel_id=1, source_target_pairs={{0,8},{2,10},{4,12},{6,14},{8,0},{10,2},{12,4},{14,6},{16,24},{18,... | collective-permute-start | bytes 9224 | tf_op jit(solution)/shard_map/ppermute | solution.py:56
  24.6 9.6 %collective-permute-start.4 = (s32[32,48]{1,0:T(8,128)S(1)}, s32[32,48]{1,0:T(8,128)S(1)}, u32[]{:S(2)}, u32[]{:S(2)}) collective-permute-start(s32[32,48]{1,0:T(8,128)S(1)} %pad_add_fusion), channel_id=1, source_target_pairs={{0,16},{2,18},{4,20},{6,22},{8,24},{10,26},{12,28},{14,30},{16,0},... | collective-permute-start | bytes 18440 | tf_op jit(solution)/shard_map/ppermute | solution.py:56
  51.1 111.3 %copy-start.1 = (s32[16]{0:T(128)S(1)}, s32[16]{0:T(128)}, u32[]{:S(2)}) copy-start(s32[16]{0:T(128)} %param.10) | copy-start | bytes 196
  51.1 125.3 %copy-start = (s32[16]{0:T(128)S(1)}, s32[16]{0:T(128)}, u32[]{:S(2)}) copy-start(s32[16]{0:T(128)} %param.11) | copy-start | bytes 196
  145.8 4.4 %collective-permute-start.5 = (f32[4,4,768]{2,1,0:T(4,128)S(1)}, f32[4,4,768]{2,1,0:T(4,128)S(1)}, u32[]{:S(2)}, u32[]{:S(2)}) collective-permute-start(f32[4,4,768]{2,1,0:T(4,128)S(1)} %reshape.101), channel_id=1, source_target_pairs={{0,2},{2,0},{4,6},{6,4},{8,10},{10,8},{12,14},{14,12},{16,18},{18,... | collective-permute-start | bytes 147464 | tf_op jit(solution)/shard_map/ppermute | solution.py:66
  150.3 5.7 %collective-permute-start.6 = (f32[4,4,768]{2,1,0:T(4,128)S(1)}, f32[4,4,768]{2,1,0:T(4,128)S(1)}, u32[]{:S(2)}, u32[]{:S(2)}) collective-permute-start(f32[4,4,768]{2,1,0:T(4,128)S(1)} %pad_maximum_fusion), channel_id=1, source_target_pairs={{0,4},{2,6},{4,0},{6,2},{8,12},{10,14},{12,8},{14,10},{16,20},{18,... | collective-permute-start | bytes 147464 | tf_op jit(solution)/shard_map/ppermute | solution.py:66
  156.0 4.5 %collective-permute-start.7 = (f32[4,4,768]{2,1,0:T(4,128)S(1)}, f32[4,4,768]{2,1,0:T(4,128)S(1)}, u32[]{:S(2)}, u32[]{:S(2)}) collective-permute-start(f32[4,4,768]{2,1,0:T(4,128)S(1)} %pad_maximum_fusion.1), channel_id=1, source_target_pairs={{0,8},{2,10},{4,12},{6,14},{8,0},{10,2},{12,4},{14,6},{16,24},{18,... | collective-permute-start | bytes 147464 | tf_op jit(solution)/shard_map/ppermute | solution.py:66
  160.6 5.7 %collective-permute-start.8 = (f32[4,4,768]{2,1,0:T(4,128)S(1)}, f32[4,4,768]{2,1,0:T(4,128)S(1)}, u32[]{:S(2)}, u32[]{:S(2)}) collective-permute-start(f32[4,4,768]{2,1,0:T(4,128)S(1)} %pad_maximum_fusion.2), channel_id=1, source_target_pairs={{0,16},{2,18},{4,20},{6,22},{8,24},{10,26},{12,28},{14,30},{16,0},... | collective-permute-start | bytes 147464 | tf_op jit(solution)/shard_map/ppermute | solution.py:66
  166.4 1.2 collective-permute-start.9
  167.8 3.6 %collective-permute-start.10 = (f32[16]{0:T(128)S(1)}, f32[16]{0:T(128)S(1)}, u32[]{:S(2)}, u32[]{:S(2)}) collective-permute-start(f32[16]{0:T(128)S(1)} %select_reduce_fusion), channel_id=1, source_target_pairs={{0,32},{32,0},{64,96},{96,64},{1,33},{33,1},{65,97},{97,65},{2,34}... | collective-permute-start | bytes 200 | tf_op jit(solution)/shard_map/ppermute | solution.py:66
  171.4 5.1 %collective-permute-start.11 = (f32[16]{0:T(128)S(1)}, f32[16]{0:T(128)S(1)}, u32[]{:S(2)}, u32[]{:S(2)}) collective-permute-start(f32[16]{0:T(128)S(1)} %add.179), channel_id=1, source_target_pairs={{0,64},{32,96},{64,0},{96,32},{1,65},{33,97},{65,1},{97,33},{2,66}... | collective-permute-start | bytes 200 | tf_op jit(solution)/shard_map/ppermute | solution.py:66
Sparse Core Ops, SparseCore 0:
  11.1 92.1 all-gather.1

commit v10 on v4

--- a/solution.py
+++ b/solution.py
@@ -6,7 +6,7 @@
 from jax.sharding import PartitionSpec as P
 
 norm_eps = 1e-06
-BLOCK = 1536
+BLOCK = 3072
 
 
 def block_stats(rows, tokens, weight, offset):

time: 183 us -> 188 us (1.027)
  other arithmetic: 28.8 us -> 32.9 us
    reduce_sum x2 -> x1, other arithmetic: 8.09 us -> 12.2 us  [block_stats(): exp_total = jnp.sum(exps, axis=1)]
    dot_general x2 -> x1, matrix products: 33.1 us -> 33.5 us  [block_stats(): logits = jnp.dot(rows, weight, preferred_element_type=jnp.float32)]
where the time goes in v10:
time: 188 us
  waiting for transfers between devices  88.1 us (47%)
  matrix products  33.5 us (18%)
  other arithmetic  32.9 us (18%)
  starting transfers between devices  17.6 us (9%)
  between operations  14.2 us (8%)
    all_gather x1, waiting for transfers between devices, body(): lax.all_gather(normed.reshape(own_rows, model_width), 'chip', axis=0, til...  58.7 us
    dot_general x1, matrix products, block_stats(): logits = jnp.dot(rows, weight, preferred_element_type=jnp.float32)  33.5 us
    ppermute x6, waiting for transfers between devices, xor_reduce(): x = combine(x, lax.ppermute(x, axis, [(i, i ^ bit) for i in range(size)]))  17.5 us
    reduce_sum x1, other arithmetic, block_stats(): exp_total = jnp.sum(exps, axis=1)  12.2 us
    ppermute x4, waiting for transfers between devices, xor_gather(): other = lax.ppermute(x, axis, [(i, i ^ bit) for i in range(size)])  10.8 us
    ppermute x6, starting transfers between devices, xor_reduce(): x = combine(x, lax.ppermute(x, axis, [(i, i ^ bit) for i in range(size)]))  9.72 us
    concatenate x1, other arithmetic, body(): jnp.concatenate([jnp.where(first, head_weight, other), jnp.where(first, o...  8.27 us
    ppermute x4, starting transfers between devices, xor_gather(): other = lax.ppermute(x, axis, [(i, i ^ bit) for i in range(size)])  7.63 us
  transfers between devices with their start and end apart: 13, of which 12 were waited for; matrix products, arithmetic and copies ran while one was open for 9% of the time, Pallas kernels for 0%

profile of v10, /device:TPU:2, one launch (start us, length us, event | category | flops | bytes accessed | tf_op | source)
XLA Modules:
  0.0 187.7 jit_solution(6169663031713923458)
XLA Ops:
  7.2 0.0 all-gather.2.cloned.1.call-start
  7.2 1.4 fusion.1
  8.6 2.3 %fusion.3 = bf16[4,48,2048]{2,1,0:T(8,128)(2,1)} fusion(bf16[4,48,2048]{2,1,0:T(8,128)(2,1)} %param.6, f32[2048]{0:T(1024)} %param.7, f32[4,48]{1,0:T(4,128)S(1)} %add_rsqrt_fusion), kind=kLoop, calls=%fused_computation.12 | loop fusion | flops 1572864 | bytes 1581824 | tf_op jit(solution)/shard_map/convert_element_type | solution.py:59
  10.9 0.0 all-gather.2.cloned.1.call-update
  10.9 0.1 collective-permute-start
  11.0 0.5 collective-permute-start.1
  11.5 3.4 %collective-permute-done.1 = s32[4,48]{1,0:T(4,128)S(1)} collective-permute-done((s32[4,48]{1,0:T(4,128)}, s32[4,48]{1,0:T(4,128)S(1)}, u32[]{:S(2)}, u32[]{:S(2)}) %collective-permute-start.1) | collective-permute-done | bytes 800 | tf_op jit(solution)/shard_map/ppermute | solution.py:33
  14.9 0.7 broadcast_select_fusion.9
  15.6 2.2 %collective-permute-start.2 = (s32[8,48]{1,0:T(8,128)S(1)}, s32[8,48]{1,0:T(8,128)S(1)}, u32[]{:S(2)}, u32[]{:S(2)}) collective-permute-start(s32[8,48]{1,0:T(8,128)S(1)} %pad_add_fusion.2), channel_id=1, source_target_pairs={{0,4},{2,6},{4,0},{6,2},{8,12},{10,14},{12,8},{14,10},{16,20},{18,... | collective-permute-start | bytes 4616 | tf_op jit(solution)/shard_map/ppermute | solution.py:33
  17.8 3.0 %collective-permute-done.2 = s32[8,48]{1,0:T(8,128)S(1)} collective-permute-done((s32[8,48]{1,0:T(8,128)S(1)}, s32[8,48]{1,0:T(8,128)S(1)}, u32[]{:S(2)}, u32[]{:S(2)}) %collective-permute-start.2) | collective-permute-done | bytes 1568 | tf_op jit(solution)/shard_map/ppermute | solution.py:33
  20.8 1.7 collective-permute-start.3
  22.4 2.1 %collective-permute-done.3 = s32[16,48]{1,0:T(8,128)S(1)} collective-permute-done((s32[16,48]{1,0:T(8,128)S(1)}, s32[16,48]{1,0:T(8,128)S(1)}, u32[]{:S(2)}, u32[]{:S(2)}) %collective-permute-start.3) | collective-permute-done | bytes 3104 | tf_op jit(solution)/shard_map/ppermute | solution.py:33
  24.5 3.3 %collective-permute-start.4 = (s32[32,48]{1,0:T(8,128)S(1)}, s32[32,48]{1,0:T(8,128)S(1)}, u32[]{:S(2)}, u32[]{:S(2)}) collective-permute-start(s32[32,48]{1,0:T(8,128)S(1)} %pad_add_fusion), channel_id=1, source_target_pairs={{0,16},{2,18},{4,20},{6,22},{8,24},{10,26},{12,28},{14,30},{16,0},... | collective-permute-start | bytes 18440 | tf_op jit(solution)/shard_map/ppermute | solution.py:33
  27.8 2.4 %collective-permute-done.4 = s32[32,48]{1,0:T(8,128)S(1)} collective-permute-done((s32[32,48]{1,0:T(8,128)S(1)}, s32[32,48]{1,0:T(8,128)S(1)}, u32[]{:S(2)}, u32[]{:S(2)}) %collective-permute-start.4) | collective-permute-done | bytes 6176 | tf_op jit(solution)/shard_map/ppermute | solution.py:33
  30.2 0.1 sub.112
  30.3 0.0 collective-permute-done
  30.3 5.9 %broadcast_select_fusion.1 = (bf16[2048,1000]{0,1:T(8,128)(2,1)}, bf16[2048,1000]{0,1:T(8,128)(2,1)}) fusion(bf16[2048,1000]{0,1:T(8,128)(2,1)} %param.8, bf16[2048,1000]{0,1:T(8,128)(2,1)} %collective-permute-done, pred[]{:T(512)S(6)} %eq.22), kind=kLoop, calls=%fused_computation.7 | loop fusion | flops 4096000 | bytes 16384001 | tf_op jit(solution)/shard_map/jit(_where)/select_n | solution.py:64
  36.2 8.3 %pad_maximum_fusion = bf16[2048,2000]{0,1:T(8,128)(2,1)} fusion(bf16[2048,1000]{0,1:T(8,128)(2,1)} %get-tuple-element.19, bf16[2048,1000]{0,1:T(8,128)(2,1)} %get-tuple-element.18), kind=kLoop, calls=%fused_computation.5 | loop fusion | flops 16384000 | bytes 16384000 | tf_op jit(solution)/shard_map/concatenate | solution.py:64
  44.5 58.7 %all-gather.2.cloned.1.call-done = bf16[3072,2048]{1,0:T(8,128)(2,1)} async-done(((bf16[192,2048]{1,0:T(8,128)(2,1)}), bf16[3072,2048]{1,0:T(8,128)(2,1)}) %all-gather.2.cloned.1.call-update) | async-done | bytes 12582928 | tf_op jit(solution)/shard_map/all_gather | solution.py:61
  103.2 33.5 %fusion.48 = (f32[3072]{0:T(1024)S(1)}, f32[3072,2000]{0,1:T(8,128)}) fusion(bf16[3072,2048]{1,0:T(8,128)(2,1)} %all-gather.2.cloned.1.call-done, bf16[2048,2000]{0,1:T(8,128)(2,1)} %pad_maximum_fusion), kind=kOutput, calls=%fused_computation.136 | convolution fusion | flops 25171963904 | bytes 45363200 | tf_op jit(solution)/shard_map/dot_general | solution.py:13
  136.7 0.1 stack.16
  136.8 0.0 copy-start.1
  136.8 0.0 copy-start
  136.9 12.2 %fusion = (f32[3072]{0:T(1024)S(1)}, f32[3072]{0:T(1024)S(1)}, f32[3072]{0:T(1024)S(1)}) fusion(f32[3072,2000]{0,1:T(8,128)} %get-tuple-element.45, f32[3072]{0:T(1024)S(1)} %get-tuple-element.44, s32[3072]{0:T(1024)S(1)} %sub.112), kind=kLoop, calls=%fused_computation.4 | loop fusion | flops 42998784 | bytes 24637440 | tf_op jit(solution)/shard_map/reduce_sum | solution.py:16
  149.1 0.1 stack.19
  149.2 0.1 stack.18
  149.3 0.1 stack.17
  149.4 0.1 reshape.101
  149.5 0.6 collective-permute-start.5
  150.2 0.1 squeeze.76
  150.3 0.1 squeeze.75
  150.4 0.1 squeeze.77
  150.5 0.1 squeeze.78
  150.6 3.1 %collective-permute-done.5 = f32[4,4,768]{2,1,0:T(4,128)S(1)} collective-permute-done((f32[4,4,768]{2,1,0:T(4,128)S(1)}, f32[4,4,768]{2,1,0:T(4,128)S(1)}, u32[]{:S(2)}, u32[]{:S(2)}) %collective-permute-start.5) | collective-permute-done | bytes 49184 | tf_op jit(solution)/shard_map/ppermute | solution.py:43
  153.8 2.2 %collective-permute-start.6 = (f32[4,4,768]{2,1,0:T(4,128)S(1)}, f32[4,4,768]{2,1,0:T(4,128)S(1)}, u32[]{:S(2)}, u32[]{:S(2)}) collective-permute-start(f32[4,4,768]{2,1,0:T(4,128)S(1)} %pad_maximum_fusion.1), channel_id=1, source_target_pairs={{0,4},{2,6},{4,0},{6,2},{8,12},{10,14},{12,8},{14,10},{16,20},{18,... | collective-permute-start | bytes 147464 | tf_op jit(solution)/shard_map/ppermute | solution.py:43
  155.9 3.5 %collective-permute-done.6 = f32[4,4,768]{2,1,0:T(4,128)S(1)} collective-permute-done((f32[4,4,768]{2,1,0:T(4,128)S(1)}, f32[4,4,768]{2,1,0:T(4,128)S(1)}, u32[]{:S(2)}, u32[]{:S(2)}) %collective-permute-start.6) | collective-permute-done | bytes 49184 | tf_op jit(solution)/shard_map/ppermute | solution.py:43
  159.5 0.3 collective-permute-start.7
  159.8 4.2 %collective-permute-done.7 = f32[4,4,768]{2,1,0:T(4,128)S(1)} collective-permute-done((f32[4,4,768]{2,1,0:T(4,128)S(1)}, f32[4,4,768]{2,1,0:T(4,128)S(1)}, u32[]{:S(2)}, u32[]{:S(2)}) %collective-permute-start.7) | collective-permute-done | bytes 49184 | tf_op jit(solution)/shard_map/ppermute | solution.py:43
  164.1 1.9 %collective-permute-start.8 = (f32[4,4,768]{2,1,0:T(4,128)S(1)}, f32[4,4,768]{2,1,0:T(4,128)S(1)}, u32[]{:S(2)}, u32[]{:S(2)}) collective-permute-start(f32[4,4,768]{2,1,0:T(4,128)S(1)} %pad_maximum_fusion.3), channel_id=1, source_target_pairs={{0,16},{2,18},{4,20},{6,22},{8,24},{10,26},{12,28},{14,30},{16,0},... | collective-permute-start | bytes 147464 | tf_op jit(solution)/shard_map/ppermute | solution.py:43
  166.0 0.0 copy-done.1
  166.0 0.1 dynamic_slice.9
  166.0 0.1 squeeze.73
  166.1 0.1 squeeze.87
  166.2 0.1 squeeze.82
  166.3 0.1 squeeze.92
  166.4 3.4 %collective-permute-done.8 = f32[4,4,768]{2,1,0:T(4,128)S(1)} collective-permute-done((f32[4,4,768]{2,1,0:T(4,128)S(1)}, f32[4,4,768]{2,1,0:T(4,128)S(1)}, u32[]{:S(2)}, u32[]{:S(2)}) %collective-permute-start.8) | collective-permute-done | bytes 49184 | tf_op jit(solution)/shard_map/ppermute | solution.py:43
  169.7 0.2 fusion.44
  169.9 0.1 collective-permute-start.9
  170.1 1.1 collective-permute-done.9
  171.2 0.1 select_reduce_fusion.1
  171.3 1.6 collective-permute-start.10
  172.9 2.0 %collective-permute-done.10 = f32[16]{0:T(128)S(1)} collective-permute-done((f32[16]{0:T(128)S(1)}, f32[16]{0:T(128)S(1)}, u32[]{:S(2)}, u32[]{:S(2)}) %collective-permute-start.10) | collective-permute-done | bytes 96 | tf_op jit(solution)/shard_map/ppermute | solution.py:43
  174.9 3.2 %collective-permute-start.11 = (f32[16]{0:T(128)S(1)}, f32[16]{0:T(128)S(1)}, u32[]{:S(2)}, u32[]{:S(2)}) collective-permute-start(f32[16]{0:T(128)S(1)} %add.177), channel_id=1, source_target_pairs={{0,64},{32,96},{64,0},{96,32},{1,65},{33,97},{65,1},{97,33},{2,66}... | collective-permute-start | bytes 200 | tf_op jit(solution)/shard_map/ppermute | solution.py:43
  178.0 0.7 constant_dynamic-slice_fusion.8
  178.7 1.3 collective-permute-done.11
  179.9 0.0 copy-done
  180.0 0.2 fusion.24
  180.1 0.2 fusion.25
  180.3 0.5 maximum_divide_fusion
  (31 shorter events, 0.4 us)
Async XLA Ops:
  7.2 96.1 %all-gather.2.cloned.1.call-start = ((), (), s32[]{:S(2)}) async-start(), calls=%async_computation | async-start | bytes 13369344 | tf_op jit(solution)/shard_map/all_gather | solution.py:61
  10.9 19.4 %collective-permute-start = (bf16[2048,1000]{0,1:T(8,128)(2,1)}, bf16[2048,1000]{0,1:T(8,128)(2,1)}, u32[]{:S(2)}, u32[]{:S(2)}) collective-permute-start(bf16[2048,1000]{0,1:T(8,128)(2,1)} %param.8), channel_id=1, source_target_pairs={{0,1},{1,0},{2,3},{3,2},{4,5},{5,4},{6,7},{7,6},{8,9},{9,8},{10,11... | collective-permute-start | bytes 12288008 | tf_op jit(solution)/shard_map/ppermute | solution.py:62
  11.0 3.9 %collective-permute-start.1 = (s32[4,48]{1,0:T(4,128)}, s32[4,48]{1,0:T(4,128)S(1)}, u32[]{:S(2)}, u32[]{:S(2)}) collective-permute-start(s32[4,48]{1,0:T(4,128)} %param.9), channel_id=1, source_target_pairs={{0,2},{2,0},{4,6},{6,4},{8,10},{10,8},{12,14},{14,12},{16,18},{18,... | collective-permute-start | bytes 2312 | tf_op jit(solution)/shard_map/ppermute | solution.py:33
  15.6 5.2 %collective-permute-start.2 = (s32[8,48]{1,0:T(8,128)S(1)}, s32[8,48]{1,0:T(8,128)S(1)}, u32[]{:S(2)}, u32[]{:S(2)}) collective-permute-start(s32[8,48]{1,0:T(8,128)S(1)} %pad_add_fusion.2), channel_id=1, source_target_pairs={{0,4},{2,6},{4,0},{6,2},{8,12},{10,14},{12,8},{14,10},{16,20},{18,... | collective-permute-start | bytes 4616 | tf_op jit(solution)/shard_map/ppermute | solution.py:33
  20.8 3.7 %collective-permute-start.3 = (s32[16,48]{1,0:T(8,128)S(1)}, s32[16,48]{1,0:T(8,128)S(1)}, u32[]{:S(2)}, u32[]{:S(2)}) collective-permute-start(s32[16,48]{1,0:T(8,128)S(1)} %pad_add_fusion.1), channel_id=1, source_target_pairs={{0,8},{2,10},{4,12},{6,14},{8,0},{10,2},{12,4},{14,6},{16,24},{18,... | collective-permute-start | bytes 9224 | tf_op jit(solution)/shard_map/ppermute | solution.py:33
  24.5 5.7 %collective-permute-start.4 = (s32[32,48]{1,0:T(8,128)S(1)}, s32[32,48]{1,0:T(8,128)S(1)}, u32[]{:S(2)}, u32[]{:S(2)}) collective-permute-start(s32[32,48]{1,0:T(8,128)S(1)} %pad_add_fusion), channel_id=1, source_target_pairs={{0,16},{2,18},{4,20},{6,22},{8,24},{10,26},{12,28},{14,30},{16,0},... | collective-permute-start | bytes 18440 | tf_op jit(solution)/shard_map/ppermute | solution.py:33
  136.8 29.1 %copy-start.1 = (s32[16]{0:T(128)S(1)}, s32[16]{0:T(128)}, u32[]{:S(2)}) copy-start(s32[16]{0:T(128)} %param.10) | copy-start | bytes 196
  136.8 43.1 %copy-start = (s32[16]{0:T(128)S(1)}, s32[16]{0:T(128)}, u32[]{:S(2)}) copy-start(s32[16]{0:T(128)} %param.11) | copy-start | bytes 196
  149.5 4.2 %collective-permute-start.5 = (f32[4,4,768]{2,1,0:T(4,128)S(1)}, f32[4,4,768]{2,1,0:T(4,128)S(1)}, u32[]{:S(2)}, u32[]{:S(2)}) collective-permute-start(f32[4,4,768]{2,1,0:T(4,128)S(1)} %reshape.101), channel_id=1, source_target_pairs={{0,2},{2,0},{4,6},{6,4},{8,10},{10,8},{12,14},{14,12},{16,18},{18,... | collective-permute-start | bytes 147464 | tf_op jit(solution)/shard_map/ppermute | solution.py:43
  153.8 5.7 %collective-permute-start.6 = (f32[4,4,768]{2,1,0:T(4,128)S(1)}, f32[4,4,768]{2,1,0:T(4,128)S(1)}, u32[]{:S(2)}, u32[]{:S(2)}) collective-permute-start(f32[4,4,768]{2,1,0:T(4,128)S(1)} %pad_maximum_fusion.1), channel_id=1, source_target_pairs={{0,4},{2,6},{4,0},{6,2},{8,12},{10,14},{12,8},{14,10},{16,20},{18,... | collective-permute-start | bytes 147464 | tf_op jit(solution)/shard_map/ppermute | solution.py:43
  159.5 4.5 %collective-permute-start.7 = (f32[4,4,768]{2,1,0:T(4,128)S(1)}, f32[4,4,768]{2,1,0:T(4,128)S(1)}, u32[]{:S(2)}, u32[]{:S(2)}) collective-permute-start(f32[4,4,768]{2,1,0:T(4,128)S(1)} %pad_maximum_fusion.2), channel_id=1, source_target_pairs={{0,8},{2,10},{4,12},{6,14},{8,0},{10,2},{12,4},{14,6},{16,24},{18,... | collective-permute-start | bytes 147464 | tf_op jit(solution)/shard_map/ppermute | solution.py:43
  164.1 5.7 %collective-permute-start.8 = (f32[4,4,768]{2,1,0:T(4,128)S(1)}, f32[4,4,768]{2,1,0:T(4,128)S(1)}, u32[]{:S(2)}, u32[]{:S(2)}) collective-permute-start(f32[4,4,768]{2,1,0:T(4,128)S(1)} %pad_maximum_fusion.3), channel_id=1, source_target_pairs={{0,16},{2,18},{4,20},{6,22},{8,24},{10,26},{12,28},{14,30},{16,0},... | collective-permute-start | bytes 147464 | tf_op jit(solution)/shard_map/ppermute | solution.py:43
  169.9 1.2 collective-permute-start.9
  171.3 3.6 %collective-permute-start.10 = (f32[16]{0:T(128)S(1)}, f32[16]{0:T(128)S(1)}, u32[]{:S(2)}, u32[]{:S(2)}) collective-permute-start(f32[16]{0:T(128)S(1)} %select_reduce_fusion.1), channel_id=1, source_target_pairs={{0,32},{32,0},{64,96},{96,64},{1,33},{33,1},{65,97},{97,65},{2,34}... | collective-permute-start | bytes 200 | tf_op jit(solution)/shard_map/ppermute | solution.py:43
  174.9 5.1 %collective-permute-start.11 = (f32[16]{0:T(128)S(1)}, f32[16]{0:T(128)S(1)}, u32[]{:S(2)}, u32[]{:S(2)}) collective-permute-start(f32[16]{0:T(128)S(1)} %add.177), channel_id=1, source_target_pairs={{0,64},{32,96},{64,0},{96,32},{1,65},{33,97},{65,1},{97,33},{2,66}... | collective-permute-start | bytes 200 | tf_op jit(solution)/shard_map/ppermute | solution.py:43
Sparse Core Ops, SparseCore 0:
  11.0 92.1 all-gather.1

commit v11 on v4

--- a/solution.py
+++ b/solution.py
@@ -70,10 +70,10 @@
     blocks = []
     for start in range(0, req_dev * half_len, BLOCK):
         size = min(BLOCK, req_dev * half_len - start)
-        blocks.append(block_stats(flat_rows[start : start + size], flat_tokens[start : start + size], weight, offset))
+        part = block_stats(flat_rows[start : start + size], flat_tokens[start : start + size], weight, offset)
+        blocks.append(xor_reduce(part, "chip", n_chip, merge))
     stats = jnp.concatenate(blocks, axis=1).reshape(4, n_chip, req_dev, pos_dev)
     stats = stats.transpose(0, 2, 1, 3).reshape(4, req_dev, half_len)
-    stats = xor_reduce(stats, "chip", n_chip, merge)
     row_top, exp_total, moment, token_logit = stats[0], stats[1], stats[2], stats[3]
     log_total = row_top + jnp.log(exp_total)
     raw_logprob = token_logit - log_total

time: 183 us -> 184 us (level)
  waiting for transfers between devices: 88.1 us -> 78.5 us
  starting transfers between devices: 17.6 us -> 26.7 us
    ppermute x6 -> x10, starting transfers between devices: 9.72 us -> 18.8 us  [xor_reduce(): x = combine(x, lax.ppermute(x, axis, [(i, i ^ bit) for i in range(size)]))]
    ppermute x6 -> x10, waiting for transfers between devices: 17.5 us -> 8.75 us  [xor_reduce(): x = combine(x, lax.ppermute(x, axis, [(i, i ^ bit) for i in range(size)]))]
  transfers between devices with their start and end apart: 13 -> 17, of which waited for: 12 -> 12; matrix products, arithmetic and copies ran while one was open for 9% -> 20% of each run, Pallas kernels for 0% -> 0%
where the time goes in v11:
time: 184 us; the launch traced here: 183 us
  waiting for transfers between devices  78.5 us (43%)
  matrix products  32.9 us (18%)
  other arithmetic  29.4 us (16%)
  starting transfers between devices  26.7 us (15%)
  between operations  14.3 us (8%)
    all_gather x1, waiting for transfers between devices, body(): lax.all_gather(normed.reshape(own_rows, model_width), 'chip', axis=0, til...  58.7 us
    dot_general x2, matrix products, block_stats(): logits = jnp.dot(rows, weight, preferred_element_type=jnp.float32)  32.9 us
    ppermute x10, starting transfers between devices, xor_reduce(): x = combine(x, lax.ppermute(x, axis, [(i, i ^ bit) for i in range(size)]))  18.8 us
    ppermute x4, waiting for transfers between devices, xor_gather(): other = lax.ppermute(x, axis, [(i, i ^ bit) for i in range(size)])  9.99 us
    ppermute x10, waiting for transfers between devices, xor_reduce(): x = combine(x, lax.ppermute(x, axis, [(i, i ^ bit) for i in range(size)]))  8.75 us
    concatenate x1, other arithmetic, body(): jnp.concatenate([jnp.where(first, head_weight, other), jnp.where(first, o...  8.24 us
    reduce_sum x2, other arithmetic, block_stats(): exp_total = jnp.sum(exps, axis=1)  8.09 us
    ppermute x4, starting transfers between devices, xor_gather(): other = lax.ppermute(x, axis, [(i, i ^ bit) for i in range(size)])  7.63 us
  transfers between devices with their start and end apart: 17, of which 12 were waited for; matrix products, arithmetic and copies ran while one was open for 20% of the time, Pallas kernels for 0%

profile of v11, /device:TPU:2, one launch (start us, length us, event | category | flops | bytes accessed | tf_op | source)
XLA Modules:
  0.0 183.1 jit_solution(15313377424496642568)
XLA Ops:
  7.2 0.0 all-gather.2.cloned.1.call-start
  7.2 1.4 fusion.6
  8.6 2.3 %fusion.8 = bf16[4,48,2048]{2,1,0:T(8,128)(2,1)} fusion(bf16[4,48,2048]{2,1,0:T(8,128)(2,1)} %param.6, f32[2048]{0:T(1024)} %param.7, f32[4,48]{1,0:T(4,128)S(1)} %add_rsqrt_fusion), kind=kLoop, calls=%fused_computation.21 | loop fusion | flops 1572864 | bytes 1581824 | tf_op jit(solution)/shard_map/convert_element_type | solution.py:59
  10.9 0.0 all-gather.2.cloned.1.call-update
  10.9 0.1 collective-permute-start
  11.0 0.5 collective-permute-start.1
  11.5 0.7 dynamic_slice.9
  12.3 2.6 %collective-permute-done.1 = s32[4,48]{1,0:T(4,128)S(1)} collective-permute-done((s32[4,48]{1,0:T(4,128)}, s32[4,48]{1,0:T(4,128)S(1)}, u32[]{:S(2)}, u32[]{:S(2)}) %collective-permute-start.1) | collective-permute-done | bytes 800 | tf_op jit(solution)/shard_map/ppermute | solution.py:33
  14.9 0.7 broadcast_select_fusion.7
  15.6 2.2 %collective-permute-start.2 = (s32[8,48]{1,0:T(8,128)S(1)}, s32[8,48]{1,0:T(8,128)S(1)}, u32[]{:S(2)}, u32[]{:S(2)}) collective-permute-start(s32[8,48]{1,0:T(8,128)S(1)} %pad_add_fusion.2), channel_id=1, source_target_pairs={{0,4},{2,6},{4,0},{6,2},{8,12},{10,14},{12,8},{14,10},{16,20},{18,... | collective-permute-start | bytes 4616 | tf_op jit(solution)/shard_map/ppermute | solution.py:33
  17.8 0.1 broadcast_compare_fusion
  17.9 2.9 %collective-permute-done.2 = s32[8,48]{1,0:T(8,128)S(1)} collective-permute-done((s32[8,48]{1,0:T(8,128)S(1)}, s32[8,48]{1,0:T(8,128)S(1)}, u32[]{:S(2)}, u32[]{:S(2)}) %collective-permute-start.2) | collective-permute-done | bytes 1568 | tf_op jit(solution)/shard_map/ppermute | solution.py:33
  20.8 1.7 collective-permute-start.3
  22.5 2.0 %collective-permute-done.3 = s32[16,48]{1,0:T(8,128)S(1)} collective-permute-done((s32[16,48]{1,0:T(8,128)S(1)}, s32[16,48]{1,0:T(8,128)S(1)}, u32[]{:S(2)}, u32[]{:S(2)}) %collective-permute-start.3) | collective-permute-done | bytes 3104 | tf_op jit(solution)/shard_map/ppermute | solution.py:33
  24.5 3.3 %collective-permute-start.4 = (s32[32,48]{1,0:T(8,128)S(1)}, s32[32,48]{1,0:T(8,128)S(1)}, u32[]{:S(2)}, u32[]{:S(2)}) collective-permute-start(s32[32,48]{1,0:T(8,128)S(1)} %pad_add_fusion), channel_id=1, source_target_pairs={{0,16},{2,18},{4,20},{6,22},{8,24},{10,26},{12,28},{14,30},{16,0},... | collective-permute-start | bytes 18440 | tf_op jit(solution)/shard_map/ppermute | solution.py:33
  27.8 2.4 %collective-permute-done.4 = s32[32,48]{1,0:T(8,128)S(1)} collective-permute-done((s32[32,48]{1,0:T(8,128)S(1)}, s32[32,48]{1,0:T(8,128)S(1)}, u32[]{:S(2)}, u32[]{:S(2)}) %collective-permute-start.4) | collective-permute-done | bytes 6176 | tf_op jit(solution)/shard_map/ppermute | solution.py:33
  30.2 0.1 sub.208
  30.3 0.1 sub.220
  30.4 0.0 collective-permute-done
  30.4 5.9 %broadcast_select_fusion.1 = (bf16[2048,1000]{0,1:T(8,128)(2,1)}, bf16[2048,1000]{0,1:T(8,128)(2,1)}) fusion(bf16[2048,1000]{0,1:T(8,128)(2,1)} %param.8, bf16[2048,1000]{0,1:T(8,128)(2,1)} %collective-permute-done, pred[]{:T(512)S(6)} %eq.28), kind=kLoop, calls=%fused_computation.16 | loop fusion | flops 4096000 | bytes 16384001 | tf_op jit(solution)/shard_map/jit(_where)/select_n | solution.py:64
  36.3 8.2 %pad_maximum_fusion = bf16[2048,2000]{0,1:T(8,128)(2,1)} fusion(bf16[2048,1000]{0,1:T(8,128)(2,1)} %get-tuple-element.26, bf16[2048,1000]{0,1:T(8,128)(2,1)} %get-tuple-element.25), kind=kLoop, calls=%fused_computation.10 | loop fusion | flops 16384000 | bytes 16384000 | tf_op jit(solution)/shard_map/concatenate | solution.py:64
  44.5 58.7 %all-gather.2.cloned.1.call-done = bf16[3072,2048]{1,0:T(8,128)(2,1)} async-done(((bf16[192,2048]{1,0:T(8,128)(2,1)}), bf16[3072,2048]{1,0:T(8,128)(2,1)}) %all-gather.2.cloned.1.call-update) | async-done | bytes 12582928 | tf_op jit(solution)/shard_map/all_gather | solution.py:61
  103.2 17.2 %fusion.50 = (f32[1536]{0:T(1024)S(1)}, f32[1536,2000]{0,1:T(8,128)S(1)}) fusion(bf16[2048,2000]{0,1:T(8,128)(2,1)} %pad_maximum_fusion, bf16[3072,2048]{1,0:T(8,128)(2,1)} %all-gather.2.cloned.1.call-done), kind=kOutput, calls=%fused_computation.155 | convolution fusion | flops 12585981952 | bytes 26777600 | tf_op jit(solution)/shard_map/dot_general | solution.py:13
  120.4 0.0 copy-start
  120.4 4.0 %fusion.1 = (f32[1536]{0:T(1024)S(1)}, f32[1536]{0:T(1024)S(1)}, f32[1536]{0:T(1024)S(1)}) fusion(f32[1536,2000]{0,1:T(8,128)S(1)} %get-tuple-element.61, f32[1536]{0:T(1024)S(1)} %get-tuple-element.60, s32[1536]{0:T(1024)S(1)} %sub.208), kind=kLoop, calls=%fused_computation.9 | loop fusion | flops 21499392 | bytes 12318720 | tf_op jit(solution)/shard_map/reduce_sum | solution.py:16
  124.6 0.8 collective-permute-start.5
  125.4 0.0 copy-done
  125.4 15.7 %fusion.49 = (f32[1536]{0:T(1024)S(1)}, f32[1536,2000]{0,1:T(8,128)S(1)}) fusion(bf16[2048,2000]{0,1:T(8,128)(2,1)S(1)} %copy-done, bf16[3072,2048]{1,0:T(8,128)(2,1)} %all-gather.2.cloned.1.call-done), kind=kOutput, calls=%fused_computation.154 | convolution fusion | flops 12585981952 | bytes 26777600 | tf_op jit(solution)/shard_map/dot_general | solution.py:13
  141.1 0.0 copy-start.1
  141.2 4.0 %fusion = (f32[1536]{0:T(1024)S(1)}, f32[1536]{0:T(1024)S(1)}, f32[1536]{0:T(1024)S(1)}) fusion(f32[1536,2000]{0,1:T(8,128)S(1)} %get-tuple-element.59, f32[1536]{0:T(1024)S(1)} %get-tuple-element.58, s32[1536]{0:T(1024)S(1)} %sub.220), kind=kLoop, calls=%fused_computation.4 | loop fusion | flops 21499392 | bytes 12318720 | tf_op jit(solution)/shard_map/reduce_sum | solution.py:16
  145.3 1.5 collective-permute-start.9
  146.8 0.0 collective-permute-done.5
  147.0 2.2 %collective-permute-start.6 = (f32[4,1536]{1,0:T(4,128)S(1)}, f32[4,1536]{1,0:T(4,128)S(1)}, u32[]{:S(2)}, u32[]{:S(2)}) collective-permute-start(f32[4,1536]{1,0:T(4,128)S(1)} %pad_maximum_fusion.2), channel_id=1, source_target_pairs={{0,4},{2,6},{4,0},{6,2},{8,12},{10,14},{12,8},{14,10},{16,20},{18,... | collective-permute-start | bytes 73736 | tf_op jit(solution)/shard_map/ppermute | solution.py:43
  149.1 0.1 collective-permute-done.9
  149.3 2.4 %collective-permute-start.10 = (f32[4,1536]{1,0:T(4,128)S(1)}, f32[4,1536]{1,0:T(4,128)S(1)}, u32[]{:S(2)}, u32[]{:S(2)}) collective-permute-start(f32[4,1536]{1,0:T(4,128)S(1)} %pad_maximum_fusion.6), channel_id=1, source_target_pairs={{0,4},{2,6},{4,0},{6,2},{8,12},{10,14},{12,8},{14,10},{16,20},{18,... | collective-permute-start | bytes 73736 | tf_op jit(solution)/shard_map/ppermute | solution.py:43
  151.8 0.7 collective-permute-done.6
  152.6 0.2 collective-permute-start.7
  152.8 1.9 %collective-permute-done.10 = f32[4,1536]{1,0:T(4,128)S(1)} collective-permute-done((f32[4,1536]{1,0:T(4,128)S(1)}, f32[4,1536]{1,0:T(4,128)S(1)}, u32[]{:S(2)}, u32[]{:S(2)}) %collective-permute-start.10) | collective-permute-done | bytes 24608 | tf_op jit(solution)/shard_map/ppermute | solution.py:43
  154.8 1.7 collective-permute-start.11
  156.5 0.0 collective-permute-done.7
  156.6 2.7 %collective-permute-start.8 = (f32[4,1536]{1,0:T(4,128)S(1)}, f32[4,1536]{1,0:T(4,128)S(1)}, u32[]{:S(2)}, u32[]{:S(2)}) collective-permute-start(f32[4,1536]{1,0:T(4,128)S(1)} %pad_maximum_fusion.4), channel_id=1, source_target_pairs={{0,16},{2,18},{4,20},{6,22},{8,24},{10,26},{12,28},{14,30},{16,0},... | collective-permute-start | bytes 73736 | tf_op jit(solution)/shard_map/ppermute | solution.py:43
  159.3 0.0 collective-permute-done.11
  159.4 2.6 %collective-permute-start.12 = (f32[4,1536]{1,0:T(4,128)S(1)}, f32[4,1536]{1,0:T(4,128)S(1)}, u32[]{:S(2)}, u32[]{:S(2)}) collective-permute-start(f32[4,1536]{1,0:T(4,128)S(1)} %pad_maximum_fusion.8), channel_id=1, source_target_pairs={{0,16},{2,18},{4,20},{6,22},{8,24},{10,26},{12,28},{14,30},{16,0},... | collective-permute-start | bytes 73736 | tf_op jit(solution)/shard_map/ppermute | solution.py:43
  162.0 0.0 collective-permute-done.8
  162.1 2.8 %collective-permute-done.12 = f32[4,1536]{1,0:T(4,128)S(1)} collective-permute-done((f32[4,1536]{1,0:T(4,128)S(1)}, f32[4,1536]{1,0:T(4,128)S(1)}, u32[]{:S(2)}, u32[]{:S(2)}) %collective-permute-start.12) | collective-permute-done | bytes 24608 | tf_op jit(solution)/shard_map/ppermute | solution.py:43
  164.9 0.1 maximum_maximum_fusion
  164.9 0.2 reshape.154
  165.1 0.2 select_reduce_fusion.2
  165.3 0.1 collective-permute-start.13
  165.4 0.1 sub.230
  165.5 1.0 collective-permute-done.13
  166.6 0.1 select_reduce_fusion.3
  166.6 1.6 collective-permute-start.14
  168.2 0.1 sub.232
  168.3 1.9 %collective-permute-done.14 = f32[16]{0:T(128)S(1)} collective-permute-done((f32[16]{0:T(128)S(1)}, f32[16]{0:T(128)S(1)}, u32[]{:S(2)}, u32[]{:S(2)}) %collective-permute-start.14) | collective-permute-done | bytes 96 | tf_op jit(solution)/shard_map/ppermute | solution.py:43
  170.2 3.1 %collective-permute-start.15 = (f32[16]{0:T(128)S(1)}, f32[16]{0:T(128)S(1)}, u32[]{:S(2)}, u32[]{:S(2)}) collective-permute-start(f32[16]{0:T(128)S(1)} %add.261), channel_id=1, source_target_pairs={{0,64},{32,96},{64,0},{96,32},{1,65},{33,97},{65,1},{97,33},{2,66}... | collective-permute-start | bytes 200 | tf_op jit(solution)/shard_map/ppermute | solution.py:43
  173.4 0.7 dynamic-slice_select_fusion
  174.1 1.3 collective-permute-done.15
  175.3 0.0 copy-done.1
  175.3 0.2 fusion.15
  175.5 0.2 fusion.16
  175.7 0.5 maximum_divide_fusion
  (46 shorter events, 0.9 us)
Async XLA Ops:
  7.2 96.1 %all-gather.2.cloned.1.call-start = ((), (), s32[]{:S(2)}) async-start(), calls=%async_computation | async-start | bytes 13369344 | tf_op jit(solution)/shard_map/all_gather | solution.py:61
  10.9 19.5 %collective-permute-start = (bf16[2048,1000]{0,1:T(8,128)(2,1)}, bf16[2048,1000]{0,1:T(8,128)(2,1)}, u32[]{:S(2)}, u32[]{:S(2)}) collective-permute-start(bf16[2048,1000]{0,1:T(8,128)(2,1)} %param.8), channel_id=1, source_target_pairs={{0,1},{1,0},{2,3},{3,2},{4,5},{5,4},{6,7},{7,6},{8,9},{9,8},{10,11... | collective-permute-start | bytes 12288008 | tf_op jit(solution)/shard_map/ppermute | solution.py:62
  11.0 3.9 %collective-permute-start.1 = (s32[4,48]{1,0:T(4,128)}, s32[4,48]{1,0:T(4,128)S(1)}, u32[]{:S(2)}, u32[]{:S(2)}) collective-permute-start(s32[4,48]{1,0:T(4,128)} %param.9), channel_id=1, source_target_pairs={{0,2},{2,0},{4,6},{6,4},{8,10},{10,8},{12,14},{14,12},{16,18},{18,... | collective-permute-start | bytes 2312 | tf_op jit(solution)/shard_map/ppermute | solution.py:33
  15.6 5.2 %collective-permute-start.2 = (s32[8,48]{1,0:T(8,128)S(1)}, s32[8,48]{1,0:T(8,128)S(1)}, u32[]{:S(2)}, u32[]{:S(2)}) collective-permute-start(s32[8,48]{1,0:T(8,128)S(1)} %pad_add_fusion.2), channel_id=1, source_target_pairs={{0,4},{2,6},{4,0},{6,2},{8,12},{10,14},{12,8},{14,10},{16,20},{18,... | collective-permute-start | bytes 4616 | tf_op jit(solution)/shard_map/ppermute | solution.py:33
  20.8 3.7 %collective-permute-start.3 = (s32[16,48]{1,0:T(8,128)S(1)}, s32[16,48]{1,0:T(8,128)S(1)}, u32[]{:S(2)}, u32[]{:S(2)}) collective-permute-start(s32[16,48]{1,0:T(8,128)S(1)} %pad_add_fusion.1), channel_id=1, source_target_pairs={{0,8},{2,10},{4,12},{6,14},{8,0},{10,2},{12,4},{14,6},{16,24},{18,... | collective-permute-start | bytes 9224 | tf_op jit(solution)/shard_map/ppermute | solution.py:33
  24.5 5.7 %collective-permute-start.4 = (s32[32,48]{1,0:T(8,128)S(1)}, s32[32,48]{1,0:T(8,128)S(1)}, u32[]{:S(2)}, u32[]{:S(2)}) collective-permute-start(s32[32,48]{1,0:T(8,128)S(1)} %pad_add_fusion), channel_id=1, source_target_pairs={{0,16},{2,18},{4,20},{6,22},{8,24},{10,26},{12,28},{14,30},{16,0},... | collective-permute-start | bytes 18440 | tf_op jit(solution)/shard_map/ppermute | solution.py:33
  120.4 5.0 %copy-start = (bf16[2048,2000]{0,1:T(8,128)(2,1)S(1)}, bf16[2048,2000]{0,1:T(8,128)(2,1)}, u32[]{:S(2)}) copy-start(bf16[2048,2000]{0,1:T(8,128)(2,1)} %pad_maximum_fusion) | copy-start | bytes 24576004
  124.6 22.3 %collective-permute-start.5 = (f32[4,1536]{1,0:T(4,128)S(1)}, f32[4,1536]{1,0:T(4,128)S(1)}, u32[]{:S(2)}, u32[]{:S(2)}) collective-permute-start(f32[4,1536]{1,0:T(4,128)S(1)} %pad_maximum_fusion.1), channel_id=1, source_target_pairs={{0,2},{2,0},{4,6},{6,4},{8,10},{10,8},{12,14},{14,12},{16,18},{18,... | collective-permute-start | bytes 73736 | tf_op jit(solution)/shard_map/ppermute | solution.py:43
  141.1 34.2 %copy-start.1 = (s32[16]{0:T(128)S(1)}, s32[16]{0:T(128)}, u32[]{:S(2)}) copy-start(s32[16]{0:T(128)} %param.11) | copy-start | bytes 196
  145.3 3.9 %collective-permute-start.9 = (f32[4,1536]{1,0:T(4,128)S(1)}, f32[4,1536]{1,0:T(4,128)S(1)}, u32[]{:S(2)}, u32[]{:S(2)}) collective-permute-start(f32[4,1536]{1,0:T(4,128)S(1)} %pad_maximum_fusion.5), channel_id=1, source_target_pairs={{0,2},{2,0},{4,6},{6,4},{8,10},{10,8},{12,14},{14,12},{16,18},{18,... | collective-permute-start | bytes 73736 | tf_op jit(solution)/shard_map/ppermute | solution.py:43
  147.0 5.5 %collective-permute-start.6 = (f32[4,1536]{1,0:T(4,128)S(1)}, f32[4,1536]{1,0:T(4,128)S(1)}, u32[]{:S(2)}, u32[]{:S(2)}) collective-permute-start(f32[4,1536]{1,0:T(4,128)S(1)} %pad_maximum_fusion.2), channel_id=1, source_target_pairs={{0,4},{2,6},{4,0},{6,2},{8,12},{10,14},{12,8},{14,10},{16,20},{18,... | collective-permute-start | bytes 73736 | tf_op jit(solution)/shard_map/ppermute | solution.py:43
  149.3 5.4 %collective-permute-start.10 = (f32[4,1536]{1,0:T(4,128)S(1)}, f32[4,1536]{1,0:T(4,128)S(1)}, u32[]{:S(2)}, u32[]{:S(2)}) collective-permute-start(f32[4,1536]{1,0:T(4,128)S(1)} %pad_maximum_fusion.6), channel_id=1, source_target_pairs={{0,4},{2,6},{4,0},{6,2},{8,12},{10,14},{12,8},{14,10},{16,20},{18,... | collective-permute-start | bytes 73736 | tf_op jit(solution)/shard_map/ppermute | solution.py:43
  152.6 3.9 %collective-permute-start.7 = (f32[4,1536]{1,0:T(4,128)S(1)}, f32[4,1536]{1,0:T(4,128)S(1)}, u32[]{:S(2)}, u32[]{:S(2)}) collective-permute-start(f32[4,1536]{1,0:T(4,128)S(1)} %pad_maximum_fusion.3), channel_id=1, source_target_pairs={{0,8},{2,10},{4,12},{6,14},{8,0},{10,2},{12,4},{14,6},{16,24},{18,... | collective-permute-start | bytes 73736 | tf_op jit(solution)/shard_map/ppermute | solution.py:43
  154.8 4.5 %collective-permute-start.11 = (f32[4,1536]{1,0:T(4,128)S(1)}, f32[4,1536]{1,0:T(4,128)S(1)}, u32[]{:S(2)}, u32[]{:S(2)}) collective-permute-start(f32[4,1536]{1,0:T(4,128)S(1)} %pad_maximum_fusion.7), channel_id=1, source_target_pairs={{0,8},{2,10},{4,12},{6,14},{8,0},{10,2},{12,4},{14,6},{16,24},{18,... | collective-permute-start | bytes 73736 | tf_op jit(solution)/shard_map/ppermute | solution.py:43
  156.6 5.4 %collective-permute-start.8 = (f32[4,1536]{1,0:T(4,128)S(1)}, f32[4,1536]{1,0:T(4,128)S(1)}, u32[]{:S(2)}, u32[]{:S(2)}) collective-permute-start(f32[4,1536]{1,0:T(4,128)S(1)} %pad_maximum_fusion.4), channel_id=1, source_target_pairs={{0,16},{2,18},{4,20},{6,22},{8,24},{10,26},{12,28},{14,30},{16,0},... | collective-permute-start | bytes 73736 | tf_op jit(solution)/shard_map/ppermute | solution.py:43
  159.4 5.4 %collective-permute-start.12 = (f32[4,1536]{1,0:T(4,128)S(1)}, f32[4,1536]{1,0:T(4,128)S(1)}, u32[]{:S(2)}, u32[]{:S(2)}) collective-permute-start(f32[4,1536]{1,0:T(4,128)S(1)} %pad_maximum_fusion.8), channel_id=1, source_target_pairs={{0,16},{2,18},{4,20},{6,22},{8,24},{10,26},{12,28},{14,30},{16,0},... | collective-permute-start | bytes 73736 | tf_op jit(solution)/shard_map/ppermute | solution.py:43
  165.3 1.2 collective-permute-start.13
  166.6 3.6 %collective-permute-start.14 = (f32[16]{0:T(128)S(1)}, f32[16]{0:T(128)S(1)}, u32[]{:S(2)}, u32[]{:S(2)}) collective-permute-start(f32[16]{0:T(128)S(1)} %select_reduce_fusion.3), channel_id=1, source_target_pairs={{0,32},{32,0},{64,96},{96,64},{1,33},{33,1},{65,97},{97,65},{2,34}... | collective-permute-start | bytes 200 | tf_op jit(solution)/shard_map/ppermute | solution.py:43
  170.2 5.1 %collective-permute-start.15 = (f32[16]{0:T(128)S(1)}, f32[16]{0:T(128)S(1)}, u32[]{:S(2)}, u32[]{:S(2)}) collective-permute-start(f32[16]{0:T(128)S(1)} %add.261), channel_id=1, source_target_pairs={{0,64},{32,96},{64,0},{96,32},{1,65},{33,97},{65,1},{97,33},{2,66}... | collective-permute-start | bytes 200 | tf_op jit(solution)/shard_map/ppermute | solution.py:43
Sparse Core Ops, SparseCore 0:
  11.0 92.1 all-gather.1
